TPU v7x, 256 devices: a whole 4x4x8 slice. The times are simulated.
256 devices in a mesh: section: 8 (over x, core), expert: 32 (over z, y).
Axes of the slice: x: 4, y: 4, z: 8, core: 2. Of those that a mesh axis runs over, the one named last changes fastest.
Arguments:
- tokens: bfloat16 [8, 2304, 2048], P(None, 'expert'), may hold values from -6 to 6
- w_in: bfloat16 [8, 2048, 2048], P('section', 'expert'), may hold values from -0.125 to 0.125
- w_out: bfloat16 [8, 2048, 2048], P('section', 'expert'), may hold values from -0.125 to 0.125
- router: bfloat16 [2048, 32], replicated, may hold values from -0.125 to 0.125
- exp_in: bfloat16 [32, 2048, 2048], P('expert', None, 'section'), may hold values from -0.125 to 0.125
- exp_out: bfloat16 [32, 2048, 2048], P('expert', 'section'), may hold values from -0.375 to 0.375
- active_rows: int32 [4608], P('expert'), may hold values from 0 to 575, as said below
- active_expert: int32 [4608, 1], P('expert'), may hold values from 0 to 31; in each aligned block of 144 rows (0 to 143, 144 to 287, ...) at most 13 rows name the same one
Outputs:
- updated: bfloat16 [8, 2304, 2048], P(None, 'expert', 'section')
Inputs may be any that keep to these rules, and one draw needn't show every extreme that they name: `active_rows`: the 144 entries of one token block name distinct rows of its 576 rows. `active_expert`: among the 144 entries of one token block no expert is named more than 13 times.
All inputs are finite; a program needn't handle non-finite values.
Results may differ from a plain program's by a relative error of at most 0.024.
Values may be sent and summed in bfloat16 or wider, within the bound.
No kernel may reach another device: no remote copies, remote signals or barrier semaphores. Data moves between devices by JAX's collectives and lax.ppermute only.
A program may use at most 64 MiB of HBM per device.

v0:
```python
import jax
import jax.numpy as jnp
from jax import lax
from jax.sharding import PartitionSpec as P


def from_behind(value, axis, steps):
    count = lax.axis_size(axis)
    initial, last = (max(0, -steps), min(count, count - steps))
    return lax.ppermute(value, axis, [(source, source + steps) for source in range(initial, last)])


def spread(shard, axis, root):
    mine = lax.axis_index(axis) == root
    return lax.psum(jnp.where(mine, shard, jnp.zeros_like(shard)), axis)


def normalize(rows):
    wide = rows.astype(jnp.float32)
    scale = lax.rsqrt(jnp.mean(wide * wide, axis=-1, keepdims=True) + 1e-05)
    return wide * scale


def processor(stream, w_first, w_second):
    normed = normalize(stream).astype(jnp.bfloat16)
    hidden = jax.nn.silu(jnp.dot(normed, w_first, preferred_element_type=jnp.float32)).astype(
        jnp.bfloat16
    )
    branch = jnp.dot(hidden, w_second, preferred_element_type=jnp.float32)
    return (stream.astype(jnp.float32) + branch).astype(jnp.bfloat16)


def local(tokens, w_in, w_out, router, exp_in, exp_out, active_rows, active_expert):
    n_section = lax.axis_size("section")
    section = lax.axis_index("section")
    micro, tok_dev, width = tokens.shape
    w_first, w_second = (
        lax.all_gather(w_in, "expert", axis=1, tiled=True),
        lax.all_gather(w_out, "expert", axis=1, tiled=True),
    )
    w_first = w_first[0]
    w_second = w_second[0]
    last = n_section - 1

    def run_layer(stream):
        return processor(stream, w_first, w_second)

    def skip_layer(stream):
        return jnp.zeros_like(stream)

    def tick(step, carry):
        incoming, collected = carry
        micro_index = step - section
        valid = (micro_index >= 0) & (micro_index < micro)
        clamped = jnp.clip(micro_index, 0, micro - 1)
        fresh = lax.dynamic_index_in_dim(tokens, clamped, 0, keepdims=False)
        stream = jnp.where(section == 0, fresh, incoming)
        result = lax.cond(valid, run_layer, skip_layer, stream)
        updated = lax.dynamic_update_index_in_dim(collected, result, clamped, 0)
        collected = jnp.where(valid & (section == last), updated, collected)
        passed = from_behind(result, "section", 1)
        return (passed, collected)

    start = (jnp.zeros((tok_dev, width), jnp.bfloat16), jnp.zeros_like(tokens))
    passed, collected = lax.fori_loop(0, micro + n_section - 1, tick, start)
    final = spread(collected, "section", last)
    rows_dev = micro * tok_dev
    flat = final.reshape(rows_dev, width)
    n_exp = router.shape[1]
    act_dev = active_rows.shape[0]
    capacity = 3 * act_dev // n_exp
    picked = jnp.take(flat, active_rows, axis=0)
    contact = normalize(picked).astype(jnp.bfloat16)
    chosen = active_expert[:, 0]
    onehot = chosen[:, None] == jnp.arange(n_exp, dtype=jnp.int32)[None, :]
    logits = jnp.dot(contact, router, preferred_element_type=jnp.float32)
    gate = jax.nn.sigmoid(jnp.sum(jnp.where(onehot, logits, 0.0), axis=1))
    counts = onehot.astype(jnp.int32)
    earlier = jnp.cumsum(counts, axis=0) - counts
    rank = jnp.sum(earlier * counts, axis=1)
    position = chosen * capacity + rank
    placing = (jnp.arange(n_exp * capacity, dtype=jnp.int32)[:, None] == position[None, :]).astype(
        jnp.bfloat16
    )
    outgoing = jnp.dot(placing, contact, preferred_element_type=jnp.float32).astype(jnp.bfloat16)
    outgoing = outgoing.reshape(n_exp, capacity, width)
    e_first = exp_in[0]
    e_second = exp_out[0]
    arrived = lax.all_to_all(outgoing, "expert", split_axis=0, concat_axis=0, tiled=True)
    sources, slots, _ = arrived.shape
    rows = arrived.reshape(sources * slots, width)
    hidden = jax.nn.silu(jnp.dot(rows, e_first, preferred_element_type=jnp.float32)).astype(
        jnp.bfloat16
    )
    partial_value = jnp.dot(hidden, e_second, preferred_element_type=jnp.float32).reshape(
        sources, slots, width
    )
    part_width = width // n_section
    returned = lax.all_to_all(
        partial_value.astype(jnp.bfloat16), "expert", split_axis=0, concat_axis=0, tiled=True
    ).astype(partial_value.dtype)
    mine = jnp.take(returned.reshape(n_exp * capacity, width), position, axis=0)
    added = lax.psum_scatter(
        (gate[:, None] * mine).astype(jnp.bfloat16), "section", scatter_dimension=1, tiled=True
    ).astype(jnp.float32)
    base = lax.dynamic_slice_in_dim(flat, section * part_width, part_width, 1).astype(jnp.float32)
    mixed = base.at[active_rows].add(added)
    return mixed.astype(jnp.bfloat16).reshape(micro, tok_dev, part_width)


def solution(mesh):
    return jax.shard_map(
        local,
        mesh=mesh,
        in_specs=(
            P(None, "expert", None),
            P("section", "expert", None),
            P("section", "expert", None),
            P(),
            P("expert", None, "section"),
            P("expert", "section", None),
            P("expert"),
            P("expert", None),
        ),
        out_specs=P(None, "expert", "section"),
        check_vma=False,
    )
```

profile of v0, /device:TPU:7, one launch (start us, length us, event | category | flops | bytes accessed | tf_op | source)
XLA Modules:
  0.0 730.6 jit_solution(625709644638391980)
XLA Ops:
  9.4 100.7 %all-gather.3.cloned.1.call-done = bf16[1,2048,2048]{2,1,0:T(8,128)(2,1)} async-done(((bf16[1,64,2048]{2,1,0:T(8,128)(2,1)}), bf16[1,2048,2048]{2,1,0:T(8,128)(2,1)}) %all-gather.3.cloned.1.call-update) | async-done | bytes 8388624 | tf_op jit(solution)/shard_map/all_gather | solution.py:38
  110.0 97.6 %all-gather.5.cloned.1.call-done = bf16[1,2048,2048]{2,1,0:T(8,128)(2,1)} async-done(((bf16[1,64,2048]{2,1,0:T(8,128)(2,1)}), bf16[1,2048,2048]{2,1,0:T(8,128)(2,1)}) %all-gather.5.cloned.1.call-update) | async-done | bytes 8388624 | tf_op jit(solution)/shard_map/all_gather | solution.py:39
  207.6 1.7 broadcast.91
  209.3 274.5 %while.16 = (s32[]{:T(128)}, bf16[72,2048]{1,0:T(8,128)(2,1)S(1)}, bf16[8,72,2048]{2,1,0:T(8,128)(2,1)}, s32[]{:T(128)}, pred[]{:T(512)}, /*index=5*/bf16[8,72,2...) while((s32[]{:T(128)}, bf16[72,2048]{1,0:T(8,128)(2,1)S(1)}, ...), condition=%wide.region_4.5_spmd, body=%wide.region_0.4_spmd.sunk | while | flops 1210613888 | bytes 21500040 | solution.py:65
  211.4 1.7 select_dynamic-update-slice_fusion.2
  213.2 1.5 collective-permute-done
  216.8 1.7 select_dynamic-update-slice_fusion.2
  218.6 5.2 collective-permute-done
  225.8 1.7 select_dynamic-update-slice_fusion.2
  227.6 5.2 collective-permute-done
  234.9 1.7 select_dynamic-update-slice_fusion.2
  236.6 5.2 collective-permute-done
  243.9 1.7 select_dynamic-update-slice_fusion.2
  245.6 5.2 collective-permute-done
  252.9 1.7 select_dynamic-update-slice_fusion.2
  254.7 5.2 collective-permute-done
  261.9 1.7 select_dynamic-update-slice_fusion.2
  263.7 63.9 %collective-permute-done = bf16[72,2048]{1,0:T(8,128)(2,1)S(1)} collective-permute-done((bf16[72,2048]{1,0:T(8,128)(2,1)}, bf16[72,2048]{1,0:T(8,128)(2,1)S(1)}, u32[]{:S(2)}, u32[]{:S(2)}) %collective-permute-start) | collective-permute-done | bytes 294944 | tf_op jit(solution)/shard_map/while/body/eval_jaxpr/ppermute | solution.py:10
  327.6 11.8 %conditional.2 = (bf16[72,2048]{1,0:T(8,128)(2,1)}, bf16[1,72,2048]{2,1,0:T(8,128)(2,1)S(1)}) conditional(s32[]{:T(128)} %convert_element_type.109, () %tuple.47, (pred[]{:T(512)}, bf16[8,72,2048]{2,1,0:T(8,128)(2,1)}, s32[]{:T(128)}, bf16[72,2048]{1,0:T(8,128)(2,1)S(1)}, bf16[2048,2048]{1,0:T(8,128)(2,1)}, ...), branch_computations={%region_1.1_spmd, %region_2.3_spmd} | conditional | flops 1210466432 | bytes 19434868 | solution.py:58
  328.8 9.7 %fusion = bf16[72,2048]{1,0:T(8,128)(2,1)} fusion(bf16[2048,2048]{1,0:T(8,128)(2,1)} %get-tuple-element.195, bf16[2048,2048]{1,0:T(8,128)(2,1)} %get-tuple-element.194, f32[72]{0:T(128)S(1)} %add_rsqrt_fusion, bf16[72,2048]{1,0:T(8,128)(2,1)S(1)} %get-tuple-element.193, bf16[8,72,2048]{2,1,0:T(8,128)(2,1)} %get-tuple-element.191, s32[]{:T(128)} %get-tuple-element.192, ...), kind=kOutput, calls=%fused_computation.4 | convolution fusion | flops 1209876480 | bytes 18254336 | tf_op jit(solution)/shard_map/while/body/eval_jaxpr/cond/branch_1_fun/dot_general | solution.py:29
  340.8 1.7 select_dynamic-update-slice_fusion.2
  342.5 5.2 collective-permute-done
  347.7 11.8 %conditional.2 = (bf16[72,2048]{1,0:T(8,128)(2,1)}, bf16[1,72,2048]{2,1,0:T(8,128)(2,1)S(1)}) conditional(s32[]{:T(128)} %convert_element_type.109, () %tuple.47, (pred[]{:T(512)}, bf16[8,72,2048]{2,1,0:T(8,128)(2,1)}, s32[]{:T(128)}, bf16[72,2048]{1,0:T(8,128)(2,1)S(1)}, bf16[2048,2048]{1,0:T(8,128)(2,1)}, ...), branch_computations={%region_1.1_spmd, %region_2.3_spmd} | conditional | flops 1210466432 | bytes 19434868 | solution.py:58
  348.9 9.7 %fusion = bf16[72,2048]{1,0:T(8,128)(2,1)} fusion(bf16[2048,2048]{1,0:T(8,128)(2,1)} %get-tuple-element.195, bf16[2048,2048]{1,0:T(8,128)(2,1)} %get-tuple-element.194, f32[72]{0:T(128)S(1)} %add_rsqrt_fusion, bf16[72,2048]{1,0:T(8,128)(2,1)S(1)} %get-tuple-element.193, bf16[8,72,2048]{2,1,0:T(8,128)(2,1)} %get-tuple-element.191, s32[]{:T(128)} %get-tuple-element.192, ...), kind=kOutput, calls=%fused_computation.4 | convolution fusion | flops 1209876480 | bytes 18254336 | tf_op jit(solution)/shard_map/while/body/eval_jaxpr/cond/branch_1_fun/dot_general | solution.py:29
  360.9 1.7 select_dynamic-update-slice_fusion.2
  362.6 5.2 collective-permute-done
  367.8 11.8 %conditional.2 = (bf16[72,2048]{1,0:T(8,128)(2,1)}, bf16[1,72,2048]{2,1,0:T(8,128)(2,1)S(1)}) conditional(s32[]{:T(128)} %convert_element_type.109, () %tuple.47, (pred[]{:T(512)}, bf16[8,72,2048]{2,1,0:T(8,128)(2,1)}, s32[]{:T(128)}, bf16[72,2048]{1,0:T(8,128)(2,1)S(1)}, bf16[2048,2048]{1,0:T(8,128)(2,1)}, ...), branch_computations={%region_1.1_spmd, %region_2.3_spmd} | conditional | flops 1210466432 | bytes 19434868 | solution.py:58
  369.0 9.7 %fusion = bf16[72,2048]{1,0:T(8,128)(2,1)} fusion(bf16[2048,2048]{1,0:T(8,128)(2,1)} %get-tuple-element.195, bf16[2048,2048]{1,0:T(8,128)(2,1)} %get-tuple-element.194, f32[72]{0:T(128)S(1)} %add_rsqrt_fusion, bf16[72,2048]{1,0:T(8,128)(2,1)S(1)} %get-tuple-element.193, bf16[8,72,2048]{2,1,0:T(8,128)(2,1)} %get-tuple-element.191, s32[]{:T(128)} %get-tuple-element.192, ...), kind=kOutput, calls=%fused_computation.4 | convolution fusion | flops 1209876480 | bytes 18254336 | tf_op jit(solution)/shard_map/while/body/eval_jaxpr/cond/branch_1_fun/dot_general | solution.py:29
  380.9 1.7 select_dynamic-update-slice_fusion.2
  382.7 5.2 collective-permute-done
  387.9 11.8 %conditional.2 = (bf16[72,2048]{1,0:T(8,128)(2,1)}, bf16[1,72,2048]{2,1,0:T(8,128)(2,1)S(1)}) conditional(s32[]{:T(128)} %convert_element_type.109, () %tuple.47, (pred[]{:T(512)}, bf16[8,72,2048]{2,1,0:T(8,128)(2,1)}, s32[]{:T(128)}, bf16[72,2048]{1,0:T(8,128)(2,1)S(1)}, bf16[2048,2048]{1,0:T(8,128)(2,1)}, ...), branch_computations={%region_1.1_spmd, %region_2.3_spmd} | conditional | flops 1210466432 | bytes 19434868 | solution.py:58
  389.1 9.7 %fusion = bf16[72,2048]{1,0:T(8,128)(2,1)} fusion(bf16[2048,2048]{1,0:T(8,128)(2,1)} %get-tuple-element.195, bf16[2048,2048]{1,0:T(8,128)(2,1)} %get-tuple-element.194, f32[72]{0:T(128)S(1)} %add_rsqrt_fusion, bf16[72,2048]{1,0:T(8,128)(2,1)S(1)} %get-tuple-element.193, bf16[8,72,2048]{2,1,0:T(8,128)(2,1)} %get-tuple-element.191, s32[]{:T(128)} %get-tuple-element.192, ...), kind=kOutput, calls=%fused_computation.4 | convolution fusion | flops 1209876480 | bytes 18254336 | tf_op jit(solution)/shard_map/while/body/eval_jaxpr/cond/branch_1_fun/dot_general | solution.py:29
  401.0 1.7 select_dynamic-update-slice_fusion.2
  402.8 5.2 collective-permute-done
  408.0 11.8 %conditional.2 = (bf16[72,2048]{1,0:T(8,128)(2,1)}, bf16[1,72,2048]{2,1,0:T(8,128)(2,1)S(1)}) conditional(s32[]{:T(128)} %convert_element_type.109, () %tuple.47, (pred[]{:T(512)}, bf16[8,72,2048]{2,1,0:T(8,128)(2,1)}, s32[]{:T(128)}, bf16[72,2048]{1,0:T(8,128)(2,1)S(1)}, bf16[2048,2048]{1,0:T(8,128)(2,1)}, ...), branch_computations={%region_1.1_spmd, %region_2.3_spmd} | conditional | flops 1210466432 | bytes 19434868 | solution.py:58
  409.2 9.7 %fusion = bf16[72,2048]{1,0:T(8,128)(2,1)} fusion(bf16[2048,2048]{1,0:T(8,128)(2,1)} %get-tuple-element.195, bf16[2048,2048]{1,0:T(8,128)(2,1)} %get-tuple-element.194, f32[72]{0:T(128)S(1)} %add_rsqrt_fusion, bf16[72,2048]{1,0:T(8,128)(2,1)S(1)} %get-tuple-element.193, bf16[8,72,2048]{2,1,0:T(8,128)(2,1)} %get-tuple-element.191, s32[]{:T(128)} %get-tuple-element.192, ...), kind=kOutput, calls=%fused_computation.4 | convolution fusion | flops 1209876480 | bytes 18254336 | tf_op jit(solution)/shard_map/while/body/eval_jaxpr/cond/branch_1_fun/dot_general | solution.py:29
  421.1 1.8 select_dynamic-update-slice_fusion.2
  422.9 5.2 collective-permute-done
  428.1 11.8 %conditional.2 = (bf16[72,2048]{1,0:T(8,128)(2,1)}, bf16[1,72,2048]{2,1,0:T(8,128)(2,1)S(1)}) conditional(s32[]{:T(128)} %convert_element_type.109, () %tuple.47, (pred[]{:T(512)}, bf16[8,72,2048]{2,1,0:T(8,128)(2,1)}, s32[]{:T(128)}, bf16[72,2048]{1,0:T(8,128)(2,1)S(1)}, bf16[2048,2048]{1,0:T(8,128)(2,1)}, ...), branch_computations={%region_1.1_spmd, %region_2.3_spmd} | conditional | flops 1210466432 | bytes 19434868 | solution.py:58
  429.2 9.7 %fusion = bf16[72,2048]{1,0:T(8,128)(2,1)} fusion(bf16[2048,2048]{1,0:T(8,128)(2,1)} %get-tuple-element.195, bf16[2048,2048]{1,0:T(8,128)(2,1)} %get-tuple-element.194, f32[72]{0:T(128)S(1)} %add_rsqrt_fusion, bf16[72,2048]{1,0:T(8,128)(2,1)S(1)} %get-tuple-element.193, bf16[8,72,2048]{2,1,0:T(8,128)(2,1)} %get-tuple-element.191, s32[]{:T(128)} %get-tuple-element.192, ...), kind=kOutput, calls=%fused_computation.4 | convolution fusion | flops 1209876480 | bytes 18254336 | tf_op jit(solution)/shard_map/while/body/eval_jaxpr/cond/branch_1_fun/dot_general | solution.py:29
  441.2 1.8 select_dynamic-update-slice_fusion.2
  443.0 5.2 collective-permute-done
  448.2 11.8 %conditional.2 = (bf16[72,2048]{1,0:T(8,128)(2,1)}, bf16[1,72,2048]{2,1,0:T(8,128)(2,1)S(1)}) conditional(s32[]{:T(128)} %convert_element_type.109, () %tuple.47, (pred[]{:T(512)}, bf16[8,72,2048]{2,1,0:T(8,128)(2,1)}, s32[]{:T(128)}, bf16[72,2048]{1,0:T(8,128)(2,1)S(1)}, bf16[2048,2048]{1,0:T(8,128)(2,1)}, ...), branch_computations={%region_1.1_spmd, %region_2.3_spmd} | conditional | flops 1210466432 | bytes 19434868 | solution.py:58
  449.3 9.7 %fusion = bf16[72,2048]{1,0:T(8,128)(2,1)} fusion(bf16[2048,2048]{1,0:T(8,128)(2,1)} %get-tuple-element.195, bf16[2048,2048]{1,0:T(8,128)(2,1)} %get-tuple-element.194, f32[72]{0:T(128)S(1)} %add_rsqrt_fusion, bf16[72,2048]{1,0:T(8,128)(2,1)S(1)} %get-tuple-element.193, bf16[8,72,2048]{2,1,0:T(8,128)(2,1)} %get-tuple-element.191, s32[]{:T(128)} %get-tuple-element.192, ...), kind=kOutput, calls=%fused_computation.4 | convolution fusion | flops 1209876480 | bytes 18254336 | tf_op jit(solution)/shard_map/while/body/eval_jaxpr/cond/branch_1_fun/dot_general | solution.py:29
  461.3 1.8 select_dynamic-update-slice_fusion.2
  463.1 5.2 collective-permute-done
  468.3 11.8 %conditional.2 = (bf16[72,2048]{1,0:T(8,128)(2,1)}, bf16[1,72,2048]{2,1,0:T(8,128)(2,1)S(1)}) conditional(s32[]{:T(128)} %convert_element_type.109, () %tuple.47, (pred[]{:T(512)}, bf16[8,72,2048]{2,1,0:T(8,128)(2,1)}, s32[]{:T(128)}, bf16[72,2048]{1,0:T(8,128)(2,1)S(1)}, bf16[2048,2048]{1,0:T(8,128)(2,1)}, ...), branch_computations={%region_1.1_spmd, %region_2.3_spmd} | conditional | flops 1210466432 | bytes 19434868 | solution.py:58
  469.4 9.7 %fusion = bf16[72,2048]{1,0:T(8,128)(2,1)} fusion(bf16[2048,2048]{1,0:T(8,128)(2,1)} %get-tuple-element.195, bf16[2048,2048]{1,0:T(8,128)(2,1)} %get-tuple-element.194, f32[72]{0:T(128)S(1)} %add_rsqrt_fusion, bf16[72,2048]{1,0:T(8,128)(2,1)S(1)} %get-tuple-element.193, bf16[8,72,2048]{2,1,0:T(8,128)(2,1)} %get-tuple-element.191, s32[]{:T(128)} %get-tuple-element.192, ...), kind=kOutput, calls=%fused_computation.4 | convolution fusion | flops 1209876480 | bytes 18254336 | tf_op jit(solution)/shard_map/while/body/eval_jaxpr/cond/branch_1_fun/dot_general | solution.py:29
  481.4 1.8 select_dynamic-update-slice_fusion.2
  483.8 3.2 broadcast_select_fusion
  487.8 66.5 %all-reduce.3.cloned.1.call-done = bf16[576,2048]{1,0:T(8,128)(2,1)} async-done(((bf16[576,2048]{1,0:T(8,128)(2,1)}), bf16[576,2048]{1,0:T(8,128)(2,1)}) %all-reduce.3.cloned.1.call-update) | async-done | bytes 2359312 | tf_op jit(solution)/shard_map/psum | solution.py:15
  554.3 3.5 gather_fusion
  558.7 1.9 convolution_convert_fusion.1
  560.6 1.8 reshape.75
  562.3 59.9 %all_to_all.10 = bf16[32,13,2048]{2,1,0:T(8,128)(2,1)} all-to-all(bf16[32,13,2048]{2,1,0:T(8,128)(2,1)S(1)} %reshape.75), channel_id=1, replica_groups=mesh['section'=8,'expert'=32] {'expert'}, dimensions={0} | all-to-all | bytes 3407872 | tf_op jit(solution)/shard_map/all_to_all | solution.py:89
  622.2 1.8 reshape.76
  624.1 1.9 multiply_convert_fusion.3
  626.6 2.3 copy.18
  629.0 5.6 all-to-all-start.1
  636.1 46.9 %all-to-all-done.1 = bf16[32,13,2048]{2,1,0:T(8,128)(2,1)S(1)} async-done(((bf16[32,13,2048]{2,1,0:T(8,128)(2,1)}), bf16[32,13,2048]{2,1,0:T(8,128)(2,1)S(1)}, u32[]{:S(2)}, u32[]{:S(2)}) %all-to-all-start.1) | async-done | bytes 1703968 | tf_op jit(solution)/shard_map/all_to_all | solution.py:99
  683.0 2.0 reshape.82
  685.0 3.5 gather_fusion.1
  690.6 30.8 %reduce-scatter.2.cloned.1.call-done = bf16[144,256]{1,0:T(8,128)(2,1)} async-done(((bf16[144,2048]{1,0:T(8,128)(2,1)}), bf16[144,256]{1,0:T(8,128)(2,1)}) %reduce-scatter.2.cloned.1.call-update) | async-done | bytes 73744 | tf_op jit(solution)/shard_map/reduce_scatter | solution.py:103
  721.4 2.0 scatter_custom_fusion
  (103 shorter events, 57.0 us)
Async XLA Ops:
  6.5 619.5 %copy-start = (bf16[1,256,2048]{2,1,0:T(8,128)(2,1)S(1)}, bf16[1,256,2048]{2,1,0:T(8,128)(2,1)}, u32[]{:S(2)}) copy-start(bf16[1,256,2048]{2,1,0:T(8,128)(2,1)} %param.17) | copy-start | bytes 3145732
  6.5 103.5 %all-gather.3.cloned.1.call-start = ((), (), s32[]{:S(2)}) async-start(), calls=%async_computation.3 | async-start | bytes 8650752 | tf_op jit(solution)/shard_map/all_gather | solution.py:38
  7.3 200.3 %all-gather.5.cloned.1.call-start = ((), (), s32[]{:S(2)}) async-start(), calls=%async_computation.4 | async-start | bytes 8650752 | tf_op jit(solution)/shard_map/all_gather | solution.py:39
  8.0 546.3 %all-reduce.3.cloned.1.call-start = ((), (), s32[]{:S(2)}) async-start(), calls=%async_computation.5 | async-start | bytes 4718592 | tf_op jit(solution)/shard_map/psum | solution.py:15
  210.1 4.6 collective-permute-start
  215.5 8.3 %collective-permute-start = (bf16[72,2048]{1,0:T(8,128)(2,1)}, bf16[72,2048]{1,0:T(8,128)(2,1)S(1)}, u32[]{:S(2)}, u32[]{:S(2)}) collective-permute-start(bf16[72,2048]{1,0:T(8,128)(2,1)} %get-tuple-element.287), channel_id=1, source_target_pairs={{0,32},{32,64},{64,96},{96,128},{128,160},{160,192},{192,224},{1,3... | collective-permute-start | bytes 884744 | tf_op jit(solution)/shard_map/while/body/eval_jaxpr/ppermute | solution.py:10
  224.5 8.3 %collective-permute-start = (bf16[72,2048]{1,0:T(8,128)(2,1)}, bf16[72,2048]{1,0:T(8,128)(2,1)S(1)}, u32[]{:S(2)}, u32[]{:S(2)}) collective-permute-start(bf16[72,2048]{1,0:T(8,128)(2,1)} %get-tuple-element.287), channel_id=1, source_target_pairs={{0,32},{32,64},{64,96},{96,128},{128,160},{160,192},{192,224},{1,3... | collective-permute-start | bytes 884744 | tf_op jit(solution)/shard_map/while/body/eval_jaxpr/ppermute | solution.py:10
  233.6 8.3 %collective-permute-start = (bf16[72,2048]{1,0:T(8,128)(2,1)}, bf16[72,2048]{1,0:T(8,128)(2,1)S(1)}, u32[]{:S(2)}, u32[]{:S(2)}) collective-permute-start(bf16[72,2048]{1,0:T(8,128)(2,1)} %get-tuple-element.287), channel_id=1, source_target_pairs={{0,32},{32,64},{64,96},{96,128},{128,160},{160,192},{192,224},{1,3... | collective-permute-start | bytes 884744 | tf_op jit(solution)/shard_map/while/body/eval_jaxpr/ppermute | solution.py:10
  242.6 8.3 %collective-permute-start = (bf16[72,2048]{1,0:T(8,128)(2,1)}, bf16[72,2048]{1,0:T(8,128)(2,1)S(1)}, u32[]{:S(2)}, u32[]{:S(2)}) collective-permute-start(bf16[72,2048]{1,0:T(8,128)(2,1)} %get-tuple-element.287), channel_id=1, source_target_pairs={{0,32},{32,64},{64,96},{96,128},{128,160},{160,192},{192,224},{1,3... | collective-permute-start | bytes 884744 | tf_op jit(solution)/shard_map/while/body/eval_jaxpr/ppermute | solution.py:10
  251.6 8.3 %collective-permute-start = (bf16[72,2048]{1,0:T(8,128)(2,1)}, bf16[72,2048]{1,0:T(8,128)(2,1)S(1)}, u32[]{:S(2)}, u32[]{:S(2)}) collective-permute-start(bf16[72,2048]{1,0:T(8,128)(2,1)} %get-tuple-element.287), channel_id=1, source_target_pairs={{0,32},{32,64},{64,96},{96,128},{128,160},{160,192},{192,224},{1,3... | collective-permute-start | bytes 884744 | tf_op jit(solution)/shard_map/while/body/eval_jaxpr/ppermute | solution.py:10
  260.6 67.0 %collective-permute-start = (bf16[72,2048]{1,0:T(8,128)(2,1)}, bf16[72,2048]{1,0:T(8,128)(2,1)S(1)}, u32[]{:S(2)}, u32[]{:S(2)}) collective-permute-start(bf16[72,2048]{1,0:T(8,128)(2,1)} %get-tuple-element.287), channel_id=1, source_target_pairs={{0,32},{32,64},{64,96},{96,128},{128,160},{160,192},{192,224},{1,3... | collective-permute-start | bytes 884744 | tf_op jit(solution)/shard_map/while/body/eval_jaxpr/ppermute | solution.py:10
  339.5 8.2 %collective-permute-start = (bf16[72,2048]{1,0:T(8,128)(2,1)}, bf16[72,2048]{1,0:T(8,128)(2,1)S(1)}, u32[]{:S(2)}, u32[]{:S(2)}) collective-permute-start(bf16[72,2048]{1,0:T(8,128)(2,1)} %get-tuple-element.287), channel_id=1, source_target_pairs={{0,32},{32,64},{64,96},{96,128},{128,160},{160,192},{192,224},{1,3... | collective-permute-start | bytes 884744 | tf_op jit(solution)/shard_map/while/body/eval_jaxpr/ppermute | solution.py:10
  359.6 8.2 %collective-permute-start = (bf16[72,2048]{1,0:T(8,128)(2,1)}, bf16[72,2048]{1,0:T(8,128)(2,1)S(1)}, u32[]{:S(2)}, u32[]{:S(2)}) collective-permute-start(bf16[72,2048]{1,0:T(8,128)(2,1)} %get-tuple-element.287), channel_id=1, source_target_pairs={{0,32},{32,64},{64,96},{96,128},{128,160},{160,192},{192,224},{1,3... | collective-permute-start | bytes 884744 | tf_op jit(solution)/shard_map/while/body/eval_jaxpr/ppermute | solution.py:10
  379.7 8.2 %collective-permute-start = (bf16[72,2048]{1,0:T(8,128)(2,1)}, bf16[72,2048]{1,0:T(8,128)(2,1)S(1)}, u32[]{:S(2)}, u32[]{:S(2)}) collective-permute-start(bf16[72,2048]{1,0:T(8,128)(2,1)} %get-tuple-element.287), channel_id=1, source_target_pairs={{0,32},{32,64},{64,96},{96,128},{128,160},{160,192},{192,224},{1,3... | collective-permute-start | bytes 884744 | tf_op jit(solution)/shard_map/while/body/eval_jaxpr/ppermute | solution.py:10
  399.7 8.2 %collective-permute-start = (bf16[72,2048]{1,0:T(8,128)(2,1)}, bf16[72,2048]{1,0:T(8,128)(2,1)S(1)}, u32[]{:S(2)}, u32[]{:S(2)}) collective-permute-start(bf16[72,2048]{1,0:T(8,128)(2,1)} %get-tuple-element.287), channel_id=1, source_target_pairs={{0,32},{32,64},{64,96},{96,128},{128,160},{160,192},{192,224},{1,3... | collective-permute-start | bytes 884744 | tf_op jit(solution)/shard_map/while/body/eval_jaxpr/ppermute | solution.py:10
  419.8 8.2 %collective-permute-start = (bf16[72,2048]{1,0:T(8,128)(2,1)}, bf16[72,2048]{1,0:T(8,128)(2,1)S(1)}, u32[]{:S(2)}, u32[]{:S(2)}) collective-permute-start(bf16[72,2048]{1,0:T(8,128)(2,1)} %get-tuple-element.287), channel_id=1, source_target_pairs={{0,32},{32,64},{64,96},{96,128},{128,160},{160,192},{192,224},{1,3... | collective-permute-start | bytes 884744 | tf_op jit(solution)/shard_map/while/body/eval_jaxpr/ppermute | solution.py:10
  439.9 8.2 %collective-permute-start = (bf16[72,2048]{1,0:T(8,128)(2,1)}, bf16[72,2048]{1,0:T(8,128)(2,1)S(1)}, u32[]{:S(2)}, u32[]{:S(2)}) collective-permute-start(bf16[72,2048]{1,0:T(8,128)(2,1)} %get-tuple-element.287), channel_id=1, source_target_pairs={{0,32},{32,64},{64,96},{96,128},{128,160},{160,192},{192,224},{1,3... | collective-permute-start | bytes 884744 | tf_op jit(solution)/shard_map/while/body/eval_jaxpr/ppermute | solution.py:10
  460.0 8.2 %collective-permute-start = (bf16[72,2048]{1,0:T(8,128)(2,1)}, bf16[72,2048]{1,0:T(8,128)(2,1)S(1)}, u32[]{:S(2)}, u32[]{:S(2)}) collective-permute-start(bf16[72,2048]{1,0:T(8,128)(2,1)} %get-tuple-element.287), channel_id=1, source_target_pairs={{0,32},{32,64},{64,96},{96,128},{128,160},{160,192},{192,224},{1,3... | collective-permute-start | bytes 884744 | tf_op jit(solution)/shard_map/while/body/eval_jaxpr/ppermute | solution.py:10
  480.1 3.7 collective-permute-start
  487.0 0.7 copy-start.3
  487.0 0.8 copy-start.2
  557.9 0.8 copy-start.1
  629.0 5.7 copy-start.4
  629.0 54.0 %all-to-all-start.1 = ((bf16[32,13,2048]{2,1,0:T(8,128)(2,1)}), bf16[32,13,2048]{2,1,0:T(8,128)(2,1)S(1)}, u32[]{:S(2)}, u32[]{:S(2)}) async-start(bf16[32,13,2048]{2,1,0:T(8,128)(2,1)} %copy.18), calls=%async_computation.1 | async-start | bytes 4194304 | tf_op jit(solution)/shard_map/all_to_all | solution.py:99
  634.5 86.8 %reduce-scatter.2.cloned.1.call-start = ((), (), s32[]{:S(2)}) async-start(), calls=%async_computation.6 | async-start | bytes 663552 | tf_op jit(solution)/shard_map/reduce_scatter | solution.py:103
Sparse Core Ops, SparseCore 0:
  9.9 100.0 all-gather.2
  112.6 94.9 all-gather.4
  487.2 67.1 all-reduce.2
  689.7 31.6 reduce-scatter.1
where the time goes:
time: 734 us; the launch traced here: 731 us
  waiting for transfers between devices  472 us (64%)
  matrix products  83.5 us (11%)
  blocking collectives  59.9 us (8%)
  other arithmetic  45.3 us (6%)
  local copies, waits for them, and re-layouts  30.9 us (4%)
  starting transfers between devices  25 us (3%)
  between operations  13.3 us (2%)
    ppermute x15, waiting for transfers between devices, from_behind(): lax.ppermute(value, axis, [(source, source + steps) for source in range(i...  128 us
    all_gather x1, waiting for transfers between devices, local(): lax.all_gather(w_in, 'expert', axis=1, tiled=True)  101 us
    all_gather x1, waiting for transfers between devices, local(): lax.all_gather(w_out, 'expert', axis=1, tiled=True)  97.6 us
    dot_general x8, matrix products, processor(): branch = jnp.dot(hidden, w_second, preferred_element_type=jnp.float32)  77.7 us
    psum x1, waiting for transfers between devices, spread(): return lax.psum(jnp.where(mine, shard, jnp.zeros_like(shard)), axis)  66.5 us
    all_to_all x1, blocking collectives, local(): lax.all_to_all(outgoing, 'expert', split_axis=0, concat_axis=0, tiled=True)  59.9 us
    all_to_all x1, waiting for transfers between devices, local(): lax.all_to_all(partial_value.astype(jnp.bfloat16), 'expert', split_axis=0...  46.9 us
    reduce_scatter x1, waiting for transfers between devices, local(): lax.psum_scatter((gate[:, None] * mine).astype(jnp.bfloat16), 'section',...  30.8 us
  transfers between devices with their start and end apart: 20, of which 20 were waited for; matrix products, arithmetic and copies ran while one was open for 4% of the time, Pallas kernels for 0%

commit v1 on v0

--- a/solution.py
+++ b/solution.py
@@ -8,11 +8,6 @@
     count = lax.axis_size(axis)
     initial, last = (max(0, -steps), min(count, count - steps))
     return lax.ppermute(value, axis, [(source, source + steps) for source in range(initial, last)])
-
-
-def spread(shard, axis, root):
-    mine = lax.axis_index(axis) == root
-    return lax.psum(jnp.where(mine, shard, jnp.zeros_like(shard)), axis)
 
 
 def normalize(rows):
@@ -32,7 +27,9 @@
 
 def local(tokens, w_in, w_out, router, exp_in, exp_out, active_rows, active_expert):
     n_section = lax.axis_size("section")
+    n_expert = lax.axis_size("expert")
     section = lax.axis_index("section")
+    expert_index = lax.axis_index("expert")
     micro, tok_dev, width = tokens.shape
     w_first, w_second = (
         lax.all_gather(w_in, "expert", axis=1, tiled=True),
@@ -63,48 +60,55 @@
 
     start = (jnp.zeros((tok_dev, width), jnp.bfloat16), jnp.zeros_like(tokens))
     passed, collected = lax.fori_loop(0, micro + n_section - 1, tick, start)
-    final = spread(collected, "section", last)
     rows_dev = micro * tok_dev
-    flat = final.reshape(rows_dev, width)
+    flat = collected.reshape(rows_dev, width)
     n_exp = router.shape[1]
-    act_dev = active_rows.shape[0]
-    capacity = 3 * act_dev // n_exp
-    picked = jnp.take(flat, active_rows, axis=0)
-    contact = normalize(picked).astype(jnp.bfloat16)
+    part_width = width // n_section
+    per_sub = 2
+    ranks = n_section * per_sub
     chosen = active_expert[:, 0]
     onehot = chosen[:, None] == jnp.arange(n_exp, dtype=jnp.int32)[None, :]
-    logits = jnp.dot(contact, router, preferred_element_type=jnp.float32)
-    gate = jax.nn.sigmoid(jnp.sum(jnp.where(onehot, logits, 0.0), axis=1))
     counts = onehot.astype(jnp.int32)
     earlier = jnp.cumsum(counts, axis=0) - counts
     rank = jnp.sum(earlier * counts, axis=1)
-    position = chosen * capacity + rank
-    placing = (jnp.arange(n_exp * capacity, dtype=jnp.int32)[:, None] == position[None, :]).astype(
-        jnp.bfloat16
-    )
-    outgoing = jnp.dot(placing, contact, preferred_element_type=jnp.float32).astype(jnp.bfloat16)
-    outgoing = outgoing.reshape(n_exp, capacity, width)
+    picked = jnp.take(flat, active_rows, axis=0)
+    contact = normalize(picked).astype(jnp.bfloat16)
+    share = rank // per_sub
+    slot = (share * n_exp + chosen) * per_sub + rank % per_sub
+    placing = (
+        jnp.arange(n_section * n_exp * per_sub, dtype=jnp.int32)[:, None] == slot[None, :]
+    ).astype(jnp.bfloat16)
+    dispatch = jnp.dot(placing, contact, preferred_element_type=jnp.float32).astype(jnp.bfloat16)
+    dispatch = dispatch.reshape(n_section, n_exp * per_sub, width)
+    columns = flat.reshape(rows_dev, n_section, part_width).transpose(1, 0, 2)
+    columns = columns.reshape(n_section, rows_dev * part_width // width, width)
+    payload = jnp.concatenate([columns, dispatch], axis=1)
+    mine = payload[last]
+    for target in range(n_section - 1):
+        got = lax.ppermute(payload[target], "section", [(last, target)])
+        mine = jnp.where(section == target, got, mine)
+    base_rows = rows_dev * part_width // width
+    base = mine[:base_rows].reshape(rows_dev, part_width)
+    outgoing = mine[base_rows:].reshape(n_exp, per_sub, width)
+    arrived = lax.all_to_all(outgoing, "expert", split_axis=0, concat_axis=0, tiled=True)
+    rows = lax.all_gather(arrived, "section", axis=0, tiled=True).reshape(-1, width)
     e_first = exp_in[0]
     e_second = exp_out[0]
-    arrived = lax.all_to_all(outgoing, "expert", split_axis=0, concat_axis=0, tiled=True)
-    sources, slots, _ = arrived.shape
-    rows = arrived.reshape(sources * slots, width)
+    column = lax.dynamic_slice_in_dim(router, expert_index, 1, 1)
+    logits = jnp.dot(rows, column, preferred_element_type=jnp.float32)[:, 0]
+    gate = jax.nn.sigmoid(logits)
     hidden = jax.nn.silu(jnp.dot(rows, e_first, preferred_element_type=jnp.float32)).astype(
         jnp.bfloat16
     )
-    partial_value = jnp.dot(hidden, e_second, preferred_element_type=jnp.float32).reshape(
-        sources, slots, width
-    )
-    part_width = width // n_section
-    returned = lax.all_to_all(
-        partial_value.astype(jnp.bfloat16), "expert", split_axis=0, concat_axis=0, tiled=True
-    ).astype(partial_value.dtype)
-    mine = jnp.take(returned.reshape(n_exp * capacity, width), position, axis=0)
-    added = lax.psum_scatter(
-        (gate[:, None] * mine).astype(jnp.bfloat16), "section", scatter_dimension=1, tiled=True
-    ).astype(jnp.float32)
-    base = lax.dynamic_slice_in_dim(flat, section * part_width, part_width, 1).astype(jnp.float32)
-    mixed = base.at[active_rows].add(added)
+    partial_value = jnp.dot(hidden, e_second, preferred_element_type=jnp.float32)
+    scaled = (gate[:, None] * partial_value).astype(jnp.bfloat16)
+    summed = lax.psum_scatter(scaled, "section", scatter_dimension=1, tiled=True)
+    summed = summed.reshape(n_section, n_expert, per_sub, part_width).transpose(1, 0, 2, 3)
+    returned = lax.all_to_all(summed, "expert", split_axis=0, concat_axis=0, tiled=True)
+    returned = returned.reshape(n_exp * ranks, part_width)
+    position = chosen * ranks + rank
+    added = jnp.take(returned, position, axis=0).astype(jnp.float32)
+    mixed = base.astype(jnp.float32).at[active_rows].add(added)
     return mixed.astype(jnp.bfloat16).reshape(micro, tok_dev, part_width)
 
 

time: 734 us -> 665 us (0.906)
  blocking collectives: 59.9 us -> 15.7 us
  waiting for transfers between devices: 472 us -> 432 us
  starting transfers between devices: 25 us -> 42.7 us
  other arithmetic: 45.3 us -> 31.1 us
  local copies, waits for them, and re-layouts: 30.9 us -> 40.5 us
    psum x1 -> x0, waiting for transfers between devices: 66.5 us -> none  [spread(): return lax.psum(jnp.where(mine, shard, jnp.zeros_like(shard)), axis)]
    all_to_all x1, blocking collectives: 59.9 us -> 15.7 us  [local(): lax.all_to_all(outgoing, 'expert', split_axis=0, concat_axis=0, tiled=True)]
    all_to_all x1, waiting for transfers between devices: 46.9 us -> 12.6 us  [local(): lax.all_to_all(summed, 'expert', split_axis=0, concat_axis=0, tiled=True)]
    all_gather x0 -> x1, waiting for transfers between devices: none -> 24.6 us  [local(): lax.all_gather(arrived, 'section', axis=0, tiled=True).reshape(-1, width)]
    ppermute x15, waiting for transfers between devices: 128 us -> 149 us  [from_behind(): lax.ppermute(value, axis, [(source, source + steps) for source in range(i...]
    select_n x15, other arithmetic: 26.3 us -> 9.16 us  [tick(): collected = jnp.where(valid & (section == last), updated, collected)]
    ppermute x0 -> x7, starting transfers between devices: none -> 13.9 us  [local(): got = lax.ppermute(payload[target], 'section', [(last, target)])]
    ppermute x0 -> x7, waiting for transfers between devices: none -> 13.1 us  [local(): got = lax.ppermute(payload[target], 'section', [(last, target)])]
  transfers between devices with their start and end apart: 20 -> 27, of which waited for: 20 -> 23; matrix products, arithmetic and copies ran while one was open for 4% -> 2% of each run, Pallas kernels for 0% -> 0%
where the time goes in v1:
time: 665 us; the launch traced here: 663 us
  waiting for transfers between devices  432 us (65%)
  matrix products  87 us (13%)
  starting transfers between devices  42.7 us (6%)
  local copies, waits for them, and re-layouts  40.5 us (6%)
  other arithmetic  31.1 us (5%)
  blocking collectives  15.7 us (2%)
  between operations  13.3 us (2%)
    ppermute x15, waiting for transfers between devices, from_behind(): lax.ppermute(value, axis, [(source, source + steps) for source in range(i...  149 us
    all_gather x1, waiting for transfers between devices, local(): lax.all_gather(w_out, 'expert', axis=1, tiled=True)  97.6 us
    all_gather x1, waiting for transfers between devices, local(): lax.all_gather(w_in, 'expert', axis=1, tiled=True)  97.6 us
    dot_general x8, matrix products, processor(): branch = jnp.dot(hidden, w_second, preferred_element_type=jnp.float32)  78.8 us
    reduce_scatter x1, waiting for transfers between devices, local(): lax.psum_scatter(scaled, 'section', scatter_dimension=1, tiled=True)  36.3 us
    all_gather x1, waiting for transfers between devices, local(): lax.all_gather(arrived, 'section', axis=0, tiled=True).reshape(-1, width)  24.6 us
    ppermute x15, starting transfers between devices, from_behind(): lax.ppermute(value, axis, [(source, source + steps) for source in range(i...  19.2 us
    all_to_all x1, blocking collectives, local(): lax.all_to_all(outgoing, 'expert', split_axis=0, concat_axis=0, tiled=True)  15.7 us
  transfers between devices with their start and end apart: 27, of which 23 were waited for; matrix products, arithmetic and copies ran while one was open for 2% of the time, Pallas kernels for 0%

profile of v1, /device:TPU:7, one launch (start us, length us, event | category | flops | bytes accessed | tf_op | source)
XLA Modules:
  0.0 662.8 jit_solution(12632711766562289976)
XLA Ops:
  12.4 97.6 %all-gather.4.cloned.1.call-done = bf16[1,2048,2048]{2,1,0:T(8,128)(2,1)} async-done(((bf16[1,64,2048]{2,1,0:T(8,128)(2,1)}), bf16[1,2048,2048]{2,1,0:T(8,128)(2,1)}) %all-gather.4.cloned.1.call-update) | async-done | bytes 8388624 | tf_op jit(solution)/shard_map/all_gather | solution.py:35
  110.0 97.6 %all-gather.6.cloned.1.call-done = bf16[1,2048,2048]{2,1,0:T(8,128)(2,1)} async-done(((bf16[1,64,2048]{2,1,0:T(8,128)(2,1)}), bf16[1,2048,2048]{2,1,0:T(8,128)(2,1)}) %all-gather.6.cloned.1.call-update) | async-done | bytes 8388624 | tf_op jit(solution)/shard_map/all_gather | solution.py:36
  208.6 290.4 %while.16 = (s32[]{:T(128)}, bf16[72,2048]{1,0:T(8,128)(2,1)}, bf16[8,72,2048]{2,1,0:T(8,128)(2,1)S(1)}, s32[]{:T(128)}, pred[]{:T(512)}, /*index=5*/bf16[8,72,2...) while((s32[]{:T(128)}, bf16[72,2048]{1,0:T(8,128)(2,1)}, ...), condition=%wide.region_4.5_spmd, body=%wide.region_0.4_spmd.sunk | while | flops 1210613888 | bytes 21499308 | solution.py:62
  211.5 3.3 collective-permute-done
  217.7 6.9 %collective-permute-done = bf16[72,2048]{1,0:T(8,128)(2,1)} collective-permute-done((bf16[72,2048]{1,0:T(8,128)(2,1)}, bf16[72,2048]{1,0:T(8,128)(2,1)}, u32[]{:S(2)}, u32[]{:S(2)}) %collective-permute-start) | collective-permute-done | bytes 294944 | tf_op jit(solution)/shard_map/while/body/eval_jaxpr/ppermute | solution.py:10
  227.5 6.9 %collective-permute-done = bf16[72,2048]{1,0:T(8,128)(2,1)} collective-permute-done((bf16[72,2048]{1,0:T(8,128)(2,1)}, bf16[72,2048]{1,0:T(8,128)(2,1)}, u32[]{:S(2)}, u32[]{:S(2)}) %collective-permute-start) | collective-permute-done | bytes 294944 | tf_op jit(solution)/shard_map/while/body/eval_jaxpr/ppermute | solution.py:10
  234.5 1.5 conditional.2
  237.4 6.9 %collective-permute-done = bf16[72,2048]{1,0:T(8,128)(2,1)} collective-permute-done((bf16[72,2048]{1,0:T(8,128)(2,1)}, bf16[72,2048]{1,0:T(8,128)(2,1)}, u32[]{:S(2)}, u32[]{:S(2)}) %collective-permute-start) | collective-permute-done | bytes 294944 | tf_op jit(solution)/shard_map/while/body/eval_jaxpr/ppermute | solution.py:10
  247.2 6.9 %collective-permute-done = bf16[72,2048]{1,0:T(8,128)(2,1)} collective-permute-done((bf16[72,2048]{1,0:T(8,128)(2,1)}, bf16[72,2048]{1,0:T(8,128)(2,1)}, u32[]{:S(2)}, u32[]{:S(2)}) %collective-permute-start) | collective-permute-done | bytes 294944 | tf_op jit(solution)/shard_map/while/body/eval_jaxpr/ppermute | solution.py:10
  257.0 6.9 %collective-permute-done = bf16[72,2048]{1,0:T(8,128)(2,1)} collective-permute-done((bf16[72,2048]{1,0:T(8,128)(2,1)}, bf16[72,2048]{1,0:T(8,128)(2,1)}, u32[]{:S(2)}, u32[]{:S(2)}) %collective-permute-start) | collective-permute-done | bytes 294944 | tf_op jit(solution)/shard_map/while/body/eval_jaxpr/ppermute | solution.py:10
  266.8 67.4 %collective-permute-done = bf16[72,2048]{1,0:T(8,128)(2,1)} collective-permute-done((bf16[72,2048]{1,0:T(8,128)(2,1)}, bf16[72,2048]{1,0:T(8,128)(2,1)}, u32[]{:S(2)}, u32[]{:S(2)}) %collective-permute-start) | collective-permute-done | bytes 294944 | tf_op jit(solution)/shard_map/while/body/eval_jaxpr/ppermute | solution.py:10
  334.3 12.8 %conditional.2 = (bf16[72,2048]{1,0:T(8,128)(2,1)}, bf16[1,72,2048]{2,1,0:T(8,128)(2,1)}) conditional(s32[]{:T(128)} %convert_element_type.108, () %tuple.53, (pred[]{:T(512)}, bf16[8,72,2048]{2,1,0:T(8,128)(2,1)}, s32[]{:T(128)}, bf16[72,2048]{1,0:T(8,128)(2,1)}, bf16[2048,2048]{1,0:T(8,128)(2,1)}, /*index=5*/bf16[2048,2048]{1,0:T(8,128)(2,1)}) %tuple.54), branch_computations={%region_1.1_spmd, %region_2.3_spmd} | conditional | flops 1210466432 | bytes 19434644 | solution.py:55
  335.6 9.8 %fusion = bf16[72,2048]{1,0:T(8,128)(2,1)} fusion(bf16[2048,2048]{1,0:T(8,128)(2,1)} %get-tuple-element.195, bf16[2048,2048]{1,0:T(8,128)(2,1)} %get-tuple-element.194, f32[72]{0:T(128)S(1)} %add_rsqrt_fusion, bf16[72,2048]{1,0:T(8,128)(2,1)} %get-tuple-element.193, bf16[8,72,2048]{2,1,0:T(8,128)(2,1)} %get-tuple-element.191, s32[]{:T(128)} %get-tuple-element.192, ...), kind=kOutput, calls=%fused_computation.4 | convolution fusion | flops 1209876480 | bytes 18254112 | tf_op jit(solution)/shard_map/while/body/eval_jaxpr/cond/branch_1_fun/dot_general | solution.py:24
  345.4 1.7 copy.30
  349.5 6.0 collective-permute-done
  355.4 12.8 %conditional.2 = (bf16[72,2048]{1,0:T(8,128)(2,1)}, bf16[1,72,2048]{2,1,0:T(8,128)(2,1)}) conditional(s32[]{:T(128)} %convert_element_type.108, () %tuple.53, (pred[]{:T(512)}, bf16[8,72,2048]{2,1,0:T(8,128)(2,1)}, s32[]{:T(128)}, bf16[72,2048]{1,0:T(8,128)(2,1)}, bf16[2048,2048]{1,0:T(8,128)(2,1)}, /*index=5*/bf16[2048,2048]{1,0:T(8,128)(2,1)}) %tuple.54), branch_computations={%region_1.1_spmd, %region_2.3_spmd} | conditional | flops 1210466432 | bytes 19434644 | solution.py:55
  356.7 9.8 %fusion = bf16[72,2048]{1,0:T(8,128)(2,1)} fusion(bf16[2048,2048]{1,0:T(8,128)(2,1)} %get-tuple-element.195, bf16[2048,2048]{1,0:T(8,128)(2,1)} %get-tuple-element.194, f32[72]{0:T(128)S(1)} %add_rsqrt_fusion, bf16[72,2048]{1,0:T(8,128)(2,1)} %get-tuple-element.193, bf16[8,72,2048]{2,1,0:T(8,128)(2,1)} %get-tuple-element.191, s32[]{:T(128)} %get-tuple-element.192, ...), kind=kOutput, calls=%fused_computation.4 | convolution fusion | flops 1209876480 | bytes 18254112 | tf_op jit(solution)/shard_map/while/body/eval_jaxpr/cond/branch_1_fun/dot_general | solution.py:24
  366.6 1.7 copy.30
  370.6 6.0 collective-permute-done
  376.6 12.8 %conditional.2 = (bf16[72,2048]{1,0:T(8,128)(2,1)}, bf16[1,72,2048]{2,1,0:T(8,128)(2,1)}) conditional(s32[]{:T(128)} %convert_element_type.108, () %tuple.53, (pred[]{:T(512)}, bf16[8,72,2048]{2,1,0:T(8,128)(2,1)}, s32[]{:T(128)}, bf16[72,2048]{1,0:T(8,128)(2,1)}, bf16[2048,2048]{1,0:T(8,128)(2,1)}, /*index=5*/bf16[2048,2048]{1,0:T(8,128)(2,1)}) %tuple.54), branch_computations={%region_1.1_spmd, %region_2.3_spmd} | conditional | flops 1210466432 | bytes 19434644 | solution.py:55
  377.9 9.8 %fusion = bf16[72,2048]{1,0:T(8,128)(2,1)} fusion(bf16[2048,2048]{1,0:T(8,128)(2,1)} %get-tuple-element.195, bf16[2048,2048]{1,0:T(8,128)(2,1)} %get-tuple-element.194, f32[72]{0:T(128)S(1)} %add_rsqrt_fusion, bf16[72,2048]{1,0:T(8,128)(2,1)} %get-tuple-element.193, bf16[8,72,2048]{2,1,0:T(8,128)(2,1)} %get-tuple-element.191, s32[]{:T(128)} %get-tuple-element.192, ...), kind=kOutput, calls=%fused_computation.4 | convolution fusion | flops 1209876480 | bytes 18254112 | tf_op jit(solution)/shard_map/while/body/eval_jaxpr/cond/branch_1_fun/dot_general | solution.py:24
  387.7 1.7 copy.30
  391.8 6.0 collective-permute-done
  397.8 12.8 %conditional.2 = (bf16[72,2048]{1,0:T(8,128)(2,1)}, bf16[1,72,2048]{2,1,0:T(8,128)(2,1)}) conditional(s32[]{:T(128)} %convert_element_type.108, () %tuple.53, (pred[]{:T(512)}, bf16[8,72,2048]{2,1,0:T(8,128)(2,1)}, s32[]{:T(128)}, bf16[72,2048]{1,0:T(8,128)(2,1)}, bf16[2048,2048]{1,0:T(8,128)(2,1)}, /*index=5*/bf16[2048,2048]{1,0:T(8,128)(2,1)}) %tuple.54), branch_computations={%region_1.1_spmd, %region_2.3_spmd} | conditional | flops 1210466432 | bytes 19434644 | solution.py:55
  399.0 9.8 %fusion = bf16[72,2048]{1,0:T(8,128)(2,1)} fusion(bf16[2048,2048]{1,0:T(8,128)(2,1)} %get-tuple-element.195, bf16[2048,2048]{1,0:T(8,128)(2,1)} %get-tuple-element.194, f32[72]{0:T(128)S(1)} %add_rsqrt_fusion, bf16[72,2048]{1,0:T(8,128)(2,1)} %get-tuple-element.193, bf16[8,72,2048]{2,1,0:T(8,128)(2,1)} %get-tuple-element.191, s32[]{:T(128)} %get-tuple-element.192, ...), kind=kOutput, calls=%fused_computation.4 | convolution fusion | flops 1209876480 | bytes 18254112 | tf_op jit(solution)/shard_map/while/body/eval_jaxpr/cond/branch_1_fun/dot_general | solution.py:24
  408.9 1.7 copy.30
  412.9 6.0 collective-permute-done
  418.9 12.8 %conditional.2 = (bf16[72,2048]{1,0:T(8,128)(2,1)}, bf16[1,72,2048]{2,1,0:T(8,128)(2,1)}) conditional(s32[]{:T(128)} %convert_element_type.108, () %tuple.53, (pred[]{:T(512)}, bf16[8,72,2048]{2,1,0:T(8,128)(2,1)}, s32[]{:T(128)}, bf16[72,2048]{1,0:T(8,128)(2,1)}, bf16[2048,2048]{1,0:T(8,128)(2,1)}, /*index=5*/bf16[2048,2048]{1,0:T(8,128)(2,1)}) %tuple.54), branch_computations={%region_1.1_spmd, %region_2.3_spmd} | conditional | flops 1210466432 | bytes 19434644 | solution.py:55
  420.2 9.8 %fusion = bf16[72,2048]{1,0:T(8,128)(2,1)} fusion(bf16[2048,2048]{1,0:T(8,128)(2,1)} %get-tuple-element.195, bf16[2048,2048]{1,0:T(8,128)(2,1)} %get-tuple-element.194, f32[72]{0:T(128)S(1)} %add_rsqrt_fusion, bf16[72,2048]{1,0:T(8,128)(2,1)} %get-tuple-element.193, bf16[8,72,2048]{2,1,0:T(8,128)(2,1)} %get-tuple-element.191, s32[]{:T(128)} %get-tuple-element.192, ...), kind=kOutput, calls=%fused_computation.4 | convolution fusion | flops 1209876480 | bytes 18254112 | tf_op jit(solution)/shard_map/while/body/eval_jaxpr/cond/branch_1_fun/dot_general | solution.py:24
  430.0 1.7 copy.30
  434.1 6.0 collective-permute-done
  440.1 12.8 %conditional.2 = (bf16[72,2048]{1,0:T(8,128)(2,1)}, bf16[1,72,2048]{2,1,0:T(8,128)(2,1)}) conditional(s32[]{:T(128)} %convert_element_type.108, () %tuple.53, (pred[]{:T(512)}, bf16[8,72,2048]{2,1,0:T(8,128)(2,1)}, s32[]{:T(128)}, bf16[72,2048]{1,0:T(8,128)(2,1)}, bf16[2048,2048]{1,0:T(8,128)(2,1)}, /*index=5*/bf16[2048,2048]{1,0:T(8,128)(2,1)}) %tuple.54), branch_computations={%region_1.1_spmd, %region_2.3_spmd} | conditional | flops 1210466432 | bytes 19434644 | solution.py:55
  441.3 9.8 %fusion = bf16[72,2048]{1,0:T(8,128)(2,1)} fusion(bf16[2048,2048]{1,0:T(8,128)(2,1)} %get-tuple-element.195, bf16[2048,2048]{1,0:T(8,128)(2,1)} %get-tuple-element.194, f32[72]{0:T(128)S(1)} %add_rsqrt_fusion, bf16[72,2048]{1,0:T(8,128)(2,1)} %get-tuple-element.193, bf16[8,72,2048]{2,1,0:T(8,128)(2,1)} %get-tuple-element.191, s32[]{:T(128)} %get-tuple-element.192, ...), kind=kOutput, calls=%fused_computation.4 | convolution fusion | flops 1209876480 | bytes 18254112 | tf_op jit(solution)/shard_map/while/body/eval_jaxpr/cond/branch_1_fun/dot_general | solution.py:24
  451.2 1.7 copy.30
  455.2 6.0 collective-permute-done
  461.2 12.8 %conditional.2 = (bf16[72,2048]{1,0:T(8,128)(2,1)}, bf16[1,72,2048]{2,1,0:T(8,128)(2,1)}) conditional(s32[]{:T(128)} %convert_element_type.108, () %tuple.53, (pred[]{:T(512)}, bf16[8,72,2048]{2,1,0:T(8,128)(2,1)}, s32[]{:T(128)}, bf16[72,2048]{1,0:T(8,128)(2,1)}, bf16[2048,2048]{1,0:T(8,128)(2,1)}, /*index=5*/bf16[2048,2048]{1,0:T(8,128)(2,1)}) %tuple.54), branch_computations={%region_1.1_spmd, %region_2.3_spmd} | conditional | flops 1210466432 | bytes 19434644 | solution.py:55
  462.5 9.8 %fusion = bf16[72,2048]{1,0:T(8,128)(2,1)} fusion(bf16[2048,2048]{1,0:T(8,128)(2,1)} %get-tuple-element.195, bf16[2048,2048]{1,0:T(8,128)(2,1)} %get-tuple-element.194, f32[72]{0:T(128)S(1)} %add_rsqrt_fusion, bf16[72,2048]{1,0:T(8,128)(2,1)} %get-tuple-element.193, bf16[8,72,2048]{2,1,0:T(8,128)(2,1)} %get-tuple-element.191, s32[]{:T(128)} %get-tuple-element.192, ...), kind=kOutput, calls=%fused_computation.4 | convolution fusion | flops 1209876480 | bytes 18254112 | tf_op jit(solution)/shard_map/while/body/eval_jaxpr/cond/branch_1_fun/dot_general | solution.py:24
  472.4 1.7 copy.30
  476.4 6.0 collective-permute-done
  482.4 12.8 %conditional.2 = (bf16[72,2048]{1,0:T(8,128)(2,1)}, bf16[1,72,2048]{2,1,0:T(8,128)(2,1)}) conditional(s32[]{:T(128)} %convert_element_type.108, () %tuple.53, (pred[]{:T(512)}, bf16[8,72,2048]{2,1,0:T(8,128)(2,1)}, s32[]{:T(128)}, bf16[72,2048]{1,0:T(8,128)(2,1)}, bf16[2048,2048]{1,0:T(8,128)(2,1)}, /*index=5*/bf16[2048,2048]{1,0:T(8,128)(2,1)}) %tuple.54), branch_computations={%region_1.1_spmd, %region_2.3_spmd} | conditional | flops 1210466432 | bytes 19434644 | solution.py:55
  483.7 9.8 %fusion = bf16[72,2048]{1,0:T(8,128)(2,1)} fusion(bf16[2048,2048]{1,0:T(8,128)(2,1)} %get-tuple-element.195, bf16[2048,2048]{1,0:T(8,128)(2,1)} %get-tuple-element.194, f32[72]{0:T(128)S(1)} %add_rsqrt_fusion, bf16[72,2048]{1,0:T(8,128)(2,1)} %get-tuple-element.193, bf16[8,72,2048]{2,1,0:T(8,128)(2,1)} %get-tuple-element.191, s32[]{:T(128)} %get-tuple-element.192, ...), kind=kOutput, calls=%fused_computation.4 | convolution fusion | flops 1209876480 | bytes 18254112 | tf_op jit(solution)/shard_map/while/body/eval_jaxpr/cond/branch_1_fun/dot_general | solution.py:24
  493.5 1.7 copy.30
  499.0 1.8 gather_fusion
  503.0 1.9 copy.25
  504.9 3.7 reshape.112
  508.6 1.9 convolution_convert_fusion
  510.5 1.7 fusion.43
  512.7 2.1 collective-permute-start.1
  516.1 2.1 collective-permute-start.3
  518.2 2.1 collective-permute-start.4
  520.3 2.1 collective-permute-start.5
  522.4 2.1 collective-permute-start.6
  525.3 2.1 collective-permute-start.7
  528.6 6.0 collective-permute-done.4
  534.6 6.0 collective-permute-done.5
  540.6 1.7 fusion.36
  543.3 15.7 %all_to_all.10 = bf16[32,2,2048]{2,1,0:T(2,128)(2,1)} all-to-all(bf16[32,2,2048]{2,1,0:T(2,128)(2,1)S(1)} %reshape.117), channel_id=1, replica_groups=mesh['section'=8,'expert'=32] {'expert'}, dimensions={0} | all-to-all | bytes 524288 | tf_op jit(solution)/shard_map/all_to_all | solution.py:93
  559.2 24.6 %all-gather.8.cloned.1.call-done = bf16[256,2,2048]{2,1,0:T(2,128)(2,1)} async-done(((bf16[32,2,2048]{2,1,0:T(2,128)(2,1)}), bf16[256,2,2048]{2,1,0:T(2,128)(2,1)}) %all-gather.8.cloned.1.call-update) | async-done | bytes 2097168 | tf_op jit(solution)/shard_map/all_gather | solution.py:94
  583.8 2.7 reshape.118
  588.0 4.9 multiply_convert_fusion.2
  593.0 36.3 %reduce-scatter.2.cloned.1.call-done = bf16[512,256]{1,0:T(8,128)(2,1)} async-done(((bf16[512,2048]{1,0:T(8,128)(2,1)}), bf16[512,256]{1,0:T(8,128)(2,1)}) %reduce-scatter.2.cloned.1.call-update) | async-done | bytes 262160 | tf_op jit(solution)/shard_map/reduce_scatter | solution.py:105
  631.2 9.3 %all-to-all-start.1 = ((bf16[32,8,2,256]{3,2,1,0:T(2,128)(2,1)}), bf16[32,8,2,256]{3,2,1,0:T(2,128)(2,1)S(1)}, u32[]{:S(2)}, u32[]{:S(2)}) async-start(bf16[32,8,2,256]{3,2,1,0:T(2,128)(2,1)} %bitcast.85), calls=%async_computation.2 | async-start | bytes 524288 | tf_op jit(solution)/shard_map/all_to_all | solution.py:107
  640.7 12.6 %all-to-all-done.1 = bf16[32,8,2,256]{3,2,1,0:T(2,128)(2,1)S(1)} async-done(((bf16[32,8,2,256]{3,2,1,0:T(2,128)(2,1)}), bf16[32,8,2,256]{3,2,1,0:T(2,128)(2,1)S(1)}, u32[]{:S(2)}, u32[]{:S(2)}) %all-to-all-start.1) | async-done | bytes 262176 | tf_op jit(solution)/shard_map/all_to_all | solution.py:107
  653.4 2.1 scatter_custom_fusion
  (124 shorter events, 77.6 us)
Async XLA Ops:
  6.5 581.4 %copy-start = (bf16[1,256,2048]{2,1,0:T(8,128)(2,1)S(1)}, bf16[1,256,2048]{2,1,0:T(8,128)(2,1)}, u32[]{:S(2)}) copy-start(bf16[1,256,2048]{2,1,0:T(8,128)(2,1)} %param.17) | copy-start | bytes 3145732
  6.5 103.5 %all-gather.4.cloned.1.call-start = ((), (), s32[]{:S(2)}) async-start(), calls=%async_computation.3 | async-start | bytes 8650752 | tf_op jit(solution)/shard_map/all_gather | solution.py:35
  7.3 200.3 %all-gather.6.cloned.1.call-start = ((), (), s32[]{:S(2)}) async-start(), calls=%async_computation.4 | async-start | bytes 8650752 | tf_op jit(solution)/shard_map/all_gather | solution.py:36
  8.0 575.8 %all-gather.8.cloned.1.call-start = ((), (), s32[]{:S(2)}) async-start(), calls=%async_computation.5 | async-start | bytes 2359296 | tf_op jit(solution)/shard_map/all_gather | solution.py:94
  210.1 4.7 collective-permute-start
  216.3 8.3 %collective-permute-start = (bf16[72,2048]{1,0:T(8,128)(2,1)}, bf16[72,2048]{1,0:T(8,128)(2,1)}, u32[]{:S(2)}, u32[]{:S(2)}) collective-permute-start(bf16[72,2048]{1,0:T(8,128)(2,1)} %get-tuple-element.294), channel_id=1, source_target_pairs={{0,32},{32,64},{64,96},{96,128},{128,160},{160,192},{192,224},{1,3... | collective-permute-start | bytes 884744 | tf_op jit(solution)/shard_map/while/body/eval_jaxpr/ppermute | solution.py:10
  226.1 8.3 %collective-permute-start = (bf16[72,2048]{1,0:T(8,128)(2,1)}, bf16[72,2048]{1,0:T(8,128)(2,1)}, u32[]{:S(2)}, u32[]{:S(2)}) collective-permute-start(bf16[72,2048]{1,0:T(8,128)(2,1)} %get-tuple-element.294), channel_id=1, source_target_pairs={{0,32},{32,64},{64,96},{96,128},{128,160},{160,192},{192,224},{1,3... | collective-permute-start | bytes 884744 | tf_op jit(solution)/shard_map/while/body/eval_jaxpr/ppermute | solution.py:10
  236.0 8.3 %collective-permute-start = (bf16[72,2048]{1,0:T(8,128)(2,1)}, bf16[72,2048]{1,0:T(8,128)(2,1)}, u32[]{:S(2)}, u32[]{:S(2)}) collective-permute-start(bf16[72,2048]{1,0:T(8,128)(2,1)} %get-tuple-element.294), channel_id=1, source_target_pairs={{0,32},{32,64},{64,96},{96,128},{128,160},{160,192},{192,224},{1,3... | collective-permute-start | bytes 884744 | tf_op jit(solution)/shard_map/while/body/eval_jaxpr/ppermute | solution.py:10
  245.8 8.3 %collective-permute-start = (bf16[72,2048]{1,0:T(8,128)(2,1)}, bf16[72,2048]{1,0:T(8,128)(2,1)}, u32[]{:S(2)}, u32[]{:S(2)}) collective-permute-start(bf16[72,2048]{1,0:T(8,128)(2,1)} %get-tuple-element.294), channel_id=1, source_target_pairs={{0,32},{32,64},{64,96},{96,128},{128,160},{160,192},{192,224},{1,3... | collective-permute-start | bytes 884744 | tf_op jit(solution)/shard_map/while/body/eval_jaxpr/ppermute | solution.py:10
  255.6 8.3 %collective-permute-start = (bf16[72,2048]{1,0:T(8,128)(2,1)}, bf16[72,2048]{1,0:T(8,128)(2,1)}, u32[]{:S(2)}, u32[]{:S(2)}) collective-permute-start(bf16[72,2048]{1,0:T(8,128)(2,1)} %get-tuple-element.294), channel_id=1, source_target_pairs={{0,32},{32,64},{64,96},{96,128},{128,160},{160,192},{192,224},{1,3... | collective-permute-start | bytes 884744 | tf_op jit(solution)/shard_map/while/body/eval_jaxpr/ppermute | solution.py:10
  265.4 68.8 %collective-permute-start = (bf16[72,2048]{1,0:T(8,128)(2,1)}, bf16[72,2048]{1,0:T(8,128)(2,1)}, u32[]{:S(2)}, u32[]{:S(2)}) collective-permute-start(bf16[72,2048]{1,0:T(8,128)(2,1)} %get-tuple-element.294), channel_id=1, source_target_pairs={{0,32},{32,64},{64,96},{96,128},{128,160},{160,192},{192,224},{1,3... | collective-permute-start | bytes 884744 | tf_op jit(solution)/shard_map/while/body/eval_jaxpr/ppermute | solution.py:10
  347.1 8.4 %collective-permute-start = (bf16[72,2048]{1,0:T(8,128)(2,1)}, bf16[72,2048]{1,0:T(8,128)(2,1)}, u32[]{:S(2)}, u32[]{:S(2)}) collective-permute-start(bf16[72,2048]{1,0:T(8,128)(2,1)} %get-tuple-element.294), channel_id=1, source_target_pairs={{0,32},{32,64},{64,96},{96,128},{128,160},{160,192},{192,224},{1,3... | collective-permute-start | bytes 884744 | tf_op jit(solution)/shard_map/while/body/eval_jaxpr/ppermute | solution.py:10
  368.3 8.3 %collective-permute-start = (bf16[72,2048]{1,0:T(8,128)(2,1)}, bf16[72,2048]{1,0:T(8,128)(2,1)}, u32[]{:S(2)}, u32[]{:S(2)}) collective-permute-start(bf16[72,2048]{1,0:T(8,128)(2,1)} %get-tuple-element.294), channel_id=1, source_target_pairs={{0,32},{32,64},{64,96},{96,128},{128,160},{160,192},{192,224},{1,3... | collective-permute-start | bytes 884744 | tf_op jit(solution)/shard_map/while/body/eval_jaxpr/ppermute | solution.py:10
  389.4 8.3 %collective-permute-start = (bf16[72,2048]{1,0:T(8,128)(2,1)}, bf16[72,2048]{1,0:T(8,128)(2,1)}, u32[]{:S(2)}, u32[]{:S(2)}) collective-permute-start(bf16[72,2048]{1,0:T(8,128)(2,1)} %get-tuple-element.294), channel_id=1, source_target_pairs={{0,32},{32,64},{64,96},{96,128},{128,160},{160,192},{192,224},{1,3... | collective-permute-start | bytes 884744 | tf_op jit(solution)/shard_map/while/body/eval_jaxpr/ppermute | solution.py:10
  410.6 8.3 %collective-permute-start = (bf16[72,2048]{1,0:T(8,128)(2,1)}, bf16[72,2048]{1,0:T(8,128)(2,1)}, u32[]{:S(2)}, u32[]{:S(2)}) collective-permute-start(bf16[72,2048]{1,0:T(8,128)(2,1)} %get-tuple-element.294), channel_id=1, source_target_pairs={{0,32},{32,64},{64,96},{96,128},{128,160},{160,192},{192,224},{1,3... | collective-permute-start | bytes 884744 | tf_op jit(solution)/shard_map/while/body/eval_jaxpr/ppermute | solution.py:10
  431.7 8.3 %collective-permute-start = (bf16[72,2048]{1,0:T(8,128)(2,1)}, bf16[72,2048]{1,0:T(8,128)(2,1)}, u32[]{:S(2)}, u32[]{:S(2)}) collective-permute-start(bf16[72,2048]{1,0:T(8,128)(2,1)} %get-tuple-element.294), channel_id=1, source_target_pairs={{0,32},{32,64},{64,96},{96,128},{128,160},{160,192},{192,224},{1,3... | collective-permute-start | bytes 884744 | tf_op jit(solution)/shard_map/while/body/eval_jaxpr/ppermute | solution.py:10
  452.9 8.3 %collective-permute-start = (bf16[72,2048]{1,0:T(8,128)(2,1)}, bf16[72,2048]{1,0:T(8,128)(2,1)}, u32[]{:S(2)}, u32[]{:S(2)}) collective-permute-start(bf16[72,2048]{1,0:T(8,128)(2,1)} %get-tuple-element.294), channel_id=1, source_target_pairs={{0,32},{32,64},{64,96},{96,128},{128,160},{160,192},{192,224},{1,3... | collective-permute-start | bytes 884744 | tf_op jit(solution)/shard_map/while/body/eval_jaxpr/ppermute | solution.py:10
  474.0 8.3 %collective-permute-start = (bf16[72,2048]{1,0:T(8,128)(2,1)}, bf16[72,2048]{1,0:T(8,128)(2,1)}, u32[]{:S(2)}, u32[]{:S(2)}) collective-permute-start(bf16[72,2048]{1,0:T(8,128)(2,1)} %get-tuple-element.294), channel_id=1, source_target_pairs={{0,32},{32,64},{64,96},{96,128},{128,160},{160,192},{192,224},{1,3... | collective-permute-start | bytes 884744 | tf_op jit(solution)/shard_map/while/body/eval_jaxpr/ppermute | solution.py:10
  495.2 3.8 collective-permute-start
  510.4 2.3 copy-start.1
  512.7 9.7 %collective-permute-start.1 = (bf16[136,2048]{1,0:T(8,128)(2,1)S(1)}, bf16[136,2048]{1,0:T(8,128)(2,1)S(1)}, u32[]{:S(2)}, u32[]{:S(2)}) collective-permute-start(bf16[136,2048]{1,0:T(8,128)(2,1)S(1)} %get-tuple-element.231), channel_id=1, source_target_pairs={{224,192},{225,193},{226,194},{227,195},{228,196},{229,197},{230,1... | collective-permute-start | bytes 1671176 | tf_op jit(solution)/shard_map/ppermute | solution.py:88
  514.8 9.7 %collective-permute-start.2 = (bf16[136,2048]{1,0:T(8,128)(2,1)S(1)}, bf16[136,2048]{1,0:T(8,128)(2,1)S(1)}, u32[]{:S(2)}, u32[]{:S(2)}) collective-permute-start(bf16[136,2048]{1,0:T(8,128)(2,1)S(1)} %get-tuple-element.232), channel_id=1, source_target_pairs={{224,160},{225,161},{226,162},{227,163},{228,164},{229,165},{230,1... | collective-permute-start | bytes 1671176 | tf_op jit(solution)/shard_map/ppermute | solution.py:88
  516.1 12.5 %collective-permute-start.3 = (bf16[136,2048]{1,0:T(8,128)(2,1)}, bf16[136,2048]{1,0:T(8,128)(2,1)}, u32[]{:S(2)}, u32[]{:S(2)}) collective-permute-start(bf16[136,2048]{1,0:T(8,128)(2,1)} %get-tuple-element.233), channel_id=1, source_target_pairs={{224,128},{225,129},{226,130},{227,131},{228,132},{229,133},{230,1... | collective-permute-start | bytes 1671176 | tf_op jit(solution)/shard_map/ppermute | solution.py:88
  518.2 16.3 %collective-permute-start.4 = (bf16[136,2048]{1,0:T(8,128)(2,1)}, bf16[136,2048]{1,0:T(8,128)(2,1)}, u32[]{:S(2)}, u32[]{:S(2)}) collective-permute-start(bf16[136,2048]{1,0:T(8,128)(2,1)} %get-tuple-element.234), channel_id=1, source_target_pairs={{224,96},{225,97},{226,98},{227,99},{228,100},{229,101},{230,102},... | collective-permute-start | bytes 1671176 | tf_op jit(solution)/shard_map/ppermute | solution.py:88
  520.3 20.2 %collective-permute-start.5 = (bf16[136,2048]{1,0:T(8,128)(2,1)}, bf16[136,2048]{1,0:T(8,128)(2,1)}, u32[]{:S(2)}, u32[]{:S(2)}) collective-permute-start(bf16[136,2048]{1,0:T(8,128)(2,1)} %get-tuple-element.235), channel_id=1, source_target_pairs={{224,64},{225,65},{226,66},{227,67},{228,68},{229,69},{230,70},{23... | collective-permute-start | bytes 1671176 | tf_op jit(solution)/shard_map/ppermute | solution.py:88
  522.4 2.1 copy-start.4
  522.4 18.1 %collective-permute-start.6 = (bf16[136,2048]{1,0:T(8,128)(2,1)}, bf16[136,2048]{1,0:T(8,128)(2,1)}, u32[]{:S(2)}, u32[]{:S(2)}) collective-permute-start(bf16[136,2048]{1,0:T(8,128)(2,1)} %get-tuple-element.236), channel_id=1, source_target_pairs={{224,32},{225,33},{226,34},{227,35},{228,36},{229,37},{230,38},{23... | collective-permute-start | bytes 1671176 | tf_op jit(solution)/shard_map/ppermute | solution.py:88
  524.5 0.8 copy-start.5
  525.3 15.2 %collective-permute-start.7 = (bf16[136,2048]{1,0:T(8,128)(2,1)}, bf16[136,2048]{1,0:T(8,128)(2,1)}, u32[]{:S(2)}, u32[]{:S(2)}) collective-permute-start(bf16[136,2048]{1,0:T(8,128)(2,1)} %get-tuple-element.230), channel_id=1, source_target_pairs={{224,0},{225,1},{226,2},{227,3},{228,4},{229,5},{230,6},{231,7},{2... | collective-permute-start | bytes 1671176 | tf_op jit(solution)/shard_map/ppermute | solution.py:88
  542.3 0.8 copy-start.2
  559.0 70.3 %reduce-scatter.2.cloned.1.call-start = ((), (), s32[]{:S(2)}) async-start(), calls=%async_computation.6 | async-start | bytes 2359296 | tf_op jit(solution)/shard_map/reduce_scatter | solution.py:105
  588.0 4.9 copy-start.6
  592.9 47.7 %copy-start.3 = (bf16[136,2048]{1,0:T(8,128)(2,1)S(1)}, bf16[136,2048]{1,0:T(8,128)(2,1)}, u32[]{:S(2)}) copy-start(bf16[136,2048]{1,0:T(8,128)(2,1)} %copy-done.2) | copy-start | bytes 1671172
  631.2 22.1 %all-to-all-start.1 = ((bf16[32,8,2,256]{3,2,1,0:T(2,128)(2,1)}), bf16[32,8,2,256]{3,2,1,0:T(2,128)(2,1)S(1)}, u32[]{:S(2)}, u32[]{:S(2)}) async-start(bf16[32,8,2,256]{3,2,1,0:T(2,128)(2,1)} %bitcast.85), calls=%async_computation.2 | async-start | bytes 524288 | tf_op jit(solution)/shard_map/all_to_all | solution.py:107
Sparse Core Ops, SparseCore 0:
  9.9 100.0 all-gather.3
  112.6 94.9 all-gather.5
  559.1 24.6 all-gather.7
  593.0 36.1 reduce-scatter.1

commit v2 on v1

--- a/solution.py
+++ b/solution.py
@@ -8,6 +8,31 @@
     count = lax.axis_size(axis)
     initial, last = (max(0, -steps), min(count, count - steps))
     return lax.ppermute(value, axis, [(source, source + steps) for source in range(initial, last)])
+
+
+def ring_gather(chunk, axis, size, stride):
+    index = lax.axis_index(axis)
+    count = lax.axis_size(axis)
+    place = (index // stride) % size
+
+    def shifted(step):
+        pairs = []
+        for member in range(count):
+            at = (member // stride) % size
+            to = member + (((at + step) % size) - at) * stride
+            pairs.append((member, to))
+        return pairs
+
+    out = jnp.zeros((size,) + chunk.shape, chunk.dtype)
+    out = lax.dynamic_update_index_in_dim(out, chunk, place, 0)
+    ahead, behind = chunk, chunk
+    for step in range(1, size // 2 + 1):
+        ahead = lax.ppermute(ahead, axis, shifted(1))
+        out = lax.dynamic_update_index_in_dim(out, ahead, (place - step) % size, 0)
+        if step < size - step:
+            behind = lax.ppermute(behind, axis, shifted(-1))
+            out = lax.dynamic_update_index_in_dim(out, behind, (place + step) % size, 0)
+    return out
 
 
 def normalize(rows):
@@ -31,12 +56,11 @@
     section = lax.axis_index("section")
     expert_index = lax.axis_index("expert")
     micro, tok_dev, width = tokens.shape
-    w_first, w_second = (
-        lax.all_gather(w_in, "expert", axis=1, tiled=True),
-        lax.all_gather(w_out, "expert", axis=1, tiled=True),
-    )
-    w_first = w_first[0]
-    w_second = w_second[0]
+    w_first = lax.all_gather(w_in, "expert", axis=1, tiled=True)[0]
+    inner = 4 if n_expert % 4 == 0 else 1
+    w_second = ring_gather(w_out[0], "expert", inner, 1)
+    w_second = ring_gather(w_second, "expert", n_expert // inner, inner)
+    w_second = w_second.reshape(-1, width)
     last = n_section - 1
 
     def run_layer(stream):

time: 665 us -> 632 us (0.950)
  waiting for transfers between devices: 432 us -> 372 us
  local copies, waits for them, and re-layouts: 40.5 us -> 56.9 us
  starting transfers between devices: 42.7 us -> 57.2 us
    all_gather x2 -> x1, waiting for transfers between devices: 195 us -> 0.01 us  [local(): w_first = lax.all_gather(w_in, 'expert', axis=1, tiled=True)[0]]
    ppermute x0 -> x10, waiting for transfers between devices: none -> 133 us  [the longest x6 133 us: ring_gather(): ahead = lax.ppermute(ahead, axis, shifted(1))]
    ppermute x0 -> x10, starting transfers between devices: none -> 14.7 us  [the longest x4 11.6 us: ring_gather(): behind = lax.ppermute(behind, axis, shifted(-1))]
    dynamic_update_slice x0 -> x12, local copies, waits for them, and re-layouts: none -> 10.9 us  [the longest x6 5.59 us: ring_gather(): out = lax.dynamic_update_index_in_dim(out, ahead, (place - step) % size, 0)]
  transfers between devices with their start and end apart: 27 -> 36, of which waited for: 23 -> 27; matrix products, arithmetic and copies ran while one was open for 2% -> 4% of each run, Pallas kernels for 0% -> 0%
where the time goes in v2:
time: 632 us; the launch traced here: 631 us
  waiting for transfers between devices  372 us (59%)
  matrix products  87 us (14%)
  starting transfers between devices  57.2 us (9%)
  local copies, waits for them, and re-layouts  56.9 us (9%)
  other arithmetic  27.9 us (4%)
  blocking collectives  16.2 us (3%)
  between operations  13.4 us (2%)
    ppermute x15, waiting for transfers between devices, from_behind(): lax.ppermute(value, axis, [(source, source + steps) for source in range(i...  151 us
    ppermute x6, waiting for transfers between devices, ring_gather(): ahead = lax.ppermute(ahead, axis, shifted(1))  133 us
    dot_general x8, matrix products, processor(): branch = jnp.dot(hidden, w_second, preferred_element_type=jnp.float32)  78.8 us
    reduce_scatter x1, waiting for transfers between devices, local(): lax.psum_scatter(scaled, 'section', scatter_dimension=1, tiled=True)  36.3 us
    all_gather x1, waiting for transfers between devices, local(): lax.all_gather(arrived, 'section', axis=0, tiled=True).reshape(-1, width)  24.7 us
    ppermute x15, starting transfers between devices, from_behind(): lax.ppermute(value, axis, [(source, source + steps) for source in range(i...  19.2 us
    all_to_all x1, blocking collectives, local(): lax.all_to_all(outgoing, 'expert', split_axis=0, concat_axis=0, tiled=True)  16.2 us
    ppermute x7, starting transfers between devices, local(): got = lax.ppermute(payload[target], 'section', [(last, target)])  13.9 us
  transfers between devices with their start and end apart: 36, of which 27 were waited for; matrix products, arithmetic and copies ran while one was open for 4% of the time, Pallas kernels for 0%

profile of v2, /device:TPU:7, one launch (start us, length us, event | category | flops | bytes accessed | tf_op | source)
XLA Modules:
  0.0 630.6 jit_solution(1205923773174565510)
XLA Ops:
  11.3 4.8 collective-permute-done.1
  16.2 7.5 %collective-permute-done.3 = bf16[64,2048]{1,0:T(8,128)(2,1)S(1)} collective-permute-done((bf16[64,2048]{1,0:T(8,128)(2,1)S(1)}, bf16[64,2048]{1,0:T(8,128)(2,1)S(1)}, u32[]{:S(2)}, u32[]{:S(2)}) %collective-permute-start.3) | collective-permute-done | bytes 262176 | tf_op jit(solution)/shard_map/ppermute | solution.py:30
  25.5 4.0 collective-permute-start.5
  30.5 30.7 %collective-permute-done.4 = bf16[4,64,2048]{2,1,0:T(8,128)(2,1)} collective-permute-done((bf16[4,64,2048]{2,1,0:T(8,128)(2,1)S(1)}, bf16[4,64,2048]{2,1,0:T(8,128)(2,1)}, u32[]{:S(2)}, u32[]{:S(2)}) %collective-permute-start.4) | collective-permute-done | bytes 1048608 | tf_op jit(solution)/shard_map/ppermute | solution.py:30
  61.2 2.7 collective-permute-start.7
  64.0 4.4 broadcast_in_dim.89
  69.5 31.6 %collective-permute-done.6 = bf16[4,64,2048]{2,1,0:T(8,128)(2,1)S(1)} collective-permute-done((bf16[4,64,2048]{2,1,0:T(8,128)(2,1)}, bf16[4,64,2048]{2,1,0:T(8,128)(2,1)S(1)}, u32[]{:S(2)}, u32[]{:S(2)}) %collective-permute-start.6) | collective-permute-done | bytes 1048608 | tf_op jit(solution)/shard_map/ppermute | solution.py:30
  101.1 2.4 bitcast_dynamic-update-slice_fusion.6
  104.5 3.3 collective-permute-start.9
  108.8 38.1 %collective-permute-done.8 = bf16[4,64,2048]{2,1,0:T(8,128)(2,1)S(1)} collective-permute-done((bf16[4,64,2048]{2,1,0:T(8,128)(2,1)S(1)}, bf16[4,64,2048]{2,1,0:T(8,128)(2,1)S(1)}, u32[]{:S(2)}, u32[]{:S(2)}) %collective-permute-start.8) | collective-permute-done | bytes 1048608 | tf_op jit(solution)/shard_map/ppermute | solution.py:30
  150.1 19.8 %collective-permute-done.10 = bf16[4,64,2048]{2,1,0:T(8,128)(2,1)S(1)} collective-permute-done((bf16[4,64,2048]{2,1,0:T(8,128)(2,1)S(1)}, bf16[4,64,2048]{2,1,0:T(8,128)(2,1)S(1)}, u32[]{:S(2)}, u32[]{:S(2)}) %collective-permute-start.10) | collective-permute-done | bytes 1048608 | tf_op jit(solution)/shard_map/ppermute | solution.py:30
  172.0 292.9 %while.16 = (s32[]{:T(128)}, bf16[72,2048]{1,0:T(8,128)(2,1)}, bf16[8,72,2048]{2,1,0:T(8,128)(2,1)S(1)}, s32[]{:T(128)}, pred[]{:T(512)}, /*index=5*/bf16[8,72,2...) while((s32[]{:T(128)}, bf16[72,2048]{1,0:T(8,128)(2,1)}, ...), condition=%wide.region_4.5_spmd, body=%wide.region_0.4_spmd.sunk | while | flops 1210613888 | bytes 21499308 | solution.py:86
  174.9 5.8 collective-permute-done
  183.5 6.9 %collective-permute-done = bf16[72,2048]{1,0:T(8,128)(2,1)} collective-permute-done((bf16[72,2048]{1,0:T(8,128)(2,1)}, bf16[72,2048]{1,0:T(8,128)(2,1)}, u32[]{:S(2)}, u32[]{:S(2)}) %collective-permute-start) | collective-permute-done | bytes 294944 | tf_op jit(solution)/shard_map/while/body/eval_jaxpr/ppermute | solution.py:10
  193.3 6.9 %collective-permute-done = bf16[72,2048]{1,0:T(8,128)(2,1)} collective-permute-done((bf16[72,2048]{1,0:T(8,128)(2,1)}, bf16[72,2048]{1,0:T(8,128)(2,1)}, u32[]{:S(2)}, u32[]{:S(2)}) %collective-permute-start) | collective-permute-done | bytes 294944 | tf_op jit(solution)/shard_map/while/body/eval_jaxpr/ppermute | solution.py:10
  203.2 6.9 %collective-permute-done = bf16[72,2048]{1,0:T(8,128)(2,1)} collective-permute-done((bf16[72,2048]{1,0:T(8,128)(2,1)}, bf16[72,2048]{1,0:T(8,128)(2,1)}, u32[]{:S(2)}, u32[]{:S(2)}) %collective-permute-start) | collective-permute-done | bytes 294944 | tf_op jit(solution)/shard_map/while/body/eval_jaxpr/ppermute | solution.py:10
  213.0 6.9 %collective-permute-done = bf16[72,2048]{1,0:T(8,128)(2,1)} collective-permute-done((bf16[72,2048]{1,0:T(8,128)(2,1)}, bf16[72,2048]{1,0:T(8,128)(2,1)}, u32[]{:S(2)}, u32[]{:S(2)}) %collective-permute-start) | collective-permute-done | bytes 294944 | tf_op jit(solution)/shard_map/while/body/eval_jaxpr/ppermute | solution.py:10
  222.8 6.9 %collective-permute-done = bf16[72,2048]{1,0:T(8,128)(2,1)} collective-permute-done((bf16[72,2048]{1,0:T(8,128)(2,1)}, bf16[72,2048]{1,0:T(8,128)(2,1)}, u32[]{:S(2)}, u32[]{:S(2)}) %collective-permute-start) | collective-permute-done | bytes 294944 | tf_op jit(solution)/shard_map/while/body/eval_jaxpr/ppermute | solution.py:10
  232.6 67.6 %collective-permute-done = bf16[72,2048]{1,0:T(8,128)(2,1)} collective-permute-done((bf16[72,2048]{1,0:T(8,128)(2,1)}, bf16[72,2048]{1,0:T(8,128)(2,1)}, u32[]{:S(2)}, u32[]{:S(2)}) %collective-permute-start) | collective-permute-done | bytes 294944 | tf_op jit(solution)/shard_map/while/body/eval_jaxpr/ppermute | solution.py:10
  300.2 12.8 %conditional.2 = (bf16[72,2048]{1,0:T(8,128)(2,1)}, bf16[1,72,2048]{2,1,0:T(8,128)(2,1)}) conditional(s32[]{:T(128)} %convert_element_type.108, () %tuple.54, (pred[]{:T(512)}, bf16[8,72,2048]{2,1,0:T(8,128)(2,1)}, s32[]{:T(128)}, bf16[72,2048]{1,0:T(8,128)(2,1)}, bf16[2048,2048]{1,0:T(8,128)(2,1)}, /*index=5*/bf16[2048,2048]{1,0:T(8,128)(2,1)}) %tuple.55), branch_computations={%region_1.1_spmd, %region_2.3_spmd} | conditional | flops 1210466432 | bytes 19434644 | solution.py:79
  301.5 9.8 %fusion = bf16[72,2048]{1,0:T(8,128)(2,1)} fusion(bf16[2048,2048]{1,0:T(8,128)(2,1)} %get-tuple-element.195, bf16[2048,2048]{1,0:T(8,128)(2,1)} %get-tuple-element.194, f32[72]{0:T(128)S(1)} %add_rsqrt_fusion, bf16[72,2048]{1,0:T(8,128)(2,1)} %get-tuple-element.193, bf16[8,72,2048]{2,1,0:T(8,128)(2,1)} %get-tuple-element.191, s32[]{:T(128)} %get-tuple-element.192, ...), kind=kOutput, calls=%fused_computation.4 | convolution fusion | flops 1209876480 | bytes 18254112 | tf_op jit(solution)/shard_map/while/body/eval_jaxpr/cond/branch_1_fun/dot_general | solution.py:49
  315.4 6.0 collective-permute-done
  321.4 12.8 %conditional.2 = (bf16[72,2048]{1,0:T(8,128)(2,1)}, bf16[1,72,2048]{2,1,0:T(8,128)(2,1)}) conditional(s32[]{:T(128)} %convert_element_type.108, () %tuple.54, (pred[]{:T(512)}, bf16[8,72,2048]{2,1,0:T(8,128)(2,1)}, s32[]{:T(128)}, bf16[72,2048]{1,0:T(8,128)(2,1)}, bf16[2048,2048]{1,0:T(8,128)(2,1)}, /*index=5*/bf16[2048,2048]{1,0:T(8,128)(2,1)}) %tuple.55), branch_computations={%region_1.1_spmd, %region_2.3_spmd} | conditional | flops 1210466432 | bytes 19434644 | solution.py:79
  322.6 9.8 %fusion = bf16[72,2048]{1,0:T(8,128)(2,1)} fusion(bf16[2048,2048]{1,0:T(8,128)(2,1)} %get-tuple-element.195, bf16[2048,2048]{1,0:T(8,128)(2,1)} %get-tuple-element.194, f32[72]{0:T(128)S(1)} %add_rsqrt_fusion, bf16[72,2048]{1,0:T(8,128)(2,1)} %get-tuple-element.193, bf16[8,72,2048]{2,1,0:T(8,128)(2,1)} %get-tuple-element.191, s32[]{:T(128)} %get-tuple-element.192, ...), kind=kOutput, calls=%fused_computation.4 | convolution fusion | flops 1209876480 | bytes 18254112 | tf_op jit(solution)/shard_map/while/body/eval_jaxpr/cond/branch_1_fun/dot_general | solution.py:49
  336.5 6.0 collective-permute-done
  342.5 12.8 %conditional.2 = (bf16[72,2048]{1,0:T(8,128)(2,1)}, bf16[1,72,2048]{2,1,0:T(8,128)(2,1)}) conditional(s32[]{:T(128)} %convert_element_type.108, () %tuple.54, (pred[]{:T(512)}, bf16[8,72,2048]{2,1,0:T(8,128)(2,1)}, s32[]{:T(128)}, bf16[72,2048]{1,0:T(8,128)(2,1)}, bf16[2048,2048]{1,0:T(8,128)(2,1)}, /*index=5*/bf16[2048,2048]{1,0:T(8,128)(2,1)}) %tuple.55), branch_computations={%region_1.1_spmd, %region_2.3_spmd} | conditional | flops 1210466432 | bytes 19434644 | solution.py:79
  343.8 9.8 %fusion = bf16[72,2048]{1,0:T(8,128)(2,1)} fusion(bf16[2048,2048]{1,0:T(8,128)(2,1)} %get-tuple-element.195, bf16[2048,2048]{1,0:T(8,128)(2,1)} %get-tuple-element.194, f32[72]{0:T(128)S(1)} %add_rsqrt_fusion, bf16[72,2048]{1,0:T(8,128)(2,1)} %get-tuple-element.193, bf16[8,72,2048]{2,1,0:T(8,128)(2,1)} %get-tuple-element.191, s32[]{:T(128)} %get-tuple-element.192, ...), kind=kOutput, calls=%fused_computation.4 | convolution fusion | flops 1209876480 | bytes 18254112 | tf_op jit(solution)/shard_map/while/body/eval_jaxpr/cond/branch_1_fun/dot_general | solution.py:49
  357.7 6.0 collective-permute-done
  363.7 12.8 %conditional.2 = (bf16[72,2048]{1,0:T(8,128)(2,1)}, bf16[1,72,2048]{2,1,0:T(8,128)(2,1)}) conditional(s32[]{:T(128)} %convert_element_type.108, () %tuple.54, (pred[]{:T(512)}, bf16[8,72,2048]{2,1,0:T(8,128)(2,1)}, s32[]{:T(128)}, bf16[72,2048]{1,0:T(8,128)(2,1)}, bf16[2048,2048]{1,0:T(8,128)(2,1)}, /*index=5*/bf16[2048,2048]{1,0:T(8,128)(2,1)}) %tuple.55), branch_computations={%region_1.1_spmd, %region_2.3_spmd} | conditional | flops 1210466432 | bytes 19434644 | solution.py:79
  364.9 9.8 %fusion = bf16[72,2048]{1,0:T(8,128)(2,1)} fusion(bf16[2048,2048]{1,0:T(8,128)(2,1)} %get-tuple-element.195, bf16[2048,2048]{1,0:T(8,128)(2,1)} %get-tuple-element.194, f32[72]{0:T(128)S(1)} %add_rsqrt_fusion, bf16[72,2048]{1,0:T(8,128)(2,1)} %get-tuple-element.193, bf16[8,72,2048]{2,1,0:T(8,128)(2,1)} %get-tuple-element.191, s32[]{:T(128)} %get-tuple-element.192, ...), kind=kOutput, calls=%fused_computation.4 | convolution fusion | flops 1209876480 | bytes 18254112 | tf_op jit(solution)/shard_map/while/body/eval_jaxpr/cond/branch_1_fun/dot_general | solution.py:49
  378.8 6.0 collective-permute-done
  384.8 12.8 %conditional.2 = (bf16[72,2048]{1,0:T(8,128)(2,1)}, bf16[1,72,2048]{2,1,0:T(8,128)(2,1)}) conditional(s32[]{:T(128)} %convert_element_type.108, () %tuple.54, (pred[]{:T(512)}, bf16[8,72,2048]{2,1,0:T(8,128)(2,1)}, s32[]{:T(128)}, bf16[72,2048]{1,0:T(8,128)(2,1)}, bf16[2048,2048]{1,0:T(8,128)(2,1)}, /*index=5*/bf16[2048,2048]{1,0:T(8,128)(2,1)}) %tuple.55), branch_computations={%region_1.1_spmd, %region_2.3_spmd} | conditional | flops 1210466432 | bytes 19434644 | solution.py:79
  386.1 9.8 %fusion = bf16[72,2048]{1,0:T(8,128)(2,1)} fusion(bf16[2048,2048]{1,0:T(8,128)(2,1)} %get-tuple-element.195, bf16[2048,2048]{1,0:T(8,128)(2,1)} %get-tuple-element.194, f32[72]{0:T(128)S(1)} %add_rsqrt_fusion, bf16[72,2048]{1,0:T(8,128)(2,1)} %get-tuple-element.193, bf16[8,72,2048]{2,1,0:T(8,128)(2,1)} %get-tuple-element.191, s32[]{:T(128)} %get-tuple-element.192, ...), kind=kOutput, calls=%fused_computation.4 | convolution fusion | flops 1209876480 | bytes 18254112 | tf_op jit(solution)/shard_map/while/body/eval_jaxpr/cond/branch_1_fun/dot_general | solution.py:49
  400.0 6.0 collective-permute-done
  406.0 12.8 %conditional.2 = (bf16[72,2048]{1,0:T(8,128)(2,1)}, bf16[1,72,2048]{2,1,0:T(8,128)(2,1)}) conditional(s32[]{:T(128)} %convert_element_type.108, () %tuple.54, (pred[]{:T(512)}, bf16[8,72,2048]{2,1,0:T(8,128)(2,1)}, s32[]{:T(128)}, bf16[72,2048]{1,0:T(8,128)(2,1)}, bf16[2048,2048]{1,0:T(8,128)(2,1)}, /*index=5*/bf16[2048,2048]{1,0:T(8,128)(2,1)}) %tuple.55), branch_computations={%region_1.1_spmd, %region_2.3_spmd} | conditional | flops 1210466432 | bytes 19434644 | solution.py:79
  407.2 9.8 %fusion = bf16[72,2048]{1,0:T(8,128)(2,1)} fusion(bf16[2048,2048]{1,0:T(8,128)(2,1)} %get-tuple-element.195, bf16[2048,2048]{1,0:T(8,128)(2,1)} %get-tuple-element.194, f32[72]{0:T(128)S(1)} %add_rsqrt_fusion, bf16[72,2048]{1,0:T(8,128)(2,1)} %get-tuple-element.193, bf16[8,72,2048]{2,1,0:T(8,128)(2,1)} %get-tuple-element.191, s32[]{:T(128)} %get-tuple-element.192, ...), kind=kOutput, calls=%fused_computation.4 | convolution fusion | flops 1209876480 | bytes 18254112 | tf_op jit(solution)/shard_map/while/body/eval_jaxpr/cond/branch_1_fun/dot_general | solution.py:49
  421.1 6.0 collective-permute-done
  427.1 12.8 %conditional.2 = (bf16[72,2048]{1,0:T(8,128)(2,1)}, bf16[1,72,2048]{2,1,0:T(8,128)(2,1)}) conditional(s32[]{:T(128)} %convert_element_type.108, () %tuple.54, (pred[]{:T(512)}, bf16[8,72,2048]{2,1,0:T(8,128)(2,1)}, s32[]{:T(128)}, bf16[72,2048]{1,0:T(8,128)(2,1)}, bf16[2048,2048]{1,0:T(8,128)(2,1)}, /*index=5*/bf16[2048,2048]{1,0:T(8,128)(2,1)}) %tuple.55), branch_computations={%region_1.1_spmd, %region_2.3_spmd} | conditional | flops 1210466432 | bytes 19434644 | solution.py:79
  428.4 9.8 %fusion = bf16[72,2048]{1,0:T(8,128)(2,1)} fusion(bf16[2048,2048]{1,0:T(8,128)(2,1)} %get-tuple-element.195, bf16[2048,2048]{1,0:T(8,128)(2,1)} %get-tuple-element.194, f32[72]{0:T(128)S(1)} %add_rsqrt_fusion, bf16[72,2048]{1,0:T(8,128)(2,1)} %get-tuple-element.193, bf16[8,72,2048]{2,1,0:T(8,128)(2,1)} %get-tuple-element.191, s32[]{:T(128)} %get-tuple-element.192, ...), kind=kOutput, calls=%fused_computation.4 | convolution fusion | flops 1209876480 | bytes 18254112 | tf_op jit(solution)/shard_map/while/body/eval_jaxpr/cond/branch_1_fun/dot_general | solution.py:49
  442.3 6.0 collective-permute-done
  448.3 12.8 %conditional.2 = (bf16[72,2048]{1,0:T(8,128)(2,1)}, bf16[1,72,2048]{2,1,0:T(8,128)(2,1)}) conditional(s32[]{:T(128)} %convert_element_type.108, () %tuple.54, (pred[]{:T(512)}, bf16[8,72,2048]{2,1,0:T(8,128)(2,1)}, s32[]{:T(128)}, bf16[72,2048]{1,0:T(8,128)(2,1)}, bf16[2048,2048]{1,0:T(8,128)(2,1)}, /*index=5*/bf16[2048,2048]{1,0:T(8,128)(2,1)}) %tuple.55), branch_computations={%region_1.1_spmd, %region_2.3_spmd} | conditional | flops 1210466432 | bytes 19434644 | solution.py:79
  449.5 9.8 %fusion = bf16[72,2048]{1,0:T(8,128)(2,1)} fusion(bf16[2048,2048]{1,0:T(8,128)(2,1)} %get-tuple-element.195, bf16[2048,2048]{1,0:T(8,128)(2,1)} %get-tuple-element.194, f32[72]{0:T(128)S(1)} %add_rsqrt_fusion, bf16[72,2048]{1,0:T(8,128)(2,1)} %get-tuple-element.193, bf16[8,72,2048]{2,1,0:T(8,128)(2,1)} %get-tuple-element.191, s32[]{:T(128)} %get-tuple-element.192, ...), kind=kOutput, calls=%fused_computation.4 | convolution fusion | flops 1209876480 | bytes 18254112 | tf_op jit(solution)/shard_map/while/body/eval_jaxpr/cond/branch_1_fun/dot_general | solution.py:49
  465.7 1.9 copy.25
  467.5 5.0 reshape.116
  472.5 1.8 gather_fusion
  475.9 1.9 convolution_convert_fusion
  477.8 1.8 fusion.43
  480.0 2.1 collective-permute-start.11
  483.4 2.1 collective-permute-start.13
  485.5 2.1 collective-permute-start.14
  487.6 2.1 collective-permute-start.15
  489.7 2.1 collective-permute-start.16
  492.6 2.1 collective-permute-start.17
  495.9 6.0 collective-permute-done.14
  501.9 6.0 collective-permute-done.15
  507.8 1.7 fusion.36
  510.6 16.2 %all_to_all.10 = bf16[32,2,2048]{2,1,0:T(2,128)(2,1)} all-to-all(bf16[32,2,2048]{2,1,0:T(2,128)(2,1)S(1)} %reshape.121), channel_id=1, replica_groups=mesh['section'=8,'expert'=32] {'expert'}, dimensions={0} | all-to-all | bytes 524288 | tf_op jit(solution)/shard_map/all_to_all | solution.py:117
  526.9 24.7 %all-gather.5.cloned.1.call-done = bf16[256,2,2048]{2,1,0:T(2,128)(2,1)} async-done(((bf16[32,2,2048]{2,1,0:T(2,128)(2,1)}), bf16[256,2,2048]{2,1,0:T(2,128)(2,1)}) %all-gather.5.cloned.1.call-update) | async-done | bytes 2097168 | tf_op jit(solution)/shard_map/all_gather | solution.py:118
  551.6 2.7 reshape.122
  555.8 4.9 multiply_convert_fusion.2
  560.8 36.3 %reduce-scatter.2.cloned.1.call-done = bf16[512,256]{1,0:T(8,128)(2,1)} async-done(((bf16[512,2048]{1,0:T(8,128)(2,1)}), bf16[512,256]{1,0:T(8,128)(2,1)}) %reduce-scatter.2.cloned.1.call-update) | async-done | bytes 262160 | tf_op jit(solution)/shard_map/reduce_scatter | solution.py:129
  599.0 9.3 %all-to-all-start.1 = ((bf16[32,8,2,256]{3,2,1,0:T(2,128)(2,1)}), bf16[32,8,2,256]{3,2,1,0:T(2,128)(2,1)S(1)}, u32[]{:S(2)}, u32[]{:S(2)}) async-start(bf16[32,8,2,256]{3,2,1,0:T(2,128)(2,1)} %bitcast.108), calls=%async_computation.2 | async-start | bytes 524288 | tf_op jit(solution)/shard_map/all_to_all | solution.py:131
  608.5 12.6 %all-to-all-done.1 = bf16[32,8,2,256]{3,2,1,0:T(2,128)(2,1)S(1)} async-done(((bf16[32,8,2,256]{3,2,1,0:T(2,128)(2,1)}), bf16[32,8,2,256]{3,2,1,0:T(2,128)(2,1)S(1)}, u32[]{:S(2)}, u32[]{:S(2)}) %all-to-all-start.1) | async-done | bytes 262176 | tf_op jit(solution)/shard_map/all_to_all | solution.py:131
  621.3 2.1 scatter_custom_fusion
  (158 shorter events, 101.4 us)
Async XLA Ops:
  6.5 549.3 %copy-start = (bf16[1,256,2048]{2,1,0:T(8,128)(2,1)S(1)}, bf16[1,256,2048]{2,1,0:T(8,128)(2,1)}, u32[]{:S(2)}) copy-start(bf16[1,256,2048]{2,1,0:T(8,128)(2,1)} %param.17) | copy-start | bytes 3145732
  6.5 18.9 %copy-start.7 = (s32[144,1]{0,1:T(1,128)S(1)}, s32[144,1]{0,1:T(1,128)}, u32[]{:S(2)}) copy-start(s32[144,1]{0,1:T(1,128)} %param.19) | copy-start | bytes 1732
  6.5 54.6 %copy-start.8 = (s32[144]{0:T(256)S(1)}, s32[144]{0:T(256)}, u32[]{:S(2)}) copy-start(s32[144]{0:T(256)} %param.18) | copy-start | bytes 1732
  6.5 164.4 %all-gather.3.cloned.1.call-start = ((), (), s32[]{:S(2)}) async-start(), calls=%async_computation.3 | async-start | bytes 8650752 | tf_op jit(solution)/shard_map/all_gather | solution.py:59
  7.3 544.4 %all-gather.5.cloned.1.call-start = ((), (), s32[]{:S(2)}) async-start(), calls=%async_computation.4 | async-start | bytes 2359296 | tf_op jit(solution)/shard_map/all_gather | solution.py:118
  7.3 8.8 %collective-permute-start.1 = (bf16[64,2048]{1,0:T(8,128)(2,1)}, bf16[64,2048]{1,0:T(8,128)(2,1)S(1)}, u32[]{:S(2)}, u32[]{:S(2)}) collective-permute-start(bf16[64,2048]{1,0:T(8,128)(2,1)} %bitcast.116), channel_id=1, source_target_pairs={{0,1},{1,2},{2,3},{3,0},{4,5},{5,6},{6,7},{7,4},{8,9},{9,10},{10,1... | collective-permute-start | bytes 786440 | tf_op jit(solution)/shard_map/ppermute | solution.py:30
  8.7 7.5 %collective-permute-start.2 = (bf16[64,2048]{1,0:T(8,128)(2,1)}, bf16[64,2048]{1,0:T(8,128)(2,1)S(1)}, u32[]{:S(2)}, u32[]{:S(2)}) collective-permute-start(bf16[64,2048]{1,0:T(8,128)(2,1)} %bitcast.117), channel_id=1, source_target_pairs={{0,3},{1,0},{2,1},{3,2},{4,7},{5,4},{6,5},{7,6},{8,11},{9,8},{10,9... | collective-permute-start | bytes 786440 | tf_op jit(solution)/shard_map/ppermute | solution.py:33
  16.1 7.6 %collective-permute-start.3 = (bf16[64,2048]{1,0:T(8,128)(2,1)S(1)}, bf16[64,2048]{1,0:T(8,128)(2,1)S(1)}, u32[]{:S(2)}, u32[]{:S(2)}) collective-permute-start(bf16[64,2048]{1,0:T(8,128)(2,1)S(1)} %collective-permute-done.1), channel_id=1, source_target_pairs={{0,1},{1,2},{2,3},{3,0},{4,5},{5,6},{6,7},{7,4},{8,9},{9,10},{10,1... | collective-permute-start | bytes 786440 | tf_op jit(solution)/shard_map/ppermute | solution.py:30
  23.8 37.4 %collective-permute-start.4 = (bf16[4,64,2048]{2,1,0:T(8,128)(2,1)S(1)}, bf16[4,64,2048]{2,1,0:T(8,128)(2,1)}, u32[]{:S(2)}, u32[]{:S(2)}) collective-permute-start(bf16[4,64,2048]{2,1,0:T(8,128)(2,1)S(1)} %bitcast_dynamic-update-slice_fusion.8), channel_id=1, source_target_pairs={{0,4},{1,5},{2,6},{3,7},{4,8},{5,9},{6,10},{7,11},{8,12},{9,13},{1... | collective-permute-start | bytes 3145736 | tf_op jit(solution)/shard_map/ppermute | solution.py:30
  25.5 35.7 %collective-permute-start.5 = (bf16[4,64,2048]{2,1,0:T(8,128)(2,1)S(1)}, bf16[4,64,2048]{2,1,0:T(8,128)(2,1)S(1)}, u32[]{:S(2)}, u32[]{:S(2)}) collective-permute-start(bf16[4,64,2048]{2,1,0:T(8,128)(2,1)S(1)} %bitcast_dynamic-update-slice_fusion.8), channel_id=1, source_target_pairs={{0,28},{1,29},{2,30},{3,31},{4,0},{5,1},{6,2},{7,3},{8,4},{9,5},{1... | collective-permute-start | bytes 3145736 | tf_op jit(solution)/shard_map/ppermute | solution.py:33
  61.2 39.9 %collective-permute-start.6 = (bf16[4,64,2048]{2,1,0:T(8,128)(2,1)}, bf16[4,64,2048]{2,1,0:T(8,128)(2,1)S(1)}, u32[]{:S(2)}, u32[]{:S(2)}) collective-permute-start(bf16[4,64,2048]{2,1,0:T(8,128)(2,1)} %collective-permute-done.4), channel_id=1, source_target_pairs={{0,4},{1,5},{2,6},{3,7},{4,8},{5,9},{6,10},{7,11},{8,12},{9,13},{1... | collective-permute-start | bytes 3145736 | tf_op jit(solution)/shard_map/ppermute | solution.py:30
  61.2 43.2 %collective-permute-start.7 = (bf16[4,64,2048]{2,1,0:T(8,128)(2,1)S(1)}, bf16[4,64,2048]{2,1,0:T(8,128)(2,1)S(1)}, u32[]{:S(2)}, u32[]{:S(2)}) collective-permute-start(bf16[4,64,2048]{2,1,0:T(8,128)(2,1)S(1)} %collective-permute-done.5), channel_id=1, source_target_pairs={{0,28},{1,29},{2,30},{3,31},{4,0},{5,1},{6,2},{7,3},{8,4},{9,5},{1... | collective-permute-start | bytes 3145736 | tf_op jit(solution)/shard_map/ppermute | solution.py:33
  101.0 45.9 %collective-permute-start.8 = (bf16[4,64,2048]{2,1,0:T(8,128)(2,1)S(1)}, bf16[4,64,2048]{2,1,0:T(8,128)(2,1)S(1)}, u32[]{:S(2)}, u32[]{:S(2)}) collective-permute-start(bf16[4,64,2048]{2,1,0:T(8,128)(2,1)S(1)} %collective-permute-done.6), channel_id=1, source_target_pairs={{0,4},{1,5},{2,6},{3,7},{4,8},{5,9},{6,10},{7,11},{8,12},{9,13},{1... | collective-permute-start | bytes 3145736 | tf_op jit(solution)/shard_map/ppermute | solution.py:30
  104.5 44.6 %collective-permute-start.9 = (bf16[4,64,2048]{2,1,0:T(8,128)(2,1)S(1)}, bf16[4,64,2048]{2,1,0:T(8,128)(2,1)S(1)}, u32[]{:S(2)}, u32[]{:S(2)}) collective-permute-start(bf16[4,64,2048]{2,1,0:T(8,128)(2,1)S(1)} %collective-permute-done.7), channel_id=1, source_target_pairs={{0,28},{1,29},{2,30},{3,31},{4,0},{5,1},{6,2},{7,3},{8,4},{9,5},{1... | collective-permute-start | bytes 3145736 | tf_op jit(solution)/shard_map/ppermute | solution.py:33
  146.9 22.9 %collective-permute-start.10 = (bf16[4,64,2048]{2,1,0:T(8,128)(2,1)S(1)}, bf16[4,64,2048]{2,1,0:T(8,128)(2,1)S(1)}, u32[]{:S(2)}, u32[]{:S(2)}) collective-permute-start(bf16[4,64,2048]{2,1,0:T(8,128)(2,1)S(1)} %collective-permute-done.8), channel_id=1, source_target_pairs={{0,4},{1,5},{2,6},{3,7},{4,8},{5,9},{6,10},{7,11},{8,12},{9,13},{1... | collective-permute-start | bytes 3145736 | tf_op jit(solution)/shard_map/ppermute | solution.py:30
  173.5 7.2 %collective-permute-start = (bf16[72,2048]{1,0:T(8,128)(2,1)}, bf16[72,2048]{1,0:T(8,128)(2,1)}, u32[]{:S(2)}, u32[]{:S(2)}) collective-permute-start(bf16[72,2048]{1,0:T(8,128)(2,1)} %get-tuple-element.296), channel_id=1, source_target_pairs={{0,32},{32,64},{64,96},{96,128},{128,160},{160,192},{192,224},{1,3... | collective-permute-start | bytes 884744 | tf_op jit(solution)/shard_map/while/body/eval_jaxpr/ppermute | solution.py:10
  182.1 8.3 %collective-permute-start = (bf16[72,2048]{1,0:T(8,128)(2,1)}, bf16[72,2048]{1,0:T(8,128)(2,1)}, u32[]{:S(2)}, u32[]{:S(2)}) collective-permute-start(bf16[72,2048]{1,0:T(8,128)(2,1)} %get-tuple-element.296), channel_id=1, source_target_pairs={{0,32},{32,64},{64,96},{96,128},{128,160},{160,192},{192,224},{1,3... | collective-permute-start | bytes 884744 | tf_op jit(solution)/shard_map/while/body/eval_jaxpr/ppermute | solution.py:10
  191.9 8.3 %collective-permute-start = (bf16[72,2048]{1,0:T(8,128)(2,1)}, bf16[72,2048]{1,0:T(8,128)(2,1)}, u32[]{:S(2)}, u32[]{:S(2)}) collective-permute-start(bf16[72,2048]{1,0:T(8,128)(2,1)} %get-tuple-element.296), channel_id=1, source_target_pairs={{0,32},{32,64},{64,96},{96,128},{128,160},{160,192},{192,224},{1,3... | collective-permute-start | bytes 884744 | tf_op jit(solution)/shard_map/while/body/eval_jaxpr/ppermute | solution.py:10
  201.8 8.3 %collective-permute-start = (bf16[72,2048]{1,0:T(8,128)(2,1)}, bf16[72,2048]{1,0:T(8,128)(2,1)}, u32[]{:S(2)}, u32[]{:S(2)}) collective-permute-start(bf16[72,2048]{1,0:T(8,128)(2,1)} %get-tuple-element.296), channel_id=1, source_target_pairs={{0,32},{32,64},{64,96},{96,128},{128,160},{160,192},{192,224},{1,3... | collective-permute-start | bytes 884744 | tf_op jit(solution)/shard_map/while/body/eval_jaxpr/ppermute | solution.py:10
  211.6 8.3 %collective-permute-start = (bf16[72,2048]{1,0:T(8,128)(2,1)}, bf16[72,2048]{1,0:T(8,128)(2,1)}, u32[]{:S(2)}, u32[]{:S(2)}) collective-permute-start(bf16[72,2048]{1,0:T(8,128)(2,1)} %get-tuple-element.296), channel_id=1, source_target_pairs={{0,32},{32,64},{64,96},{96,128},{128,160},{160,192},{192,224},{1,3... | collective-permute-start | bytes 884744 | tf_op jit(solution)/shard_map/while/body/eval_jaxpr/ppermute | solution.py:10
  221.4 8.3 %collective-permute-start = (bf16[72,2048]{1,0:T(8,128)(2,1)}, bf16[72,2048]{1,0:T(8,128)(2,1)}, u32[]{:S(2)}, u32[]{:S(2)}) collective-permute-start(bf16[72,2048]{1,0:T(8,128)(2,1)} %get-tuple-element.296), channel_id=1, source_target_pairs={{0,32},{32,64},{64,96},{96,128},{128,160},{160,192},{192,224},{1,3... | collective-permute-start | bytes 884744 | tf_op jit(solution)/shard_map/while/body/eval_jaxpr/ppermute | solution.py:10
  231.2 69.0 %collective-permute-start = (bf16[72,2048]{1,0:T(8,128)(2,1)}, bf16[72,2048]{1,0:T(8,128)(2,1)}, u32[]{:S(2)}, u32[]{:S(2)}) collective-permute-start(bf16[72,2048]{1,0:T(8,128)(2,1)} %get-tuple-element.296), channel_id=1, source_target_pairs={{0,32},{32,64},{64,96},{96,128},{128,160},{160,192},{192,224},{1,3... | collective-permute-start | bytes 884744 | tf_op jit(solution)/shard_map/while/body/eval_jaxpr/ppermute | solution.py:10
  313.0 8.3 %collective-permute-start = (bf16[72,2048]{1,0:T(8,128)(2,1)}, bf16[72,2048]{1,0:T(8,128)(2,1)}, u32[]{:S(2)}, u32[]{:S(2)}) collective-permute-start(bf16[72,2048]{1,0:T(8,128)(2,1)} %get-tuple-element.296), channel_id=1, source_target_pairs={{0,32},{32,64},{64,96},{96,128},{128,160},{160,192},{192,224},{1,3... | collective-permute-start | bytes 884744 | tf_op jit(solution)/shard_map/while/body/eval_jaxpr/ppermute | solution.py:10
  334.2 8.3 %collective-permute-start = (bf16[72,2048]{1,0:T(8,128)(2,1)}, bf16[72,2048]{1,0:T(8,128)(2,1)}, u32[]{:S(2)}, u32[]{:S(2)}) collective-permute-start(bf16[72,2048]{1,0:T(8,128)(2,1)} %get-tuple-element.296), channel_id=1, source_target_pairs={{0,32},{32,64},{64,96},{96,128},{128,160},{160,192},{192,224},{1,3... | collective-permute-start | bytes 884744 | tf_op jit(solution)/shard_map/while/body/eval_jaxpr/ppermute | solution.py:10
  355.3 8.3 %collective-permute-start = (bf16[72,2048]{1,0:T(8,128)(2,1)}, bf16[72,2048]{1,0:T(8,128)(2,1)}, u32[]{:S(2)}, u32[]{:S(2)}) collective-permute-start(bf16[72,2048]{1,0:T(8,128)(2,1)} %get-tuple-element.296), channel_id=1, source_target_pairs={{0,32},{32,64},{64,96},{96,128},{128,160},{160,192},{192,224},{1,3... | collective-permute-start | bytes 884744 | tf_op jit(solution)/shard_map/while/body/eval_jaxpr/ppermute | solution.py:10
  376.5 8.3 %collective-permute-start = (bf16[72,2048]{1,0:T(8,128)(2,1)}, bf16[72,2048]{1,0:T(8,128)(2,1)}, u32[]{:S(2)}, u32[]{:S(2)}) collective-permute-start(bf16[72,2048]{1,0:T(8,128)(2,1)} %get-tuple-element.296), channel_id=1, source_target_pairs={{0,32},{32,64},{64,96},{96,128},{128,160},{160,192},{192,224},{1,3... | collective-permute-start | bytes 884744 | tf_op jit(solution)/shard_map/while/body/eval_jaxpr/ppermute | solution.py:10
  397.6 8.3 %collective-permute-start = (bf16[72,2048]{1,0:T(8,128)(2,1)}, bf16[72,2048]{1,0:T(8,128)(2,1)}, u32[]{:S(2)}, u32[]{:S(2)}) collective-permute-start(bf16[72,2048]{1,0:T(8,128)(2,1)} %get-tuple-element.296), channel_id=1, source_target_pairs={{0,32},{32,64},{64,96},{96,128},{128,160},{160,192},{192,224},{1,3... | collective-permute-start | bytes 884744 | tf_op jit(solution)/shard_map/while/body/eval_jaxpr/ppermute | solution.py:10
  418.8 8.3 %collective-permute-start = (bf16[72,2048]{1,0:T(8,128)(2,1)}, bf16[72,2048]{1,0:T(8,128)(2,1)}, u32[]{:S(2)}, u32[]{:S(2)}) collective-permute-start(bf16[72,2048]{1,0:T(8,128)(2,1)} %get-tuple-element.296), channel_id=1, source_target_pairs={{0,32},{32,64},{64,96},{96,128},{128,160},{160,192},{192,224},{1,3... | collective-permute-start | bytes 884744 | tf_op jit(solution)/shard_map/while/body/eval_jaxpr/ppermute | solution.py:10
  439.9 8.3 %collective-permute-start = (bf16[72,2048]{1,0:T(8,128)(2,1)}, bf16[72,2048]{1,0:T(8,128)(2,1)}, u32[]{:S(2)}, u32[]{:S(2)}) collective-permute-start(bf16[72,2048]{1,0:T(8,128)(2,1)} %get-tuple-element.296), channel_id=1, source_target_pairs={{0,32},{32,64},{64,96},{96,128},{128,160},{160,192},{192,224},{1,3... | collective-permute-start | bytes 884744 | tf_op jit(solution)/shard_map/while/body/eval_jaxpr/ppermute | solution.py:10
  461.1 3.8 collective-permute-start
  474.3 3.4 copy-start.1
  477.8 2.2 copy-start.2
  480.0 9.7 %collective-permute-start.11 = (bf16[136,2048]{1,0:T(8,128)(2,1)S(1)}, bf16[136,2048]{1,0:T(8,128)(2,1)S(1)}, u32[]{:S(2)}, u32[]{:S(2)}) collective-permute-start(bf16[136,2048]{1,0:T(8,128)(2,1)S(1)} %get-tuple-element.231), channel_id=1, source_target_pairs={{224,192},{225,193},{226,194},{227,195},{228,196},{229,197},{230,1... | collective-permute-start | bytes 1671176 | tf_op jit(solution)/shard_map/ppermute | solution.py:112
  482.1 9.8 %collective-permute-start.12 = (bf16[136,2048]{1,0:T(8,128)(2,1)S(1)}, bf16[136,2048]{1,0:T(8,128)(2,1)S(1)}, u32[]{:S(2)}, u32[]{:S(2)}) collective-permute-start(bf16[136,2048]{1,0:T(8,128)(2,1)S(1)} %get-tuple-element.232), channel_id=1, source_target_pairs={{224,160},{225,161},{226,162},{227,163},{228,164},{229,165},{230,1... | collective-permute-start | bytes 1671176 | tf_op jit(solution)/shard_map/ppermute | solution.py:112
  483.4 12.5 %collective-permute-start.13 = (bf16[136,2048]{1,0:T(8,128)(2,1)}, bf16[136,2048]{1,0:T(8,128)(2,1)}, u32[]{:S(2)}, u32[]{:S(2)}) collective-permute-start(bf16[136,2048]{1,0:T(8,128)(2,1)} %get-tuple-element.233), channel_id=1, source_target_pairs={{224,128},{225,129},{226,130},{227,131},{228,132},{229,133},{230,1... | collective-permute-start | bytes 1671176 | tf_op jit(solution)/shard_map/ppermute | solution.py:112
  485.5 16.3 %collective-permute-start.14 = (bf16[136,2048]{1,0:T(8,128)(2,1)}, bf16[136,2048]{1,0:T(8,128)(2,1)}, u32[]{:S(2)}, u32[]{:S(2)}) collective-permute-start(bf16[136,2048]{1,0:T(8,128)(2,1)} %get-tuple-element.234), channel_id=1, source_target_pairs={{224,96},{225,97},{226,98},{227,99},{228,100},{229,101},{230,102},... | collective-permute-start | bytes 1671176 | tf_op jit(solution)/shard_map/ppermute | solution.py:112
  487.6 20.2 %collective-permute-start.15 = (bf16[136,2048]{1,0:T(8,128)(2,1)}, bf16[136,2048]{1,0:T(8,128)(2,1)}, u32[]{:S(2)}, u32[]{:S(2)}) collective-permute-start(bf16[136,2048]{1,0:T(8,128)(2,1)} %get-tuple-element.235), channel_id=1, source_target_pairs={{224,64},{225,65},{226,66},{227,67},{228,68},{229,69},{230,70},{23... | collective-permute-start | bytes 1671176 | tf_op jit(solution)/shard_map/ppermute | solution.py:112
  489.7 2.1 copy-start.5
  489.7 18.1 %collective-permute-start.16 = (bf16[136,2048]{1,0:T(8,128)(2,1)}, bf16[136,2048]{1,0:T(8,128)(2,1)}, u32[]{:S(2)}, u32[]{:S(2)}) collective-permute-start(bf16[136,2048]{1,0:T(8,128)(2,1)} %get-tuple-element.236), channel_id=1, source_target_pairs={{224,32},{225,33},{226,34},{227,35},{228,36},{229,37},{230,38},{23... | collective-permute-start | bytes 1671176 | tf_op jit(solution)/shard_map/ppermute | solution.py:112
  491.8 0.8 copy-start.6
  492.6 15.2 %collective-permute-start.17 = (bf16[136,2048]{1,0:T(8,128)(2,1)}, bf16[136,2048]{1,0:T(8,128)(2,1)}, u32[]{:S(2)}, u32[]{:S(2)}) collective-permute-start(bf16[136,2048]{1,0:T(8,128)(2,1)} %get-tuple-element.230), channel_id=1, source_target_pairs={{224,0},{225,1},{226,2},{227,3},{228,4},{229,5},{230,6},{231,7},{2... | collective-permute-start | bytes 1671176 | tf_op jit(solution)/shard_map/ppermute | solution.py:112
  509.6 0.8 copy-start.3
  526.9 70.2 %reduce-scatter.2.cloned.1.call-start = ((), (), s32[]{:S(2)}) async-start(), calls=%async_computation.5 | async-start | bytes 2359296 | tf_op jit(solution)/shard_map/reduce_scatter | solution.py:129
  560.7 47.7 %copy-start.4 = (bf16[136,2048]{1,0:T(8,128)(2,1)S(1)}, bf16[136,2048]{1,0:T(8,128)(2,1)}, u32[]{:S(2)}) copy-start(bf16[136,2048]{1,0:T(8,128)(2,1)} %copy-done.3) | copy-start | bytes 1671172
  599.0 22.1 %all-to-all-start.1 = ((bf16[32,8,2,256]{3,2,1,0:T(2,128)(2,1)}), bf16[32,8,2,256]{3,2,1,0:T(2,128)(2,1)S(1)}, u32[]{:S(2)}, u32[]{:S(2)}) async-start(bf16[32,8,2,256]{3,2,1,0:T(2,128)(2,1)} %bitcast.108), calls=%async_computation.2 | async-start | bytes 524288 | tf_op jit(solution)/shard_map/all_to_all | solution.py:131
Sparse Core Ops, SparseCore 0:
  9.9 136.1 all-gather.2
  527.0 24.6 all-gather.4
  560.9 36.1 reduce-scatter.1

commit v3 on v2

--- a/solution.py
+++ b/solution.py
@@ -69,21 +69,25 @@
     def skip_layer(stream):
         return jnp.zeros_like(stream)
 
+    groups = micro // 2 if micro % 2 == 0 else micro
+    chunks = tokens.reshape(groups, micro * tok_dev // groups, width)
+
     def tick(step, carry):
         incoming, collected = carry
         micro_index = step - section
-        valid = (micro_index >= 0) & (micro_index < micro)
-        clamped = jnp.clip(micro_index, 0, micro - 1)
-        fresh = lax.dynamic_index_in_dim(tokens, clamped, 0, keepdims=False)
+        valid = (micro_index >= 0) & (micro_index < groups)
+        clamped = jnp.clip(micro_index, 0, groups - 1)
+        fresh = lax.dynamic_index_in_dim(chunks, clamped, 0, keepdims=False)
         stream = jnp.where(section == 0, fresh, incoming)
         result = lax.cond(valid, run_layer, skip_layer, stream)
-        updated = lax.dynamic_update_index_in_dim(collected, result, clamped, 0)
-        collected = jnp.where(valid & (section == last), updated, collected)
+        held = lax.dynamic_index_in_dim(collected, clamped, 0, keepdims=False)
+        kept = jnp.where(valid & (section == last), result, held)
+        collected = lax.dynamic_update_index_in_dim(collected, kept, clamped, 0)
         passed = from_behind(result, "section", 1)
         return (passed, collected)
 
-    start = (jnp.zeros((tok_dev, width), jnp.bfloat16), jnp.zeros_like(tokens))
-    passed, collected = lax.fori_loop(0, micro + n_section - 1, tick, start)
+    start = (jnp.zeros(chunks.shape[1:], jnp.bfloat16), jnp.zeros_like(chunks))
+    passed, collected = lax.fori_loop(0, groups + n_section - 1, tick, start)
     rows_dev = micro * tok_dev
     flat = collected.reshape(rows_dev, width)
     n_exp = router.shape[1]

time: 632 us -> 559 us (0.88)
  matrix products: 87 us -> 48.1 us
  waiting for transfers between devices: 372 us -> 344 us
  local copies, waits for them, and re-layouts: 56.9 us -> 49.3 us
    dot_general x8 -> x4, matrix products: 78.8 us -> 39.9 us  [processor(): branch = jnp.dot(hidden, w_second, preferred_element_type=jnp.float32)]
    ppermute x15 -> x11, waiting for transfers between devices: 151 us -> 125 us  [from_behind(): lax.ppermute(value, axis, [(source, source + steps) for source in range(i...]
    dynamic_update_slice x0 -> x11, other arithmetic: none -> 14.1 us  [tick(): collected = lax.dynamic_update_index_in_dim(collected, kept, clamped, 0)]
    cond x8 -> x0, local copies, waits for them, and re-layouts: 13.5 us -> none
    dynamic_slice x0 -> x11, local copies, waits for them, and re-layouts: none -> 9.7 us  [tick(): held = lax.dynamic_index_in_dim(collected, clamped, 0, keepdims=False)]
    select_n x15 -> x0, other arithmetic: 9.16 us -> none  [tick(): collected = jnp.where(valid & (section == last), updated, collected)]
    ppermute x15 -> x11, starting transfers between devices: 19.2 us -> 14.1 us  [from_behind(): lax.ppermute(value, axis, [(source, source + steps) for source in range(i...]
  transfers between devices with their start and end apart: 36 -> 32, of which waited for: 27 -> 23; matrix products, arithmetic and copies ran while one was open for 4% -> 7% of each run, Pallas kernels for 0% -> 0%
where the time goes in v3:
time: 559 us; the launch traced here: 557 us
  waiting for transfers between devices  344 us (62%)
  starting transfers between devices  56.6 us (10%)
  local copies, waits for them, and re-layouts  49.3 us (9%)
  matrix products  48.1 us (9%)
  other arithmetic  29 us (5%)
  blocking collectives  16.2 us (3%)
  between operations  13.4 us (2%)
    ppermute x6, waiting for transfers between devices, ring_gather(): ahead = lax.ppermute(ahead, axis, shifted(1))  133 us
    ppermute x11, waiting for transfers between devices, from_behind(): lax.ppermute(value, axis, [(source, source + steps) for source in range(i...  125 us
    dot_general x4, matrix products, processor(): branch = jnp.dot(hidden, w_second, preferred_element_type=jnp.float32)  39.9 us
    reduce_scatter x1, waiting for transfers between devices, local(): lax.psum_scatter(scaled, 'section', scatter_dimension=1, tiled=True)  36.3 us
    all_gather x1, waiting for transfers between devices, local(): lax.all_gather(arrived, 'section', axis=0, tiled=True).reshape(-1, width)  24.5 us
    ppermute x7, starting transfers between devices, local(): got = lax.ppermute(payload[target], 'section', [(last, target)])  18.2 us
    all_to_all x1, blocking collectives, local(): lax.all_to_all(outgoing, 'expert', split_axis=0, concat_axis=0, tiled=True)  16.2 us
    dynamic_update_slice x11, other arithmetic, tick(): collected = lax.dynamic_update_index_in_dim(collected, kept, clamped, 0)  14.1 us
  transfers between devices with their start and end apart: 32, of which 23 were waited for; matrix products, arithmetic and copies ran while one was open for 7% of the time, Pallas kernels for 0%

profile of v3, /device:TPU:7, one launch (start us, length us, event | category | flops | bytes accessed | tf_op | source)
XLA Modules:
  0.0 557.3 jit_solution(10811726133254303670)
XLA Ops:
  8.7 1.5 collective-permute-start.2
  11.3 4.8 collective-permute-done.1
  16.2 7.5 %collective-permute-done.3 = bf16[64,2048]{1,0:T(8,128)(2,1)S(1)} collective-permute-done((bf16[64,2048]{1,0:T(8,128)(2,1)S(1)}, bf16[64,2048]{1,0:T(8,128)(2,1)S(1)}, u32[]{:S(2)}, u32[]{:S(2)}) %collective-permute-start.3) | collective-permute-done | bytes 262176 | tf_op jit(solution)/shard_map/ppermute | solution.py:30
  23.8 1.7 collective-permute-start.4
  25.5 4.0 collective-permute-start.5
  30.5 30.7 %collective-permute-done.4 = bf16[4,64,2048]{2,1,0:T(8,128)(2,1)} collective-permute-done((bf16[4,64,2048]{2,1,0:T(8,128)(2,1)S(1)}, bf16[4,64,2048]{2,1,0:T(8,128)(2,1)}, u32[]{:S(2)}, u32[]{:S(2)}) %collective-permute-start.4) | collective-permute-done | bytes 1048608 | tf_op jit(solution)/shard_map/ppermute | solution.py:30
  61.2 2.7 collective-permute-start.7
  64.0 4.4 broadcast_in_dim.84
  69.5 31.6 %collective-permute-done.6 = bf16[4,64,2048]{2,1,0:T(8,128)(2,1)S(1)} collective-permute-done((bf16[4,64,2048]{2,1,0:T(8,128)(2,1)}, bf16[4,64,2048]{2,1,0:T(8,128)(2,1)S(1)}, u32[]{:S(2)}, u32[]{:S(2)}) %collective-permute-start.6) | collective-permute-done | bytes 1048608 | tf_op jit(solution)/shard_map/ppermute | solution.py:30
  101.1 2.4 bitcast_dynamic-update-slice_fusion.7
  104.5 3.3 collective-permute-start.9
  108.8 38.1 %collective-permute-done.8 = bf16[4,64,2048]{2,1,0:T(8,128)(2,1)S(1)} collective-permute-done((bf16[4,64,2048]{2,1,0:T(8,128)(2,1)S(1)}, bf16[4,64,2048]{2,1,0:T(8,128)(2,1)S(1)}, u32[]{:S(2)}, u32[]{:S(2)}) %collective-permute-start.8) | collective-permute-done | bytes 1048608 | tf_op jit(solution)/shard_map/ppermute | solution.py:30
  150.1 19.8 %collective-permute-done.10 = bf16[4,64,2048]{2,1,0:T(8,128)(2,1)S(1)} collective-permute-done((bf16[4,64,2048]{2,1,0:T(8,128)(2,1)S(1)}, bf16[4,64,2048]{2,1,0:T(8,128)(2,1)S(1)}, u32[]{:S(2)}, u32[]{:S(2)}) %collective-permute-start.10) | collective-permute-done | bytes 1048608 | tf_op jit(solution)/shard_map/ppermute | solution.py:30
  172.1 215.1 %while.16 = (s32[]{:T(128)}, bf16[144,2048]{1,0:T(8,128)(2,1)}, bf16[4,144,2048]{2,1,0:T(8,128)(2,1)S(1)}, s32[]{:T(128)}, pred[]{:T(512)}, /*index=5*/bf16[4,14...) while((s32[]{:T(128)}, bf16[144,2048]{1,0:T(8,128)(2,1)}, ...), condition=%wide.region_4.5_spmd, body=%wide.region_0.4_spmd.sunk | while | flops 2421227776 | bytes 26219048 | solution.py:90
  176.5 4.2 collective-permute-done
  185.0 8.1 %collective-permute-done = bf16[144,2048]{1,0:T(8,128)(2,1)} collective-permute-done((bf16[144,2048]{1,0:T(8,128)(2,1)}, bf16[144,2048]{1,0:T(8,128)(2,1)}, u32[]{:S(2)}, u32[]{:S(2)}) %collective-permute-start) | collective-permute-done | bytes 589856 | tf_op jit(solution)/shard_map/while/body/eval_jaxpr/ppermute | solution.py:10
  197.4 8.1 %collective-permute-done = bf16[144,2048]{1,0:T(8,128)(2,1)} collective-permute-done((bf16[144,2048]{1,0:T(8,128)(2,1)}, bf16[144,2048]{1,0:T(8,128)(2,1)}, u32[]{:S(2)}, u32[]{:S(2)}) %collective-permute-start) | collective-permute-done | bytes 589856 | tf_op jit(solution)/shard_map/while/body/eval_jaxpr/ppermute | solution.py:10
  209.8 8.1 %collective-permute-done = bf16[144,2048]{1,0:T(8,128)(2,1)} collective-permute-done((bf16[144,2048]{1,0:T(8,128)(2,1)}, bf16[144,2048]{1,0:T(8,128)(2,1)}, u32[]{:S(2)}, u32[]{:S(2)}) %collective-permute-start) | collective-permute-done | bytes 589856 | tf_op jit(solution)/shard_map/while/body/eval_jaxpr/ppermute | solution.py:10
  222.2 8.1 %collective-permute-done = bf16[144,2048]{1,0:T(8,128)(2,1)} collective-permute-done((bf16[144,2048]{1,0:T(8,128)(2,1)}, bf16[144,2048]{1,0:T(8,128)(2,1)}, u32[]{:S(2)}, u32[]{:S(2)}) %collective-permute-start) | collective-permute-done | bytes 589856 | tf_op jit(solution)/shard_map/while/body/eval_jaxpr/ppermute | solution.py:10
  234.6 8.1 %collective-permute-done = bf16[144,2048]{1,0:T(8,128)(2,1)} collective-permute-done((bf16[144,2048]{1,0:T(8,128)(2,1)}, bf16[144,2048]{1,0:T(8,128)(2,1)}, u32[]{:S(2)}, u32[]{:S(2)}) %collective-permute-start) | collective-permute-done | bytes 589856 | tf_op jit(solution)/shard_map/while/body/eval_jaxpr/ppermute | solution.py:10
  247.0 55.5 %collective-permute-done = bf16[144,2048]{1,0:T(8,128)(2,1)} collective-permute-done((bf16[144,2048]{1,0:T(8,128)(2,1)}, bf16[144,2048]{1,0:T(8,128)(2,1)}, u32[]{:S(2)}, u32[]{:S(2)}) %collective-permute-start) | collective-permute-done | bytes 589856 | tf_op jit(solution)/shard_map/while/body/eval_jaxpr/ppermute | solution.py:10
  302.5 11.5 %conditional.2 = (bf16[144,2048]{1,0:T(8,128)(2,1)}) conditional(s32[]{:T(128)} %convert_element_type.108, () %tuple.50, (pred[]{:T(512)}, bf16[4,144,2048]{2,1,0:T(8,128)(2,1)}, s32[]{:T(128)}, bf16[144,2048]{1,0:T(8,128)(2,1)}, bf16[2048,2048]{1,0:T(8,128)(2,1)}, /*index=5*/bf16[2048,2048]{1,0:T(8,128)(2,1)}) %tuple.51), branch_computations={%region_1.1_spmd, %region_2.3_spmd} | conditional | flops 2420932864 | bytes 20910348 | solution.py:82
  302.5 1.5 fusion.1
  304.0 10.0 %fusion = bf16[144,2048]{1,0:T(8,128)(2,1)} fusion(bf16[2048,2048]{1,0:T(8,128)(2,1)} %get-tuple-element.196, bf16[2048,2048]{1,0:T(8,128)(2,1)} %get-tuple-element.195, f32[144]{0:T(256)S(1)} %add_rsqrt_fusion, bf16[144,2048]{1,0:T(8,128)(2,1)} %get-tuple-element.194, bf16[4,144,2048]{2,1,0:T(8,128)(2,1)} %get-tuple-element.192, s32[]{:T(128)} %get-tuple-element.193, ...), kind=kOutput, calls=%fused_computation.4 | convolution fusion | flops 2419752960 | bytes 19728960 | tf_op jit(solution)/shard_map/while/body/eval_jaxpr/cond/branch_1_fun/dot_general | solution.py:49
  316.2 1.4 bitcast_dynamic-update-slice_fusion.13
  317.6 7.9 %collective-permute-done = bf16[144,2048]{1,0:T(8,128)(2,1)} collective-permute-done((bf16[144,2048]{1,0:T(8,128)(2,1)}, bf16[144,2048]{1,0:T(8,128)(2,1)}, u32[]{:S(2)}, u32[]{:S(2)}) %collective-permute-start) | collective-permute-done | bytes 589856 | tf_op jit(solution)/shard_map/while/body/eval_jaxpr/ppermute | solution.py:10
  325.5 11.5 %conditional.2 = (bf16[144,2048]{1,0:T(8,128)(2,1)}) conditional(s32[]{:T(128)} %convert_element_type.108, () %tuple.50, (pred[]{:T(512)}, bf16[4,144,2048]{2,1,0:T(8,128)(2,1)}, s32[]{:T(128)}, bf16[144,2048]{1,0:T(8,128)(2,1)}, bf16[2048,2048]{1,0:T(8,128)(2,1)}, /*index=5*/bf16[2048,2048]{1,0:T(8,128)(2,1)}) %tuple.51), branch_computations={%region_1.1_spmd, %region_2.3_spmd} | conditional | flops 2420932864 | bytes 20910348 | solution.py:82
  325.5 1.5 fusion.1
  327.0 10.0 %fusion = bf16[144,2048]{1,0:T(8,128)(2,1)} fusion(bf16[2048,2048]{1,0:T(8,128)(2,1)} %get-tuple-element.196, bf16[2048,2048]{1,0:T(8,128)(2,1)} %get-tuple-element.195, f32[144]{0:T(256)S(1)} %add_rsqrt_fusion, bf16[144,2048]{1,0:T(8,128)(2,1)} %get-tuple-element.194, bf16[4,144,2048]{2,1,0:T(8,128)(2,1)} %get-tuple-element.192, s32[]{:T(128)} %get-tuple-element.193, ...), kind=kOutput, calls=%fused_computation.4 | convolution fusion | flops 2419752960 | bytes 19728960 | tf_op jit(solution)/shard_map/while/body/eval_jaxpr/cond/branch_1_fun/dot_general | solution.py:49
  339.1 1.4 bitcast_dynamic-update-slice_fusion.13
  340.6 7.9 %collective-permute-done = bf16[144,2048]{1,0:T(8,128)(2,1)} collective-permute-done((bf16[144,2048]{1,0:T(8,128)(2,1)}, bf16[144,2048]{1,0:T(8,128)(2,1)}, u32[]{:S(2)}, u32[]{:S(2)}) %collective-permute-start) | collective-permute-done | bytes 589856 | tf_op jit(solution)/shard_map/while/body/eval_jaxpr/ppermute | solution.py:10
  348.5 11.5 %conditional.2 = (bf16[144,2048]{1,0:T(8,128)(2,1)}) conditional(s32[]{:T(128)} %convert_element_type.108, () %tuple.50, (pred[]{:T(512)}, bf16[4,144,2048]{2,1,0:T(8,128)(2,1)}, s32[]{:T(128)}, bf16[144,2048]{1,0:T(8,128)(2,1)}, bf16[2048,2048]{1,0:T(8,128)(2,1)}, /*index=5*/bf16[2048,2048]{1,0:T(8,128)(2,1)}) %tuple.51), branch_computations={%region_1.1_spmd, %region_2.3_spmd} | conditional | flops 2420932864 | bytes 20910348 | solution.py:82
  348.5 1.5 fusion.1
  350.0 10.0 %fusion = bf16[144,2048]{1,0:T(8,128)(2,1)} fusion(bf16[2048,2048]{1,0:T(8,128)(2,1)} %get-tuple-element.196, bf16[2048,2048]{1,0:T(8,128)(2,1)} %get-tuple-element.195, f32[144]{0:T(256)S(1)} %add_rsqrt_fusion, bf16[144,2048]{1,0:T(8,128)(2,1)} %get-tuple-element.194, bf16[4,144,2048]{2,1,0:T(8,128)(2,1)} %get-tuple-element.192, s32[]{:T(128)} %get-tuple-element.193, ...), kind=kOutput, calls=%fused_computation.4 | convolution fusion | flops 2419752960 | bytes 19728960 | tf_op jit(solution)/shard_map/while/body/eval_jaxpr/cond/branch_1_fun/dot_general | solution.py:49
  362.1 1.4 bitcast_dynamic-update-slice_fusion.13
  363.5 8.0 %collective-permute-done = bf16[144,2048]{1,0:T(8,128)(2,1)} collective-permute-done((bf16[144,2048]{1,0:T(8,128)(2,1)}, bf16[144,2048]{1,0:T(8,128)(2,1)}, u32[]{:S(2)}, u32[]{:S(2)}) %collective-permute-start) | collective-permute-done | bytes 589856 | tf_op jit(solution)/shard_map/while/body/eval_jaxpr/ppermute | solution.py:10
  371.5 11.5 %conditional.2 = (bf16[144,2048]{1,0:T(8,128)(2,1)}) conditional(s32[]{:T(128)} %convert_element_type.108, () %tuple.50, (pred[]{:T(512)}, bf16[4,144,2048]{2,1,0:T(8,128)(2,1)}, s32[]{:T(128)}, bf16[144,2048]{1,0:T(8,128)(2,1)}, bf16[2048,2048]{1,0:T(8,128)(2,1)}, /*index=5*/bf16[2048,2048]{1,0:T(8,128)(2,1)}) %tuple.51), branch_computations={%region_1.1_spmd, %region_2.3_spmd} | conditional | flops 2420932864 | bytes 20910348 | solution.py:82
  371.5 1.5 fusion.1
  373.0 10.0 %fusion = bf16[144,2048]{1,0:T(8,128)(2,1)} fusion(bf16[2048,2048]{1,0:T(8,128)(2,1)} %get-tuple-element.196, bf16[2048,2048]{1,0:T(8,128)(2,1)} %get-tuple-element.195, f32[144]{0:T(256)S(1)} %add_rsqrt_fusion, bf16[144,2048]{1,0:T(8,128)(2,1)} %get-tuple-element.194, bf16[4,144,2048]{2,1,0:T(8,128)(2,1)} %get-tuple-element.192, s32[]{:T(128)} %get-tuple-element.193, ...), kind=kOutput, calls=%fused_computation.4 | convolution fusion | flops 2419752960 | bytes 19728960 | tf_op jit(solution)/shard_map/while/body/eval_jaxpr/cond/branch_1_fun/dot_general | solution.py:49
  385.2 1.4 bitcast_dynamic-update-slice_fusion.13
  388.0 1.9 copy.25
  389.9 5.0 reshape.120
  394.9 1.8 gather_fusion
  396.7 1.5 fusion.15
  398.2 1.9 convolution_convert_fusion
  400.1 1.8 fusion.43
  402.3 6.4 %collective-permute-start.11 = (bf16[136,2048]{1,0:T(8,128)(2,1)S(1)}, bf16[136,2048]{1,0:T(8,128)(2,1)S(1)}, u32[]{:S(2)}, u32[]{:S(2)}) collective-permute-start(bf16[136,2048]{1,0:T(8,128)(2,1)S(1)} %get-tuple-element.230), channel_id=1, source_target_pairs={{224,192},{225,193},{226,194},{227,195},{228,196},{229,197},{230,1... | collective-permute-start | bytes 1671176 | tf_op jit(solution)/shard_map/ppermute | solution.py:116
  410.1 2.1 collective-permute-start.13
  412.2 2.1 collective-permute-start.14
  414.3 2.1 collective-permute-start.15
  416.4 2.1 collective-permute-start.16
  419.3 2.1 collective-permute-start.17
  422.6 6.0 %collective-permute-done.14 = bf16[136,2048]{1,0:T(8,128)(2,1)} collective-permute-done((bf16[136,2048]{1,0:T(8,128)(2,1)}, bf16[136,2048]{1,0:T(8,128)(2,1)}, u32[]{:S(2)}, u32[]{:S(2)}) %collective-permute-start.14) | collective-permute-done | bytes 557088 | tf_op jit(solution)/shard_map/ppermute | solution.py:116
  428.5 6.0 %collective-permute-done.15 = bf16[136,2048]{1,0:T(8,128)(2,1)} collective-permute-done((bf16[136,2048]{1,0:T(8,128)(2,1)}, bf16[136,2048]{1,0:T(8,128)(2,1)}, u32[]{:S(2)}, u32[]{:S(2)}) %collective-permute-start.15) | collective-permute-done | bytes 557088 | tf_op jit(solution)/shard_map/ppermute | solution.py:116
  434.5 1.7 fusion.36
  437.3 16.2 %all_to_all.10 = bf16[32,2,2048]{2,1,0:T(2,128)(2,1)} all-to-all(bf16[32,2,2048]{2,1,0:T(2,128)(2,1)S(1)} %reshape.125), channel_id=1, replica_groups=mesh['section'=8,'expert'=32] {'expert'}, dimensions={0} | all-to-all | bytes 524288 | tf_op jit(solution)/shard_map/all_to_all | solution.py:121
  453.8 24.5 %all-gather.5.cloned.1.call-done = bf16[256,2,2048]{2,1,0:T(2,128)(2,1)} async-done(((bf16[32,2,2048]{2,1,0:T(2,128)(2,1)}), bf16[256,2,2048]{2,1,0:T(2,128)(2,1)}) %all-gather.5.cloned.1.call-update) | async-done | bytes 2097168 | tf_op jit(solution)/shard_map/all_gather | solution.py:122
  478.3 2.7 reshape.126
  481.1 1.4 fusion.57
  482.5 4.9 multiply_convert_fusion.2
  487.5 36.3 %reduce-scatter.2.cloned.1.call-done = bf16[512,256]{1,0:T(8,128)(2,1)} async-done(((bf16[512,2048]{1,0:T(8,128)(2,1)}), bf16[512,256]{1,0:T(8,128)(2,1)}) %reduce-scatter.2.cloned.1.call-update) | async-done | bytes 262160 | tf_op jit(solution)/shard_map/reduce_scatter | solution.py:133
  525.7 9.3 %all-to-all-start.1 = ((bf16[32,8,2,256]{3,2,1,0:T(2,128)(2,1)}), bf16[32,8,2,256]{3,2,1,0:T(2,128)(2,1)S(1)}, u32[]{:S(2)}, u32[]{:S(2)}) async-start(bf16[32,8,2,256]{3,2,1,0:T(2,128)(2,1)} %bitcast.114), calls=%async_computation.2 | async-start | bytes 524288 | tf_op jit(solution)/shard_map/all_to_all | solution.py:135
  535.2 12.6 %all-to-all-done.1 = bf16[32,8,2,256]{3,2,1,0:T(2,128)(2,1)S(1)} async-done(((bf16[32,8,2,256]{3,2,1,0:T(2,128)(2,1)}), bf16[32,8,2,256]{3,2,1,0:T(2,128)(2,1)S(1)}, u32[]{:S(2)}, u32[]{:S(2)}) %all-to-all-start.1) | async-done | bytes 262176 | tf_op jit(solution)/shard_map/all_to_all | solution.py:135
  547.9 2.1 scatter_custom_fusion
  (126 shorter events, 67.4 us)
Async XLA Ops:
  6.5 476.0 %copy-start = (bf16[1,256,2048]{2,1,0:T(8,128)(2,1)S(1)}, bf16[1,256,2048]{2,1,0:T(8,128)(2,1)}, u32[]{:S(2)}) copy-start(bf16[1,256,2048]{2,1,0:T(8,128)(2,1)} %param.17) | copy-start | bytes 3145732
  6.5 18.9 %copy-start.7 = (s32[144,1]{0,1:T(1,128)S(1)}, s32[144,1]{0,1:T(1,128)}, u32[]{:S(2)}) copy-start(s32[144,1]{0,1:T(1,128)} %param.19) | copy-start | bytes 1732
  6.5 54.6 %copy-start.8 = (s32[144]{0:T(256)S(1)}, s32[144]{0:T(256)}, u32[]{:S(2)}) copy-start(s32[144]{0:T(256)} %param.18) | copy-start | bytes 1732
  6.5 164.4 %all-gather.3.cloned.1.call-start = ((), (), s32[]{:S(2)}) async-start(), calls=%async_computation.3 | async-start | bytes 8650752 | tf_op jit(solution)/shard_map/all_gather | solution.py:59
  7.3 471.1 %all-gather.5.cloned.1.call-start = ((), (), s32[]{:S(2)}) async-start(), calls=%async_computation.4 | async-start | bytes 2359296 | tf_op jit(solution)/shard_map/all_gather | solution.py:122
  7.3 8.8 %collective-permute-start.1 = (bf16[64,2048]{1,0:T(8,128)(2,1)}, bf16[64,2048]{1,0:T(8,128)(2,1)S(1)}, u32[]{:S(2)}, u32[]{:S(2)}) collective-permute-start(bf16[64,2048]{1,0:T(8,128)(2,1)} %bitcast.126), channel_id=1, source_target_pairs={{0,1},{1,2},{2,3},{3,0},{4,5},{5,6},{6,7},{7,4},{8,9},{9,10},{10,1... | collective-permute-start | bytes 786440 | tf_op jit(solution)/shard_map/ppermute | solution.py:30
  8.7 7.5 %collective-permute-start.2 = (bf16[64,2048]{1,0:T(8,128)(2,1)}, bf16[64,2048]{1,0:T(8,128)(2,1)S(1)}, u32[]{:S(2)}, u32[]{:S(2)}) collective-permute-start(bf16[64,2048]{1,0:T(8,128)(2,1)} %bitcast.127), channel_id=1, source_target_pairs={{0,3},{1,0},{2,1},{3,2},{4,7},{5,4},{6,5},{7,6},{8,11},{9,8},{10,9... | collective-permute-start | bytes 786440 | tf_op jit(solution)/shard_map/ppermute | solution.py:33
  16.1 7.6 %collective-permute-start.3 = (bf16[64,2048]{1,0:T(8,128)(2,1)S(1)}, bf16[64,2048]{1,0:T(8,128)(2,1)S(1)}, u32[]{:S(2)}, u32[]{:S(2)}) collective-permute-start(bf16[64,2048]{1,0:T(8,128)(2,1)S(1)} %collective-permute-done.1), channel_id=1, source_target_pairs={{0,1},{1,2},{2,3},{3,0},{4,5},{5,6},{6,7},{7,4},{8,9},{9,10},{10,1... | collective-permute-start | bytes 786440 | tf_op jit(solution)/shard_map/ppermute | solution.py:30
  23.8 37.4 %collective-permute-start.4 = (bf16[4,64,2048]{2,1,0:T(8,128)(2,1)S(1)}, bf16[4,64,2048]{2,1,0:T(8,128)(2,1)}, u32[]{:S(2)}, u32[]{:S(2)}) collective-permute-start(bf16[4,64,2048]{2,1,0:T(8,128)(2,1)S(1)} %bitcast_dynamic-update-slice_fusion.9), channel_id=1, source_target_pairs={{0,4},{1,5},{2,6},{3,7},{4,8},{5,9},{6,10},{7,11},{8,12},{9,13},{1... | collective-permute-start | bytes 3145736 | tf_op jit(solution)/shard_map/ppermute | solution.py:30
  25.5 35.7 %collective-permute-start.5 = (bf16[4,64,2048]{2,1,0:T(8,128)(2,1)S(1)}, bf16[4,64,2048]{2,1,0:T(8,128)(2,1)S(1)}, u32[]{:S(2)}, u32[]{:S(2)}) collective-permute-start(bf16[4,64,2048]{2,1,0:T(8,128)(2,1)S(1)} %bitcast_dynamic-update-slice_fusion.9), channel_id=1, source_target_pairs={{0,28},{1,29},{2,30},{3,31},{4,0},{5,1},{6,2},{7,3},{8,4},{9,5},{1... | collective-permute-start | bytes 3145736 | tf_op jit(solution)/shard_map/ppermute | solution.py:33
  61.2 39.9 %collective-permute-start.6 = (bf16[4,64,2048]{2,1,0:T(8,128)(2,1)}, bf16[4,64,2048]{2,1,0:T(8,128)(2,1)S(1)}, u32[]{:S(2)}, u32[]{:S(2)}) collective-permute-start(bf16[4,64,2048]{2,1,0:T(8,128)(2,1)} %collective-permute-done.4), channel_id=1, source_target_pairs={{0,4},{1,5},{2,6},{3,7},{4,8},{5,9},{6,10},{7,11},{8,12},{9,13},{1... | collective-permute-start | bytes 3145736 | tf_op jit(solution)/shard_map/ppermute | solution.py:30
  61.2 43.2 %collective-permute-start.7 = (bf16[4,64,2048]{2,1,0:T(8,128)(2,1)S(1)}, bf16[4,64,2048]{2,1,0:T(8,128)(2,1)S(1)}, u32[]{:S(2)}, u32[]{:S(2)}) collective-permute-start(bf16[4,64,2048]{2,1,0:T(8,128)(2,1)S(1)} %collective-permute-done.5), channel_id=1, source_target_pairs={{0,28},{1,29},{2,30},{3,31},{4,0},{5,1},{6,2},{7,3},{8,4},{9,5},{1... | collective-permute-start | bytes 3145736 | tf_op jit(solution)/shard_map/ppermute | solution.py:33
  101.0 45.9 %collective-permute-start.8 = (bf16[4,64,2048]{2,1,0:T(8,128)(2,1)S(1)}, bf16[4,64,2048]{2,1,0:T(8,128)(2,1)S(1)}, u32[]{:S(2)}, u32[]{:S(2)}) collective-permute-start(bf16[4,64,2048]{2,1,0:T(8,128)(2,1)S(1)} %collective-permute-done.6), channel_id=1, source_target_pairs={{0,4},{1,5},{2,6},{3,7},{4,8},{5,9},{6,10},{7,11},{8,12},{9,13},{1... | collective-permute-start | bytes 3145736 | tf_op jit(solution)/shard_map/ppermute | solution.py:30
  104.5 44.6 %collective-permute-start.9 = (bf16[4,64,2048]{2,1,0:T(8,128)(2,1)S(1)}, bf16[4,64,2048]{2,1,0:T(8,128)(2,1)S(1)}, u32[]{:S(2)}, u32[]{:S(2)}) collective-permute-start(bf16[4,64,2048]{2,1,0:T(8,128)(2,1)S(1)} %collective-permute-done.7), channel_id=1, source_target_pairs={{0,28},{1,29},{2,30},{3,31},{4,0},{5,1},{6,2},{7,3},{8,4},{9,5},{1... | collective-permute-start | bytes 3145736 | tf_op jit(solution)/shard_map/ppermute | solution.py:33
  146.9 22.9 %collective-permute-start.10 = (bf16[4,64,2048]{2,1,0:T(8,128)(2,1)S(1)}, bf16[4,64,2048]{2,1,0:T(8,128)(2,1)S(1)}, u32[]{:S(2)}, u32[]{:S(2)}) collective-permute-start(bf16[4,64,2048]{2,1,0:T(8,128)(2,1)S(1)} %collective-permute-done.8), channel_id=1, source_target_pairs={{0,4},{1,5},{2,6},{3,7},{4,8},{5,9},{6,10},{7,11},{8,12},{9,13},{1... | collective-permute-start | bytes 3145736 | tf_op jit(solution)/shard_map/ppermute | solution.py:30
  173.1 7.6 %collective-permute-start = (bf16[144,2048]{1,0:T(8,128)(2,1)}, bf16[144,2048]{1,0:T(8,128)(2,1)}, u32[]{:S(2)}, u32[]{:S(2)}) collective-permute-start(bf16[144,2048]{1,0:T(8,128)(2,1)} %get-tuple-element.332), channel_id=1, source_target_pairs={{0,32},{32,64},{64,96},{96,128},{128,160},{160,192},{192,224},{1,3... | collective-permute-start | bytes 1769480 | tf_op jit(solution)/shard_map/while/body/eval_jaxpr/ppermute | solution.py:10
  181.6 11.5 %collective-permute-start = (bf16[144,2048]{1,0:T(8,128)(2,1)}, bf16[144,2048]{1,0:T(8,128)(2,1)}, u32[]{:S(2)}, u32[]{:S(2)}) collective-permute-start(bf16[144,2048]{1,0:T(8,128)(2,1)} %get-tuple-element.332), channel_id=1, source_target_pairs={{0,32},{32,64},{64,96},{96,128},{128,160},{160,192},{192,224},{1,3... | collective-permute-start | bytes 1769480 | tf_op jit(solution)/shard_map/while/body/eval_jaxpr/ppermute | solution.py:10
  194.0 11.5 %collective-permute-start = (bf16[144,2048]{1,0:T(8,128)(2,1)}, bf16[144,2048]{1,0:T(8,128)(2,1)}, u32[]{:S(2)}, u32[]{:S(2)}) collective-permute-start(bf16[144,2048]{1,0:T(8,128)(2,1)} %get-tuple-element.332), channel_id=1, source_target_pairs={{0,32},{32,64},{64,96},{96,128},{128,160},{160,192},{192,224},{1,3... | collective-permute-start | bytes 1769480 | tf_op jit(solution)/shard_map/while/body/eval_jaxpr/ppermute | solution.py:10
  206.4 11.5 %collective-permute-start = (bf16[144,2048]{1,0:T(8,128)(2,1)}, bf16[144,2048]{1,0:T(8,128)(2,1)}, u32[]{:S(2)}, u32[]{:S(2)}) collective-permute-start(bf16[144,2048]{1,0:T(8,128)(2,1)} %get-tuple-element.332), channel_id=1, source_target_pairs={{0,32},{32,64},{64,96},{96,128},{128,160},{160,192},{192,224},{1,3... | collective-permute-start | bytes 1769480 | tf_op jit(solution)/shard_map/while/body/eval_jaxpr/ppermute | solution.py:10
  218.8 11.5 %collective-permute-start = (bf16[144,2048]{1,0:T(8,128)(2,1)}, bf16[144,2048]{1,0:T(8,128)(2,1)}, u32[]{:S(2)}, u32[]{:S(2)}) collective-permute-start(bf16[144,2048]{1,0:T(8,128)(2,1)} %get-tuple-element.332), channel_id=1, source_target_pairs={{0,32},{32,64},{64,96},{96,128},{128,160},{160,192},{192,224},{1,3... | collective-permute-start | bytes 1769480 | tf_op jit(solution)/shard_map/while/body/eval_jaxpr/ppermute | solution.py:10
  231.2 11.5 %collective-permute-start = (bf16[144,2048]{1,0:T(8,128)(2,1)}, bf16[144,2048]{1,0:T(8,128)(2,1)}, u32[]{:S(2)}, u32[]{:S(2)}) collective-permute-start(bf16[144,2048]{1,0:T(8,128)(2,1)} %get-tuple-element.332), channel_id=1, source_target_pairs={{0,32},{32,64},{64,96},{96,128},{128,160},{160,192},{192,224},{1,3... | collective-permute-start | bytes 1769480 | tf_op jit(solution)/shard_map/while/body/eval_jaxpr/ppermute | solution.py:10
  243.6 58.9 %collective-permute-start = (bf16[144,2048]{1,0:T(8,128)(2,1)}, bf16[144,2048]{1,0:T(8,128)(2,1)}, u32[]{:S(2)}, u32[]{:S(2)}) collective-permute-start(bf16[144,2048]{1,0:T(8,128)(2,1)} %get-tuple-element.332), channel_id=1, source_target_pairs={{0,32},{32,64},{64,96},{96,128},{128,160},{160,192},{192,224},{1,3... | collective-permute-start | bytes 1769480 | tf_op jit(solution)/shard_map/while/body/eval_jaxpr/ppermute | solution.py:10
  314.0 11.4 %collective-permute-start = (bf16[144,2048]{1,0:T(8,128)(2,1)}, bf16[144,2048]{1,0:T(8,128)(2,1)}, u32[]{:S(2)}, u32[]{:S(2)}) collective-permute-start(bf16[144,2048]{1,0:T(8,128)(2,1)} %get-tuple-element.332), channel_id=1, source_target_pairs={{0,32},{32,64},{64,96},{96,128},{128,160},{160,192},{192,224},{1,3... | collective-permute-start | bytes 1769480 | tf_op jit(solution)/shard_map/while/body/eval_jaxpr/ppermute | solution.py:10
  337.0 11.5 %collective-permute-start = (bf16[144,2048]{1,0:T(8,128)(2,1)}, bf16[144,2048]{1,0:T(8,128)(2,1)}, u32[]{:S(2)}, u32[]{:S(2)}) collective-permute-start(bf16[144,2048]{1,0:T(8,128)(2,1)} %get-tuple-element.332), channel_id=1, source_target_pairs={{0,32},{32,64},{64,96},{96,128},{128,160},{160,192},{192,224},{1,3... | collective-permute-start | bytes 1769480 | tf_op jit(solution)/shard_map/while/body/eval_jaxpr/ppermute | solution.py:10
  360.0 11.5 %collective-permute-start = (bf16[144,2048]{1,0:T(8,128)(2,1)}, bf16[144,2048]{1,0:T(8,128)(2,1)}, u32[]{:S(2)}, u32[]{:S(2)}) collective-permute-start(bf16[144,2048]{1,0:T(8,128)(2,1)} %get-tuple-element.332), channel_id=1, source_target_pairs={{0,32},{32,64},{64,96},{96,128},{128,160},{160,192},{192,224},{1,3... | collective-permute-start | bytes 1769480 | tf_op jit(solution)/shard_map/while/body/eval_jaxpr/ppermute | solution.py:10
  383.0 4.2 collective-permute-start
  396.7 3.4 copy-start.1
  400.1 2.2 copy-start.2
  402.3 14.0 %collective-permute-start.11 = (bf16[136,2048]{1,0:T(8,128)(2,1)S(1)}, bf16[136,2048]{1,0:T(8,128)(2,1)S(1)}, u32[]{:S(2)}, u32[]{:S(2)}) collective-permute-start(bf16[136,2048]{1,0:T(8,128)(2,1)S(1)} %get-tuple-element.230), channel_id=1, source_target_pairs={{224,192},{225,193},{226,194},{227,195},{228,196},{229,197},{230,1... | collective-permute-start | bytes 1671176 | tf_op jit(solution)/shard_map/ppermute | solution.py:116
  408.7 9.8 %collective-permute-start.12 = (bf16[136,2048]{1,0:T(8,128)(2,1)S(1)}, bf16[136,2048]{1,0:T(8,128)(2,1)S(1)}, u32[]{:S(2)}, u32[]{:S(2)}) collective-permute-start(bf16[136,2048]{1,0:T(8,128)(2,1)S(1)} %get-tuple-element.231), channel_id=1, source_target_pairs={{224,160},{225,161},{226,162},{227,163},{228,164},{229,165},{230,1... | collective-permute-start | bytes 1671176 | tf_op jit(solution)/shard_map/ppermute | solution.py:116
  410.1 12.5 %collective-permute-start.13 = (bf16[136,2048]{1,0:T(8,128)(2,1)}, bf16[136,2048]{1,0:T(8,128)(2,1)}, u32[]{:S(2)}, u32[]{:S(2)}) collective-permute-start(bf16[136,2048]{1,0:T(8,128)(2,1)} %get-tuple-element.232), channel_id=1, source_target_pairs={{224,128},{225,129},{226,130},{227,131},{228,132},{229,133},{230,1... | collective-permute-start | bytes 1671176 | tf_op jit(solution)/shard_map/ppermute | solution.py:116
  412.2 16.3 %collective-permute-start.14 = (bf16[136,2048]{1,0:T(8,128)(2,1)}, bf16[136,2048]{1,0:T(8,128)(2,1)}, u32[]{:S(2)}, u32[]{:S(2)}) collective-permute-start(bf16[136,2048]{1,0:T(8,128)(2,1)} %get-tuple-element.233), channel_id=1, source_target_pairs={{224,96},{225,97},{226,98},{227,99},{228,100},{229,101},{230,102},... | collective-permute-start | bytes 1671176 | tf_op jit(solution)/shard_map/ppermute | solution.py:116
  414.3 20.2 %collective-permute-start.15 = (bf16[136,2048]{1,0:T(8,128)(2,1)}, bf16[136,2048]{1,0:T(8,128)(2,1)}, u32[]{:S(2)}, u32[]{:S(2)}) collective-permute-start(bf16[136,2048]{1,0:T(8,128)(2,1)} %get-tuple-element.234), channel_id=1, source_target_pairs={{224,64},{225,65},{226,66},{227,67},{228,68},{229,69},{230,70},{23... | collective-permute-start | bytes 1671176 | tf_op jit(solution)/shard_map/ppermute | solution.py:116
  416.4 2.1 copy-start.5
  416.4 18.1 %collective-permute-start.16 = (bf16[136,2048]{1,0:T(8,128)(2,1)}, bf16[136,2048]{1,0:T(8,128)(2,1)}, u32[]{:S(2)}, u32[]{:S(2)}) collective-permute-start(bf16[136,2048]{1,0:T(8,128)(2,1)} %get-tuple-element.235), channel_id=1, source_target_pairs={{224,32},{225,33},{226,34},{227,35},{228,36},{229,37},{230,38},{23... | collective-permute-start | bytes 1671176 | tf_op jit(solution)/shard_map/ppermute | solution.py:116
  418.5 0.8 copy-start.6
  419.3 15.2 %collective-permute-start.17 = (bf16[136,2048]{1,0:T(8,128)(2,1)}, bf16[136,2048]{1,0:T(8,128)(2,1)}, u32[]{:S(2)}, u32[]{:S(2)}) collective-permute-start(bf16[136,2048]{1,0:T(8,128)(2,1)} %get-tuple-element.229), channel_id=1, source_target_pairs={{224,0},{225,1},{226,2},{227,3},{228,4},{229,5},{230,6},{231,7},{2... | collective-permute-start | bytes 1671176 | tf_op jit(solution)/shard_map/ppermute | solution.py:116
  436.2 0.8 copy-start.3
  453.5 70.2 %reduce-scatter.2.cloned.1.call-start = ((), (), s32[]{:S(2)}) async-start(), calls=%async_computation.5 | async-start | bytes 2359296 | tf_op jit(solution)/shard_map/reduce_scatter | solution.py:133
  487.4 47.7 %copy-start.4 = (bf16[136,2048]{1,0:T(8,128)(2,1)S(1)}, bf16[136,2048]{1,0:T(8,128)(2,1)}, u32[]{:S(2)}) copy-start(bf16[136,2048]{1,0:T(8,128)(2,1)} %copy-done.3) | copy-start | bytes 1671172
  525.7 22.1 %all-to-all-start.1 = ((bf16[32,8,2,256]{3,2,1,0:T(2,128)(2,1)}), bf16[32,8,2,256]{3,2,1,0:T(2,128)(2,1)S(1)}, u32[]{:S(2)}, u32[]{:S(2)}) async-start(bf16[32,8,2,256]{3,2,1,0:T(2,128)(2,1)} %bitcast.114), calls=%async_computation.2 | async-start | bytes 524288 | tf_op jit(solution)/shard_map/all_to_all | solution.py:135
Sparse Core Ops, SparseCore 0:
  9.9 136.1 all-gather.2
  453.7 24.6 all-gather.4
  487.6 36.1 reduce-scatter.1

commit v4 on v3

--- a/solution.py
+++ b/solution.py
@@ -56,8 +56,10 @@
     section = lax.axis_index("section")
     expert_index = lax.axis_index("expert")
     micro, tok_dev, width = tokens.shape
-    w_first = lax.all_gather(w_in, "expert", axis=1, tiled=True)[0]
     inner = 4 if n_expert % 4 == 0 else 1
+    w_first = ring_gather(w_in[0], "expert", n_expert // inner, inner)
+    w_first = ring_gather(w_first, "expert", inner, 1)
+    w_first = w_first.transpose(1, 0, 2, 3).reshape(-1, width)
     w_second = ring_gather(w_out[0], "expert", inner, 1)
     w_second = ring_gather(w_second, "expert", n_expert // inner, inner)
     w_second = w_second.reshape(-1, width)

time: 559 us -> 545 us (0.975)
  waiting for transfers between devices: 344 us -> 317 us
  starting transfers between devices: 56.6 us -> 66.9 us
    ppermute x6 -> x12, waiting for transfers between devices: 133 us -> 104 us  [ring_gather(): ahead = lax.ppermute(ahead, axis, shifted(1))]
    ppermute x4 -> x8, starting transfers between devices: 11.6 us -> 21.5 us  [ring_gather(): behind = lax.ppermute(behind, axis, shifted(-1))]
  transfers between devices with their start and end apart: 32 -> 41, of which waited for: 23 -> 25; matrix products, arithmetic and copies ran while one was open for 7% -> 7% of each run, Pallas kernels for 0% -> 0%
where the time goes in v4:
time: 545 us; the launch traced here: 543 us
  waiting for transfers between devices  317 us (58%)
  starting transfers between devices  66.9 us (12%)
  local copies, waits for them, and re-layouts  49.5 us (9%)
  matrix products  48.1 us (9%)
  other arithmetic  31.7 us (6%)
  blocking collectives  15.8 us (3%)
  between operations  14.1 us (3%)
    ppermute x11, waiting for transfers between devices, from_behind(): lax.ppermute(value, axis, [(source, source + steps) for source in range(i...  127 us
    ppermute x12, waiting for transfers between devices, ring_gather(): ahead = lax.ppermute(ahead, axis, shifted(1))  104 us
    dot_general x4, matrix products, processor(): branch = jnp.dot(hidden, w_second, preferred_element_type=jnp.float32)  39.9 us
    reduce_scatter x1, waiting for transfers between devices, local(): lax.psum_scatter(scaled, 'section', scatter_dimension=1, tiled=True)  35.7 us
    all_gather x1, waiting for transfers between devices, local(): lax.all_gather(arrived, 'section', axis=0, tiled=True).reshape(-1, width)  24.5 us
    ppermute x8, starting transfers between devices, ring_gather(): behind = lax.ppermute(behind, axis, shifted(-1))  21.5 us
    ppermute x7, starting transfers between devices, local(): got = lax.ppermute(payload[target], 'section', [(last, target)])  18.2 us
    all_to_all x1, blocking collectives, local(): lax.all_to_all(outgoing, 'expert', split_axis=0, concat_axis=0, tiled=True)  15.8 us
  transfers between devices with their start and end apart: 41, of which 25 were waited for; matrix products, arithmetic and copies ran while one was open for 7% of the time, Pallas kernels for 0%

profile of v4, /device:TPU:7, one launch (start us, length us, event | category | flops | bytes accessed | tf_op | source)
XLA Modules:
  0.0 542.9 jit_solution(8467836857099638360)
XLA Ops:
  9.3 1.6 collective-permute-start.1
  10.9 3.9 collective-permute-start.2
  20.7 2.7 collective-permute-start.4
  24.4 3.5 collective-permute-done.13
  28.0 2.7 collective-permute-start.15
  31.9 2.7 collective-permute-start.6
  34.7 22.6 %collective-permute-done.5 = bf16[64,2048]{1,0:T(8,128)(2,1)S(1)} collective-permute-done((bf16[64,2048]{1,0:T(8,128)(2,1)S(1)}, bf16[64,2048]{1,0:T(8,128)(2,1)S(1)}, u32[]{:S(2)}, u32[]{:S(2)}) %collective-permute-start.5) | collective-permute-done | bytes 262176 | tf_op jit(solution)/shard_map/ppermute | solution.py:30
  57.4 6.4 %collective-permute-done.7 = bf16[64,2048]{1,0:T(8,128)(2,1)S(1)} collective-permute-done((bf16[64,2048]{1,0:T(8,128)(2,1)S(1)}, bf16[64,2048]{1,0:T(8,128)(2,1)S(1)}, u32[]{:S(2)}, u32[]{:S(2)}) %collective-permute-start.7) | collective-permute-done | bytes 262176 | tf_op jit(solution)/shard_map/ppermute | solution.py:30
  63.8 2.7 collective-permute-start.9
  66.5 2.7 collective-permute-start.17
  72.0 15.9 %collective-permute-done.16 = bf16[4,64,2048]{2,1,0:T(8,128)(2,1)} collective-permute-done((bf16[4,64,2048]{2,1,0:T(8,128)(2,1)}, bf16[4,64,2048]{2,1,0:T(8,128)(2,1)}, u32[]{:S(2)}, u32[]{:S(2)}) %collective-permute-start.16) | collective-permute-done | bytes 1048608 | tf_op jit(solution)/shard_map/ppermute | solution.py:30
  87.9 2.7 collective-permute-start.19
  92.1 16.0 %collective-permute-done.8 = bf16[8,64,2048]{2,1,0:T(8,128)(2,1)} collective-permute-done((bf16[8,64,2048]{2,1,0:T(8,128)(2,1)S(1)}, bf16[8,64,2048]{2,1,0:T(8,128)(2,1)}, u32[]{:S(2)}, u32[]{:S(2)}) %collective-permute-start.8) | collective-permute-done | bytes 2097184 | tf_op jit(solution)/shard_map/ppermute | solution.py:30
  108.0 1.9 bitcast_dynamic-update-slice_fusion.2
  110.3 1.9 bitcast_dynamic-update-slice_fusion.1
  112.4 19.4 %collective-permute-done.20 = bf16[4,64,2048]{2,1,0:T(8,128)(2,1)S(1)} collective-permute-done((bf16[4,64,2048]{2,1,0:T(8,128)(2,1)S(1)}, bf16[4,64,2048]{2,1,0:T(8,128)(2,1)S(1)}, u32[]{:S(2)}, u32[]{:S(2)}) %collective-permute-start.20) | collective-permute-done | bytes 1048608 | tf_op jit(solution)/shard_map/ppermute | solution.py:30
  132.0 20.0 %collective-permute-done.10 = bf16[8,64,2048]{2,1,0:T(8,128)(2,1)S(1)} collective-permute-done((bf16[8,64,2048]{2,1,0:T(8,128)(2,1)}, bf16[8,64,2048]{2,1,0:T(8,128)(2,1)S(1)}, u32[]{:S(2)}, u32[]{:S(2)}) %collective-permute-start.10) | collective-permute-done | bytes 2097184 | tf_op jit(solution)/shard_map/ppermute | solution.py:30
  153.8 1.9 copy-done.3
  155.7 217.2 %while.16 = (s32[]{:T(128)}, bf16[144,2048]{1,0:T(8,128)(2,1)}, bf16[4,144,2048]{2,1,0:T(8,128)(2,1)S(1)}, s32[]{:T(128)}, pred[]{:T(512)}, /*index=5*/bf16[4,14...) while((s32[]{:T(128)}, bf16[144,2048]{1,0:T(8,128)(2,1)}, ...), condition=%wide.region_4.5_spmd, body=%wide.region_0.4_spmd.sunk | while | flops 2421227776 | bytes 26219048 | solution.py:92
  160.0 6.3 %collective-permute-done = bf16[144,2048]{1,0:T(8,128)(2,1)} collective-permute-done((bf16[144,2048]{1,0:T(8,128)(2,1)}, bf16[144,2048]{1,0:T(8,128)(2,1)}, u32[]{:S(2)}, u32[]{:S(2)}) %collective-permute-start) | collective-permute-done | bytes 589856 | tf_op jit(solution)/shard_map/while/body/eval_jaxpr/ppermute | solution.py:10
  170.7 8.1 %collective-permute-done = bf16[144,2048]{1,0:T(8,128)(2,1)} collective-permute-done((bf16[144,2048]{1,0:T(8,128)(2,1)}, bf16[144,2048]{1,0:T(8,128)(2,1)}, u32[]{:S(2)}, u32[]{:S(2)}) %collective-permute-start) | collective-permute-done | bytes 589856 | tf_op jit(solution)/shard_map/while/body/eval_jaxpr/ppermute | solution.py:10
  183.1 8.1 %collective-permute-done = bf16[144,2048]{1,0:T(8,128)(2,1)} collective-permute-done((bf16[144,2048]{1,0:T(8,128)(2,1)}, bf16[144,2048]{1,0:T(8,128)(2,1)}, u32[]{:S(2)}, u32[]{:S(2)}) %collective-permute-start) | collective-permute-done | bytes 589856 | tf_op jit(solution)/shard_map/while/body/eval_jaxpr/ppermute | solution.py:10
  195.5 8.1 %collective-permute-done = bf16[144,2048]{1,0:T(8,128)(2,1)} collective-permute-done((bf16[144,2048]{1,0:T(8,128)(2,1)}, bf16[144,2048]{1,0:T(8,128)(2,1)}, u32[]{:S(2)}, u32[]{:S(2)}) %collective-permute-start) | collective-permute-done | bytes 589856 | tf_op jit(solution)/shard_map/while/body/eval_jaxpr/ppermute | solution.py:10
  207.9 8.1 %collective-permute-done = bf16[144,2048]{1,0:T(8,128)(2,1)} collective-permute-done((bf16[144,2048]{1,0:T(8,128)(2,1)}, bf16[144,2048]{1,0:T(8,128)(2,1)}, u32[]{:S(2)}, u32[]{:S(2)}) %collective-permute-start) | collective-permute-done | bytes 589856 | tf_op jit(solution)/shard_map/while/body/eval_jaxpr/ppermute | solution.py:10
  220.3 8.1 %collective-permute-done = bf16[144,2048]{1,0:T(8,128)(2,1)} collective-permute-done((bf16[144,2048]{1,0:T(8,128)(2,1)}, bf16[144,2048]{1,0:T(8,128)(2,1)}, u32[]{:S(2)}, u32[]{:S(2)}) %collective-permute-start) | collective-permute-done | bytes 589856 | tf_op jit(solution)/shard_map/while/body/eval_jaxpr/ppermute | solution.py:10
  232.7 55.5 %collective-permute-done = bf16[144,2048]{1,0:T(8,128)(2,1)} collective-permute-done((bf16[144,2048]{1,0:T(8,128)(2,1)}, bf16[144,2048]{1,0:T(8,128)(2,1)}, u32[]{:S(2)}, u32[]{:S(2)}) %collective-permute-start) | collective-permute-done | bytes 589856 | tf_op jit(solution)/shard_map/while/body/eval_jaxpr/ppermute | solution.py:10
  288.2 11.6 %conditional.2 = (bf16[144,2048]{1,0:T(8,128)(2,1)}) conditional(s32[]{:T(128)} %convert_element_type.108, () %tuple.50, (pred[]{:T(512)}, bf16[4,144,2048]{2,1,0:T(8,128)(2,1)}, s32[]{:T(128)}, bf16[144,2048]{1,0:T(8,128)(2,1)}, bf16[2048,2048]{1,0:T(8,128)(2,1)}, /*index=5*/bf16[2048,2048]{1,0:T(8,128)(2,1)}) %tuple.51), branch_computations={%region_1.1_spmd, %region_2.3_spmd} | conditional | flops 2420932864 | bytes 20910348 | solution.py:84
  288.2 1.5 fusion.1
  289.7 10.0 %fusion = bf16[144,2048]{1,0:T(8,128)(2,1)} fusion(bf16[2048,2048]{1,0:T(8,128)(2,1)} %get-tuple-element.196, bf16[2048,2048]{1,0:T(8,128)(2,1)} %get-tuple-element.195, f32[144]{0:T(256)S(1)} %add_rsqrt_fusion, bf16[144,2048]{1,0:T(8,128)(2,1)} %get-tuple-element.194, bf16[4,144,2048]{2,1,0:T(8,128)(2,1)} %get-tuple-element.192, s32[]{:T(128)} %get-tuple-element.193, ...), kind=kOutput, calls=%fused_computation.4 | convolution fusion | flops 2419752960 | bytes 19728960 | tf_op jit(solution)/shard_map/while/body/eval_jaxpr/cond/branch_1_fun/dot_general | solution.py:49
  303.3 7.8 %collective-permute-done = bf16[144,2048]{1,0:T(8,128)(2,1)} collective-permute-done((bf16[144,2048]{1,0:T(8,128)(2,1)}, bf16[144,2048]{1,0:T(8,128)(2,1)}, u32[]{:S(2)}, u32[]{:S(2)}) %collective-permute-start) | collective-permute-done | bytes 589856 | tf_op jit(solution)/shard_map/while/body/eval_jaxpr/ppermute | solution.py:10
  311.1 11.5 %conditional.2 = (bf16[144,2048]{1,0:T(8,128)(2,1)}) conditional(s32[]{:T(128)} %convert_element_type.108, () %tuple.50, (pred[]{:T(512)}, bf16[4,144,2048]{2,1,0:T(8,128)(2,1)}, s32[]{:T(128)}, bf16[144,2048]{1,0:T(8,128)(2,1)}, bf16[2048,2048]{1,0:T(8,128)(2,1)}, /*index=5*/bf16[2048,2048]{1,0:T(8,128)(2,1)}) %tuple.51), branch_computations={%region_1.1_spmd, %region_2.3_spmd} | conditional | flops 2420932864 | bytes 20910348 | solution.py:84
  311.1 1.5 fusion.1
  312.7 9.9 %fusion = bf16[144,2048]{1,0:T(8,128)(2,1)} fusion(bf16[2048,2048]{1,0:T(8,128)(2,1)} %get-tuple-element.196, bf16[2048,2048]{1,0:T(8,128)(2,1)} %get-tuple-element.195, f32[144]{0:T(256)S(1)} %add_rsqrt_fusion, bf16[144,2048]{1,0:T(8,128)(2,1)} %get-tuple-element.194, bf16[4,144,2048]{2,1,0:T(8,128)(2,1)} %get-tuple-element.192, s32[]{:T(128)} %get-tuple-element.193, ...), kind=kOutput, calls=%fused_computation.4 | convolution fusion | flops 2419752960 | bytes 19728960 | tf_op jit(solution)/shard_map/while/body/eval_jaxpr/cond/branch_1_fun/dot_general | solution.py:49
  326.2 7.9 %collective-permute-done = bf16[144,2048]{1,0:T(8,128)(2,1)} collective-permute-done((bf16[144,2048]{1,0:T(8,128)(2,1)}, bf16[144,2048]{1,0:T(8,128)(2,1)}, u32[]{:S(2)}, u32[]{:S(2)}) %collective-permute-start) | collective-permute-done | bytes 589856 | tf_op jit(solution)/shard_map/while/body/eval_jaxpr/ppermute | solution.py:10
  334.1 11.5 %conditional.2 = (bf16[144,2048]{1,0:T(8,128)(2,1)}) conditional(s32[]{:T(128)} %convert_element_type.108, () %tuple.50, (pred[]{:T(512)}, bf16[4,144,2048]{2,1,0:T(8,128)(2,1)}, s32[]{:T(128)}, bf16[144,2048]{1,0:T(8,128)(2,1)}, bf16[2048,2048]{1,0:T(8,128)(2,1)}, /*index=5*/bf16[2048,2048]{1,0:T(8,128)(2,1)}) %tuple.51), branch_computations={%region_1.1_spmd, %region_2.3_spmd} | conditional | flops 2420932864 | bytes 20910348 | solution.py:84
  334.1 1.5 fusion.1
  335.7 9.9 %fusion = bf16[144,2048]{1,0:T(8,128)(2,1)} fusion(bf16[2048,2048]{1,0:T(8,128)(2,1)} %get-tuple-element.196, bf16[2048,2048]{1,0:T(8,128)(2,1)} %get-tuple-element.195, f32[144]{0:T(256)S(1)} %add_rsqrt_fusion, bf16[144,2048]{1,0:T(8,128)(2,1)} %get-tuple-element.194, bf16[4,144,2048]{2,1,0:T(8,128)(2,1)} %get-tuple-element.192, s32[]{:T(128)} %get-tuple-element.193, ...), kind=kOutput, calls=%fused_computation.4 | convolution fusion | flops 2419752960 | bytes 19728960 | tf_op jit(solution)/shard_map/while/body/eval_jaxpr/cond/branch_1_fun/dot_general | solution.py:49
  349.2 8.0 %collective-permute-done = bf16[144,2048]{1,0:T(8,128)(2,1)} collective-permute-done((bf16[144,2048]{1,0:T(8,128)(2,1)}, bf16[144,2048]{1,0:T(8,128)(2,1)}, u32[]{:S(2)}, u32[]{:S(2)}) %collective-permute-start) | collective-permute-done | bytes 589856 | tf_op jit(solution)/shard_map/while/body/eval_jaxpr/ppermute | solution.py:10
  357.2 11.5 %conditional.2 = (bf16[144,2048]{1,0:T(8,128)(2,1)}) conditional(s32[]{:T(128)} %convert_element_type.108, () %tuple.50, (pred[]{:T(512)}, bf16[4,144,2048]{2,1,0:T(8,128)(2,1)}, s32[]{:T(128)}, bf16[144,2048]{1,0:T(8,128)(2,1)}, bf16[2048,2048]{1,0:T(8,128)(2,1)}, /*index=5*/bf16[2048,2048]{1,0:T(8,128)(2,1)}) %tuple.51), branch_computations={%region_1.1_spmd, %region_2.3_spmd} | conditional | flops 2420932864 | bytes 20910348 | solution.py:84
  357.2 1.5 fusion.1
  358.7 10.0 %fusion = bf16[144,2048]{1,0:T(8,128)(2,1)} fusion(bf16[2048,2048]{1,0:T(8,128)(2,1)} %get-tuple-element.196, bf16[2048,2048]{1,0:T(8,128)(2,1)} %get-tuple-element.195, f32[144]{0:T(256)S(1)} %add_rsqrt_fusion, bf16[144,2048]{1,0:T(8,128)(2,1)} %get-tuple-element.194, bf16[4,144,2048]{2,1,0:T(8,128)(2,1)} %get-tuple-element.192, s32[]{:T(128)} %get-tuple-element.193, ...), kind=kOutput, calls=%fused_computation.4 | convolution fusion | flops 2419752960 | bytes 19728960 | tf_op jit(solution)/shard_map/while/body/eval_jaxpr/cond/branch_1_fun/dot_general | solution.py:49
  373.7 1.9 copy.34
  375.6 5.0 reshape.124
  380.6 1.8 gather_fusion
  382.4 1.5 fusion.15
  384.0 1.9 convolution_convert_fusion
  385.9 1.7 fusion.43
  388.1 6.3 %collective-permute-start.21 = (bf16[136,2048]{1,0:T(8,128)(2,1)S(1)}, bf16[136,2048]{1,0:T(8,128)(2,1)S(1)}, u32[]{:S(2)}, u32[]{:S(2)}) collective-permute-start(bf16[136,2048]{1,0:T(8,128)(2,1)S(1)} %get-tuple-element.230), channel_id=1, source_target_pairs={{224,192},{225,193},{226,194},{227,195},{228,196},{229,197},{230,1... | collective-permute-start | bytes 1671176 | tf_op jit(solution)/shard_map/ppermute | solution.py:118
  395.8 2.1 collective-permute-start.23
  397.9 2.1 collective-permute-start.24
  400.0 2.1 collective-permute-start.25
  402.1 2.1 collective-permute-start.26
  405.1 2.1 collective-permute-start.27
  408.3 6.0 %collective-permute-done.24 = bf16[136,2048]{1,0:T(8,128)(2,1)} collective-permute-done((bf16[136,2048]{1,0:T(8,128)(2,1)}, bf16[136,2048]{1,0:T(8,128)(2,1)}, u32[]{:S(2)}, u32[]{:S(2)}) %collective-permute-start.24) | collective-permute-done | bytes 557088 | tf_op jit(solution)/shard_map/ppermute | solution.py:118
  414.3 6.0 %collective-permute-done.25 = bf16[136,2048]{1,0:T(8,128)(2,1)} collective-permute-done((bf16[136,2048]{1,0:T(8,128)(2,1)}, bf16[136,2048]{1,0:T(8,128)(2,1)}, u32[]{:S(2)}, u32[]{:S(2)}) %collective-permute-start.25) | collective-permute-done | bytes 557088 | tf_op jit(solution)/shard_map/ppermute | solution.py:118
  420.3 1.7 fusion.36
  423.0 15.8 %all_to_all.10 = bf16[32,2,2048]{2,1,0:T(2,128)(2,1)} all-to-all(bf16[32,2,2048]{2,1,0:T(2,128)(2,1)S(1)} %reshape.129), channel_id=1, replica_groups=mesh['section'=8,'expert'=32] {'expert'}, dimensions={0} | all-to-all | bytes 524288 | tf_op jit(solution)/shard_map/all_to_all | solution.py:123
  439.1 24.5 %all-gather.2.cloned.1.call-done = bf16[256,2,2048]{2,1,0:T(2,128)(2,1)} async-done(((bf16[32,2,2048]{2,1,0:T(2,128)(2,1)}), bf16[256,2,2048]{2,1,0:T(2,128)(2,1)}) %all-gather.2.cloned.1.call-update) | async-done | bytes 2097168 | tf_op jit(solution)/shard_map/all_gather | solution.py:124
  463.6 2.7 reshape.130
  467.8 4.9 multiply_convert_fusion.2
  473.4 35.7 %reduce-scatter.2.cloned.1.call-done = bf16[512,256]{1,0:T(8,128)(2,1)} async-done(((bf16[512,2048]{1,0:T(8,128)(2,1)}), bf16[512,256]{1,0:T(8,128)(2,1)}) %reduce-scatter.2.cloned.1.call-update) | async-done | bytes 262160 | tf_op jit(solution)/shard_map/reduce_scatter | solution.py:135
  511.0 9.3 %all-to-all-start.1 = ((bf16[32,8,2,256]{3,2,1,0:T(2,128)(2,1)}), bf16[32,8,2,256]{3,2,1,0:T(2,128)(2,1)S(1)}, u32[]{:S(2)}, u32[]{:S(2)}) async-start(bf16[32,8,2,256]{3,2,1,0:T(2,128)(2,1)} %bitcast.145), calls=%async_computation.2 | async-start | bytes 524288 | tf_op jit(solution)/shard_map/all_to_all | solution.py:137
  520.5 12.6 %all-to-all-done.1 = bf16[32,8,2,256]{3,2,1,0:T(2,128)(2,1)S(1)} async-done(((bf16[32,8,2,256]{3,2,1,0:T(2,128)(2,1)}), bf16[32,8,2,256]{3,2,1,0:T(2,128)(2,1)S(1)}, u32[]{:S(2)}, u32[]{:S(2)}) %all-to-all-start.1) | async-done | bytes 262176 | tf_op jit(solution)/shard_map/all_to_all | solution.py:137
  533.2 2.1 scatter_custom_fusion
  (161 shorter events, 79.8 us)
Async XLA Ops:
  6.5 461.3 %copy-start = (bf16[1,256,2048]{2,1,0:T(8,128)(2,1)S(1)}, bf16[1,256,2048]{2,1,0:T(8,128)(2,1)}, u32[]{:S(2)}) copy-start(bf16[1,256,2048]{2,1,0:T(8,128)(2,1)} %param.17) | copy-start | bytes 3145732
  6.5 457.1 %all-gather.2.cloned.1.call-start = ((), (), s32[]{:S(2)}) async-start(), calls=%async_computation.3 | async-start | bytes 2359296 | tf_op jit(solution)/shard_map/all_gather | solution.py:124
  6.5 13.7 %collective-permute-start.11 = (bf16[64,2048]{1,0:T(8,128)(2,1)}, bf16[64,2048]{1,0:T(8,128)(2,1)S(1)}, u32[]{:S(2)}, u32[]{:S(2)}) collective-permute-start(bf16[64,2048]{1,0:T(8,128)(2,1)} %bitcast.161), channel_id=1, source_target_pairs={{0,1},{1,2},{2,3},{3,0},{4,5},{5,6},{6,7},{7,4},{8,9},{9,10},{10,1... | collective-permute-start | bytes 786440 | tf_op jit(solution)/shard_map/ppermute | solution.py:30
  7.8 16.6 %collective-permute-start.12 = (bf16[64,2048]{1,0:T(8,128)(2,1)}, bf16[64,2048]{1,0:T(8,128)(2,1)S(1)}, u32[]{:S(2)}, u32[]{:S(2)}) collective-permute-start(bf16[64,2048]{1,0:T(8,128)(2,1)} %bitcast.162), channel_id=1, source_target_pairs={{0,3},{1,0},{2,1},{3,2},{4,7},{5,4},{6,5},{7,6},{8,11},{9,8},{10,9... | collective-permute-start | bytes 786440 | tf_op jit(solution)/shard_map/ppermute | solution.py:33
  9.3 11.4 %collective-permute-start.1 = (bf16[64,2048]{1,0:T(8,128)(2,1)}, bf16[64,2048]{1,0:T(8,128)(2,1)}, u32[]{:S(2)}, u32[]{:S(2)}) collective-permute-start(bf16[64,2048]{1,0:T(8,128)(2,1)} %bitcast.159), channel_id=1, source_target_pairs={{0,4},{1,5},{2,6},{3,7},{4,8},{5,9},{6,10},{7,11},{8,12},{9,13},{1... | collective-permute-start | bytes 786440 | tf_op jit(solution)/shard_map/ppermute | solution.py:30
  10.9 9.8 %collective-permute-start.2 = (bf16[64,2048]{1,0:T(8,128)(2,1)}, bf16[64,2048]{1,0:T(8,128)(2,1)S(1)}, u32[]{:S(2)}, u32[]{:S(2)}) collective-permute-start(bf16[64,2048]{1,0:T(8,128)(2,1)} %bitcast.160), channel_id=1, source_target_pairs={{0,28},{1,29},{2,30},{3,31},{4,0},{5,1},{6,2},{7,3},{8,4},{9,5},{1... | collective-permute-start | bytes 786440 | tf_op jit(solution)/shard_map/ppermute | solution.py:33
  16.1 4.0 copy-start.9
  20.2 7.7 %collective-permute-start.13 = (bf16[64,2048]{1,0:T(8,128)(2,1)S(1)}, bf16[64,2048]{1,0:T(8,128)(2,1)S(1)}, u32[]{:S(2)}, u32[]{:S(2)}) collective-permute-start(bf16[64,2048]{1,0:T(8,128)(2,1)S(1)} %collective-permute-done.11), channel_id=1, source_target_pairs={{0,1},{1,2},{2,3},{3,0},{4,5},{5,6},{6,7},{7,4},{8,9},{9,10},{10,1... | collective-permute-start | bytes 786440 | tf_op jit(solution)/shard_map/ppermute | solution.py:30
  20.7 10.0 %collective-permute-start.3 = (bf16[64,2048]{1,0:T(8,128)(2,1)}, bf16[64,2048]{1,0:T(8,128)(2,1)S(1)}, u32[]{:S(2)}, u32[]{:S(2)}) collective-permute-start(bf16[64,2048]{1,0:T(8,128)(2,1)} %collective-permute-done.1), channel_id=1, source_target_pairs={{0,4},{1,5},{2,6},{3,7},{4,8},{5,9},{6,10},{7,11},{8,12},{9,13},{1... | collective-permute-start | bytes 786440 | tf_op jit(solution)/shard_map/ppermute | solution.py:30
  20.7 11.2 %collective-permute-start.4 = (bf16[64,2048]{1,0:T(8,128)(2,1)S(1)}, bf16[64,2048]{1,0:T(8,128)(2,1)S(1)}, u32[]{:S(2)}, u32[]{:S(2)}) collective-permute-start(bf16[64,2048]{1,0:T(8,128)(2,1)S(1)} %collective-permute-done.2), channel_id=1, source_target_pairs={{0,28},{1,29},{2,30},{3,31},{4,0},{5,1},{6,2},{7,3},{8,4},{9,5},{1... | collective-permute-start | bytes 786440 | tf_op jit(solution)/shard_map/ppermute | solution.py:33
  27.9 38.6 %collective-permute-start.14 = (bf16[4,64,2048]{2,1,0:T(8,128)(2,1)S(1)}, bf16[4,64,2048]{2,1,0:T(8,128)(2,1)}, u32[]{:S(2)}, u32[]{:S(2)}) collective-permute-start(bf16[4,64,2048]{2,1,0:T(8,128)(2,1)S(1)} %bitcast_dynamic-update-slice_fusion.13), channel_id=1, source_target_pairs={{0,4},{1,5},{2,6},{3,7},{4,8},{5,9},{6,10},{7,11},{8,12},{9,13},{1... | collective-permute-start | bytes 3145736 | tf_op jit(solution)/shard_map/ppermute | solution.py:30
  28.0 38.5 %collective-permute-start.15 = (bf16[4,64,2048]{2,1,0:T(8,128)(2,1)S(1)}, bf16[4,64,2048]{2,1,0:T(8,128)(2,1)S(1)}, u32[]{:S(2)}, u32[]{:S(2)}) collective-permute-start(bf16[4,64,2048]{2,1,0:T(8,128)(2,1)S(1)} %bitcast_dynamic-update-slice_fusion.13), channel_id=1, source_target_pairs={{0,28},{1,29},{2,30},{3,31},{4,0},{5,1},{6,2},{7,3},{8,4},{9,5},{1... | collective-permute-start | bytes 3145736 | tf_op jit(solution)/shard_map/ppermute | solution.py:33
  30.7 26.6 %collective-permute-start.5 = (bf16[64,2048]{1,0:T(8,128)(2,1)S(1)}, bf16[64,2048]{1,0:T(8,128)(2,1)S(1)}, u32[]{:S(2)}, u32[]{:S(2)}) collective-permute-start(bf16[64,2048]{1,0:T(8,128)(2,1)S(1)} %collective-permute-done.3), channel_id=1, source_target_pairs={{0,4},{1,5},{2,6},{3,7},{4,8},{5,9},{6,10},{7,11},{8,12},{9,13},{1... | collective-permute-start | bytes 786440 | tf_op jit(solution)/shard_map/ppermute | solution.py:30
  31.9 25.4 %collective-permute-start.6 = (bf16[64,2048]{1,0:T(8,128)(2,1)S(1)}, bf16[64,2048]{1,0:T(8,128)(2,1)S(1)}, u32[]{:S(2)}, u32[]{:S(2)}) collective-permute-start(bf16[64,2048]{1,0:T(8,128)(2,1)S(1)} %collective-permute-done.4), channel_id=1, source_target_pairs={{0,28},{1,29},{2,30},{3,31},{4,0},{5,1},{6,2},{7,3},{8,4},{9,5},{1... | collective-permute-start | bytes 786440 | tf_op jit(solution)/shard_map/ppermute | solution.py:33
  57.3 6.4 %collective-permute-start.7 = (bf16[64,2048]{1,0:T(8,128)(2,1)S(1)}, bf16[64,2048]{1,0:T(8,128)(2,1)S(1)}, u32[]{:S(2)}, u32[]{:S(2)}) collective-permute-start(bf16[64,2048]{1,0:T(8,128)(2,1)S(1)} %collective-permute-done.5), channel_id=1, source_target_pairs={{0,4},{1,5},{2,6},{3,7},{4,8},{5,9},{6,10},{7,11},{8,12},{9,13},{1... | collective-permute-start | bytes 786440 | tf_op jit(solution)/shard_map/ppermute | solution.py:30
  63.7 44.3 %collective-permute-start.8 = (bf16[8,64,2048]{2,1,0:T(8,128)(2,1)S(1)}, bf16[8,64,2048]{2,1,0:T(8,128)(2,1)}, u32[]{:S(2)}, u32[]{:S(2)}) collective-permute-start(bf16[8,64,2048]{2,1,0:T(8,128)(2,1)S(1)} %bitcast_dynamic-update-slice_fusion.16), channel_id=1, source_target_pairs={{0,1},{1,2},{2,3},{3,0},{4,5},{5,6},{6,7},{7,4},{8,9},{9,10},{10,1... | collective-permute-start | bytes 6291464 | tf_op jit(solution)/shard_map/ppermute | solution.py:30
  63.8 46.4 %collective-permute-start.9 = (bf16[8,64,2048]{2,1,0:T(8,128)(2,1)S(1)}, bf16[8,64,2048]{2,1,0:T(8,128)(2,1)}, u32[]{:S(2)}, u32[]{:S(2)}) collective-permute-start(bf16[8,64,2048]{2,1,0:T(8,128)(2,1)S(1)} %bitcast_dynamic-update-slice_fusion.16), channel_id=1, source_target_pairs={{0,3},{1,0},{2,1},{3,2},{4,7},{5,4},{6,5},{7,6},{8,11},{9,8},{10,9... | collective-permute-start | bytes 6291464 | tf_op jit(solution)/shard_map/ppermute | solution.py:33
  66.5 21.4 %collective-permute-start.16 = (bf16[4,64,2048]{2,1,0:T(8,128)(2,1)}, bf16[4,64,2048]{2,1,0:T(8,128)(2,1)}, u32[]{:S(2)}, u32[]{:S(2)}) collective-permute-start(bf16[4,64,2048]{2,1,0:T(8,128)(2,1)} %collective-permute-done.14), channel_id=1, source_target_pairs={{0,4},{1,5},{2,6},{3,7},{4,8},{5,9},{6,10},{7,11},{8,12},{9,13},{1... | collective-permute-start | bytes 3145736 | tf_op jit(solution)/shard_map/ppermute | solution.py:30
  66.5 21.4 %collective-permute-start.17 = (bf16[4,64,2048]{2,1,0:T(8,128)(2,1)S(1)}, bf16[4,64,2048]{2,1,0:T(8,128)(2,1)S(1)}, u32[]{:S(2)}, u32[]{:S(2)}) collective-permute-start(bf16[4,64,2048]{2,1,0:T(8,128)(2,1)S(1)} %collective-permute-done.15), channel_id=1, source_target_pairs={{0,28},{1,29},{2,30},{3,31},{4,0},{5,1},{6,2},{7,3},{8,4},{9,5},{1... | collective-permute-start | bytes 3145736 | tf_op jit(solution)/shard_map/ppermute | solution.py:33
  87.9 22.0 %collective-permute-start.18 = (bf16[4,64,2048]{2,1,0:T(8,128)(2,1)}, bf16[4,64,2048]{2,1,0:T(8,128)(2,1)S(1)}, u32[]{:S(2)}, u32[]{:S(2)}) collective-permute-start(bf16[4,64,2048]{2,1,0:T(8,128)(2,1)} %collective-permute-done.16), channel_id=1, source_target_pairs={{0,4},{1,5},{2,6},{3,7},{4,8},{5,9},{6,10},{7,11},{8,12},{9,13},{1... | collective-permute-start | bytes 3145736 | tf_op jit(solution)/shard_map/ppermute | solution.py:30
  87.9 24.4 %collective-permute-start.19 = (bf16[4,64,2048]{2,1,0:T(8,128)(2,1)S(1)}, bf16[4,64,2048]{2,1,0:T(8,128)(2,1)S(1)}, u32[]{:S(2)}, u32[]{:S(2)}) collective-permute-start(bf16[4,64,2048]{2,1,0:T(8,128)(2,1)S(1)} %collective-permute-done.17), channel_id=1, source_target_pairs={{0,28},{1,29},{2,30},{3,31},{4,0},{5,1},{6,2},{7,3},{8,4},{9,5},{1... | collective-permute-start | bytes 3145736 | tf_op jit(solution)/shard_map/ppermute | solution.py:33
  108.0 44.0 %collective-permute-start.10 = (bf16[8,64,2048]{2,1,0:T(8,128)(2,1)}, bf16[8,64,2048]{2,1,0:T(8,128)(2,1)S(1)}, u32[]{:S(2)}, u32[]{:S(2)}) collective-permute-start(bf16[8,64,2048]{2,1,0:T(8,128)(2,1)} %collective-permute-done.8), channel_id=1, source_target_pairs={{0,1},{1,2},{2,3},{3,0},{4,5},{5,6},{6,7},{7,4},{8,9},{9,10},{10,1... | collective-permute-start | bytes 6291464 | tf_op jit(solution)/shard_map/ppermute | solution.py:30
  109.9 21.9 %collective-permute-start.20 = (bf16[4,64,2048]{2,1,0:T(8,128)(2,1)S(1)}, bf16[4,64,2048]{2,1,0:T(8,128)(2,1)S(1)}, u32[]{:S(2)}, u32[]{:S(2)}) collective-permute-start(bf16[4,64,2048]{2,1,0:T(8,128)(2,1)S(1)} %collective-permute-done.18), channel_id=1, source_target_pairs={{0,4},{1,5},{2,6},{3,7},{4,8},{5,9},{6,10},{7,11},{8,12},{9,13},{1... | collective-permute-start | bytes 3145736 | tf_op jit(solution)/shard_map/ppermute | solution.py:30
  132.0 21.8 %copy-start.2 = (bf16[8,4,64,2048]{3,2,1,0:T(8,128)(2,1)}, bf16[8,4,64,2048]{3,2,1,0:T(8,128)(2,1)S(1)}, u32[]{:S(2)}) copy-start(bf16[8,4,64,2048]{3,2,1,0:T(8,128)(2,1)S(1)} %bitcast_dynamic-update-slice_fusion.5) | copy-start | bytes 25165828
  152.3 3.4 copy-start.3
  156.6 9.7 %collective-permute-start = (bf16[144,2048]{1,0:T(8,128)(2,1)}, bf16[144,2048]{1,0:T(8,128)(2,1)}, u32[]{:S(2)}, u32[]{:S(2)}) collective-permute-start(bf16[144,2048]{1,0:T(8,128)(2,1)} %get-tuple-element.332), channel_id=1, source_target_pairs={{0,32},{32,64},{64,96},{96,128},{128,160},{160,192},{192,224},{1,3... | collective-permute-start | bytes 1769480 | tf_op jit(solution)/shard_map/while/body/eval_jaxpr/ppermute | solution.py:10
  167.2 11.5 %collective-permute-start = (bf16[144,2048]{1,0:T(8,128)(2,1)}, bf16[144,2048]{1,0:T(8,128)(2,1)}, u32[]{:S(2)}, u32[]{:S(2)}) collective-permute-start(bf16[144,2048]{1,0:T(8,128)(2,1)} %get-tuple-element.332), channel_id=1, source_target_pairs={{0,32},{32,64},{64,96},{96,128},{128,160},{160,192},{192,224},{1,3... | collective-permute-start | bytes 1769480 | tf_op jit(solution)/shard_map/while/body/eval_jaxpr/ppermute | solution.py:10
  179.7 11.5 %collective-permute-start = (bf16[144,2048]{1,0:T(8,128)(2,1)}, bf16[144,2048]{1,0:T(8,128)(2,1)}, u32[]{:S(2)}, u32[]{:S(2)}) collective-permute-start(bf16[144,2048]{1,0:T(8,128)(2,1)} %get-tuple-element.332), channel_id=1, source_target_pairs={{0,32},{32,64},{64,96},{96,128},{128,160},{160,192},{192,224},{1,3... | collective-permute-start | bytes 1769480 | tf_op jit(solution)/shard_map/while/body/eval_jaxpr/ppermute | solution.py:10
  192.1 11.5 %collective-permute-start = (bf16[144,2048]{1,0:T(8,128)(2,1)}, bf16[144,2048]{1,0:T(8,128)(2,1)}, u32[]{:S(2)}, u32[]{:S(2)}) collective-permute-start(bf16[144,2048]{1,0:T(8,128)(2,1)} %get-tuple-element.332), channel_id=1, source_target_pairs={{0,32},{32,64},{64,96},{96,128},{128,160},{160,192},{192,224},{1,3... | collective-permute-start | bytes 1769480 | tf_op jit(solution)/shard_map/while/body/eval_jaxpr/ppermute | solution.py:10
  204.5 11.5 %collective-permute-start = (bf16[144,2048]{1,0:T(8,128)(2,1)}, bf16[144,2048]{1,0:T(8,128)(2,1)}, u32[]{:S(2)}, u32[]{:S(2)}) collective-permute-start(bf16[144,2048]{1,0:T(8,128)(2,1)} %get-tuple-element.332), channel_id=1, source_target_pairs={{0,32},{32,64},{64,96},{96,128},{128,160},{160,192},{192,224},{1,3... | collective-permute-start | bytes 1769480 | tf_op jit(solution)/shard_map/while/body/eval_jaxpr/ppermute | solution.py:10
  216.9 11.5 %collective-permute-start = (bf16[144,2048]{1,0:T(8,128)(2,1)}, bf16[144,2048]{1,0:T(8,128)(2,1)}, u32[]{:S(2)}, u32[]{:S(2)}) collective-permute-start(bf16[144,2048]{1,0:T(8,128)(2,1)} %get-tuple-element.332), channel_id=1, source_target_pairs={{0,32},{32,64},{64,96},{96,128},{128,160},{160,192},{192,224},{1,3... | collective-permute-start | bytes 1769480 | tf_op jit(solution)/shard_map/while/body/eval_jaxpr/ppermute | solution.py:10
  229.3 58.9 %collective-permute-start = (bf16[144,2048]{1,0:T(8,128)(2,1)}, bf16[144,2048]{1,0:T(8,128)(2,1)}, u32[]{:S(2)}, u32[]{:S(2)}) collective-permute-start(bf16[144,2048]{1,0:T(8,128)(2,1)} %get-tuple-element.332), channel_id=1, source_target_pairs={{0,32},{32,64},{64,96},{96,128},{128,160},{160,192},{192,224},{1,3... | collective-permute-start | bytes 1769480 | tf_op jit(solution)/shard_map/while/body/eval_jaxpr/ppermute | solution.py:10
  299.7 11.4 %collective-permute-start = (bf16[144,2048]{1,0:T(8,128)(2,1)}, bf16[144,2048]{1,0:T(8,128)(2,1)}, u32[]{:S(2)}, u32[]{:S(2)}) collective-permute-start(bf16[144,2048]{1,0:T(8,128)(2,1)} %get-tuple-element.332), channel_id=1, source_target_pairs={{0,32},{32,64},{64,96},{96,128},{128,160},{160,192},{192,224},{1,3... | collective-permute-start | bytes 1769480 | tf_op jit(solution)/shard_map/while/body/eval_jaxpr/ppermute | solution.py:10
  322.6 11.5 %collective-permute-start = (bf16[144,2048]{1,0:T(8,128)(2,1)}, bf16[144,2048]{1,0:T(8,128)(2,1)}, u32[]{:S(2)}, u32[]{:S(2)}) collective-permute-start(bf16[144,2048]{1,0:T(8,128)(2,1)} %get-tuple-element.332), channel_id=1, source_target_pairs={{0,32},{32,64},{64,96},{96,128},{128,160},{160,192},{192,224},{1,3... | collective-permute-start | bytes 1769480 | tf_op jit(solution)/shard_map/while/body/eval_jaxpr/ppermute | solution.py:10
  345.6 11.6 %collective-permute-start = (bf16[144,2048]{1,0:T(8,128)(2,1)}, bf16[144,2048]{1,0:T(8,128)(2,1)}, u32[]{:S(2)}, u32[]{:S(2)}) collective-permute-start(bf16[144,2048]{1,0:T(8,128)(2,1)} %get-tuple-element.332), channel_id=1, source_target_pairs={{0,32},{32,64},{64,96},{96,128},{128,160},{160,192},{192,224},{1,3... | collective-permute-start | bytes 1769480 | tf_op jit(solution)/shard_map/while/body/eval_jaxpr/ppermute | solution.py:10
  368.7 4.2 collective-permute-start
  382.4 3.4 copy-start.1
  385.8 2.3 copy-start.4
  388.1 14.0 %collective-permute-start.21 = (bf16[136,2048]{1,0:T(8,128)(2,1)S(1)}, bf16[136,2048]{1,0:T(8,128)(2,1)S(1)}, u32[]{:S(2)}, u32[]{:S(2)}) collective-permute-start(bf16[136,2048]{1,0:T(8,128)(2,1)S(1)} %get-tuple-element.230), channel_id=1, source_target_pairs={{224,192},{225,193},{226,194},{227,195},{228,196},{229,197},{230,1... | collective-permute-start | bytes 1671176 | tf_op jit(solution)/shard_map/ppermute | solution.py:118
  394.5 9.8 %collective-permute-start.22 = (bf16[136,2048]{1,0:T(8,128)(2,1)S(1)}, bf16[136,2048]{1,0:T(8,128)(2,1)S(1)}, u32[]{:S(2)}, u32[]{:S(2)}) collective-permute-start(bf16[136,2048]{1,0:T(8,128)(2,1)S(1)} %get-tuple-element.231), channel_id=1, source_target_pairs={{224,160},{225,161},{226,162},{227,163},{228,164},{229,165},{230,1... | collective-permute-start | bytes 1671176 | tf_op jit(solution)/shard_map/ppermute | solution.py:118
  395.8 12.5 %collective-permute-start.23 = (bf16[136,2048]{1,0:T(8,128)(2,1)}, bf16[136,2048]{1,0:T(8,128)(2,1)}, u32[]{:S(2)}, u32[]{:S(2)}) collective-permute-start(bf16[136,2048]{1,0:T(8,128)(2,1)} %get-tuple-element.232), channel_id=1, source_target_pairs={{224,128},{225,129},{226,130},{227,131},{228,132},{229,133},{230,1... | collective-permute-start | bytes 1671176 | tf_op jit(solution)/shard_map/ppermute | solution.py:118
  397.9 16.3 %collective-permute-start.24 = (bf16[136,2048]{1,0:T(8,128)(2,1)}, bf16[136,2048]{1,0:T(8,128)(2,1)}, u32[]{:S(2)}, u32[]{:S(2)}) collective-permute-start(bf16[136,2048]{1,0:T(8,128)(2,1)} %get-tuple-element.233), channel_id=1, source_target_pairs={{224,96},{225,97},{226,98},{227,99},{228,100},{229,101},{230,102},... | collective-permute-start | bytes 1671176 | tf_op jit(solution)/shard_map/ppermute | solution.py:118
  400.0 20.2 %collective-permute-start.25 = (bf16[136,2048]{1,0:T(8,128)(2,1)}, bf16[136,2048]{1,0:T(8,128)(2,1)}, u32[]{:S(2)}, u32[]{:S(2)}) collective-permute-start(bf16[136,2048]{1,0:T(8,128)(2,1)} %get-tuple-element.234), channel_id=1, source_target_pairs={{224,64},{225,65},{226,66},{227,67},{228,68},{229,69},{230,70},{23... | collective-permute-start | bytes 1671176 | tf_op jit(solution)/shard_map/ppermute | solution.py:118
  402.1 2.1 copy-start.7
  402.1 18.1 %collective-permute-start.26 = (bf16[136,2048]{1,0:T(8,128)(2,1)}, bf16[136,2048]{1,0:T(8,128)(2,1)}, u32[]{:S(2)}, u32[]{:S(2)}) collective-permute-start(bf16[136,2048]{1,0:T(8,128)(2,1)} %get-tuple-element.235), channel_id=1, source_target_pairs={{224,32},{225,33},{226,34},{227,35},{228,36},{229,37},{230,38},{23... | collective-permute-start | bytes 1671176 | tf_op jit(solution)/shard_map/ppermute | solution.py:118
  404.3 0.8 copy-start.8
  405.1 15.2 %collective-permute-start.27 = (bf16[136,2048]{1,0:T(8,128)(2,1)}, bf16[136,2048]{1,0:T(8,128)(2,1)}, u32[]{:S(2)}, u32[]{:S(2)}) collective-permute-start(bf16[136,2048]{1,0:T(8,128)(2,1)} %get-tuple-element.229), channel_id=1, source_target_pairs={{224,0},{225,1},{226,2},{227,3},{228,4},{229,5},{230,6},{231,7},{2... | collective-permute-start | bytes 1671176 | tf_op jit(solution)/shard_map/ppermute | solution.py:118
  422.0 0.8 copy-start.5
  438.8 70.2 %reduce-scatter.2.cloned.1.call-start = ((), (), s32[]{:S(2)}) async-start(), calls=%async_computation.4 | async-start | bytes 2359296 | tf_op jit(solution)/shard_map/reduce_scatter | solution.py:135
  472.7 0.7 copy-start.10
  472.7 47.7 %copy-start.6 = (bf16[136,2048]{1,0:T(8,128)(2,1)S(1)}, bf16[136,2048]{1,0:T(8,128)(2,1)}, u32[]{:S(2)}) copy-start(bf16[136,2048]{1,0:T(8,128)(2,1)} %copy-done.5) | copy-start | bytes 1671172
  511.0 22.1 %all-to-all-start.1 = ((bf16[32,8,2,256]{3,2,1,0:T(2,128)(2,1)}), bf16[32,8,2,256]{3,2,1,0:T(2,128)(2,1)S(1)}, u32[]{:S(2)}, u32[]{:S(2)}) async-start(bf16[32,8,2,256]{3,2,1,0:T(2,128)(2,1)} %bitcast.145), calls=%async_computation.2 | async-start | bytes 524288 | tf_op jit(solution)/shard_map/all_to_all | solution.py:137
Sparse Core Ops, SparseCore 0:
  439.0 24.6 all-gather.1
  472.8 36.1 reduce-scatter.1
